TPU v7x, 1024 devices: a whole 4x8x16 slice. The times are simulated.
1024 devices in a mesh: outer: 16 (over z), inner: 64 (over x, y, core).
Axes of the slice: x: 4, y: 8, z: 16, core: 2. Of those that a mesh axis runs over, the one named last changes fastest.
Arguments:
- projected: bfloat16 [8192, 3, 4096], P('inner', None, 'outer'), may hold values from -6 to 6
- short_weight: float32 [7, 3, 4096], P(None, None, 'outer'), may hold values from -2.5 to 2.5
- filter_in: float32 [33, 64], replicated, may hold values from -1 to 1
- filter_bias: float32 [64], replicated, may hold values from -3.140625 to 3.140625
- filter_out: float32 [64, 4096], P(None, 'outer'), may hold values from -0.75 to 0.75
- filter_decay: float32 [4096], P('outer'), as said below
- cotangent: bfloat16 [8192, 4096], P('inner', 'outer'), may hold values from -6 to 6
Outputs:
- operator_out: bfloat16 [8192, 4096], P('inner', 'outer')
- grad_projected: bfloat16 [8192, 3, 4096], P('inner', None, 'outer')
- grad_filter: float32 [8192, 4096], P('inner', 'outer')
Inputs may be any that keep to these rules, and one draw needn't show every extreme that they name: Every rate in filter_decay is positive, at least 0.3 / 8192 and at most 1 / 30.
All inputs are finite; a program needn't handle non-finite values.
Results may differ from a plain program's by a relative error of at most 0.00155.
Values may be sent and summed in bfloat16 or wider, within the bound.
No kernel may reach another device: no remote copies, remote signals or barrier semaphores. Data moves between devices by JAX's collectives and lax.ppermute only.
A program may use at most 32 MiB of HBM per device.

v0:
```python
import math

import jax
import jax.numpy as jnp
from jax import lax
from jax.sharding import PartitionSpec as P

exact_mode = lax.Precision.HIGHEST
full_turn = 6.283185307179586


def passed_along(value, axis, by):
    length = lax.axis_size(axis)
    pairs = [(i, i + by) for i in range(length) if 0 <= i + by < length]
    return lax.ppermute(value, axis, pairs)


def turning(numbers, period, direction):
    angles = direction * full_turn / period * (numbers % period).astype(jnp.float32)
    return (jnp.cos(angles), jnp.sin(angles))


def rotate(values, cosine, sine):
    return jnp.stack([values[0] * cosine - values[1] * sine, values[0] * sine + values[1] * cosine])


def times_complex(first, second):
    return jnp.stack(
        [first[0] * second[0] - first[1] * second[1], first[0] * second[1] + first[1] * second[0]]
    )


def conjugate(values):
    return jnp.stack([values[0], -values[1]])


def mix_axis(values, count, direction, pattern):
    index = jnp.arange(count, dtype=jnp.int32)
    cosine, sine = turning(index[:, None] * index[None, :], count, direction)
    real_part = jnp.einsum(pattern, cosine, values[0], precision=exact_mode) - jnp.einsum(
        pattern, sine, values[1], precision=exact_mode
    )
    other_part = jnp.einsum(pattern, cosine, values[1], precision=exact_mode) + jnp.einsum(
        pattern, sine, values[0], precision=exact_mode
    )
    return jnp.stack([real_part, other_part])


def grid_places(parts, length):
    return (
        jnp.arange(parts, dtype=jnp.int32)[:, None] * length
        + jnp.arange(length, dtype=jnp.int32)[None, :]
    )


def forward_padded(signal):
    parts = signal.shape[1]
    length = signal.shape[2]
    seq_total = parts * length
    cosine, sine = turning(grid_places(parts, length), 2 * seq_total, -1.0)
    values = jnp.stack(
        [jnp.stack([signal, signal * cosine]), jnp.stack([jnp.zeros_like(signal), signal * sine])]
    )
    values = mix_axis(values, parts, -1.0, "ap,hrpj->hraj")
    index_a = jnp.arange(parts, dtype=jnp.int32)[:, None]
    index_j = jnp.arange(length, dtype=jnp.int32)[None, :]
    cosine, sine = turning(index_a * index_j, seq_total, -1.0)
    values = rotate(values, cosine, sine)
    return mix_axis(values, length, -1.0, "bj,hraj->hrab")


def inverse_padded(spectrum):
    parts = spectrum.shape[3]
    length = spectrum.shape[4]
    seq_total = parts * length
    values = mix_axis(spectrum, length, 1.0, "jb,hrab->hraj")
    index_a = jnp.arange(parts, dtype=jnp.int32)[:, None]
    index_j = jnp.arange(length, dtype=jnp.int32)[None, :]
    cosine, sine = turning(index_a * index_j, seq_total, 1.0)
    values = rotate(values, cosine, sine)
    values = mix_axis(values, parts, 1.0, "pa,hraj->hrpj") / seq_total
    cosine, sine = turning(grid_places(parts, length), 2 * seq_total, 1.0)
    return 0.5 * (values[0, 0] + values[0, 1] * cosine - values[1, 1] * sine)


def to_channels(stacked):
    return lax.all_to_all(
        jnp.swapaxes(stacked, 1, 2)[:, :, None, :], "inner", split_axis=1, concat_axis=2, tiled=True
    )


def to_positions(values):
    moved = lax.all_to_all(values, "inner", split_axis=2, concat_axis=1, tiled=True)
    return jnp.swapaxes(moved[:, :, 0, :], 1, 2)


def filter_features(places, seq_total, bands):
    columns = [places.astype(jnp.float32) / seq_total]
    for band in range(bands):
        stride = min(2**band, seq_total // 4)
        phases = places % (seq_total // stride) * stride
        angles = full_turn / seq_total * phases.astype(jnp.float32)
        columns.append(jnp.cos(angles))
        columns.append(jnp.sin(angles))
    return jnp.stack(columns, axis=1)


def decay_window(rates, places):
    return jnp.exp(-rates * places.astype(jnp.float32)) * jnp.sqrt(-jnp.expm1(-2.0 * rates))


def body(projected, short_weight, filter_in, filter_bias, filter_out, filter_decay, cotangent):
    parts = lax.axis_size("inner")
    inner_id = lax.axis_index("inner")
    length = projected.shape[0]
    chans = projected.shape[2]
    taps = short_weight.shape[0]
    bands = (filter_in.shape[0] - 1) // 2
    seq_total = parts * length
    slices = chans // parts
    earlier = passed_along(projected[length - taps + 1 :], "inner", 1)
    extended = jnp.concatenate([earlier, projected], axis=0)
    mixed = jnp.zeros((length, 3, chans), jnp.float32)
    for offset in range(taps):
        mixed = (
            mixed + short_weight[offset] * extended[taps - 1 - offset : taps - 1 - offset + length]
        )
    query = mixed[:, 0]
    key_part = mixed[:, 1]
    value_part = mixed[:, 2]
    product = key_part * value_part
    grad_conv = cotangent * query
    places = inner_id * length + jnp.arange(length, dtype=jnp.int32)
    activity = jnp.sin(
        jnp.dot(filter_features(places, seq_total, bands), filter_in, precision=exact_mode)
        + filter_bias
    )
    shaped = jnp.dot(activity, filter_out, precision=exact_mode)
    long_filter = shaped * decay_window(filter_decay[None, :], places[:, None])
    moved = to_channels(jnp.stack([product, long_filter, grad_conv]))
    signal_rows = moved[0]
    filter_rows = moved[1]
    grad_rows = moved[2]
    spectra = forward_padded(jnp.concatenate([signal_rows, filter_rows, grad_rows], axis=0))
    signal_spec = spectra[:, :, :slices]
    filter_spec = spectra[:, :, slices : 2 * slices]
    grad_spec = spectra[:, :, 2 * slices :]
    paired = jnp.concatenate(
        [
            times_complex(signal_spec, filter_spec),
            times_complex(conjugate(filter_spec), grad_spec),
            times_complex(grad_spec, conjugate(signal_spec)),
        ],
        axis=2,
    )
    returned = inverse_padded(paired)
    back = to_positions(returned.reshape(3, slices, parts, length))
    conv = back[0]
    grad_product = back[1]
    grad_filter = back[2] / math.sqrt(seq_total)
    operator_out = (query * conv).astype(jnp.bfloat16)
    grad_query = cotangent * conv
    grad_mixed = jnp.stack([grad_query, grad_product * value_part, grad_product * key_part], axis=1)
    later = passed_along(grad_mixed[: taps - 1], "inner", -1)
    tailed = jnp.concatenate([grad_mixed, later], axis=0)
    grad_projected = jnp.zeros((length, 3, chans), jnp.float32)
    for offset in range(taps):
        grad_projected = grad_projected + short_weight[offset] * tailed[offset : offset + length]
    return (operator_out, grad_projected.astype(jnp.bfloat16), grad_filter)


def solution(mesh):
    in_specs = (
        P("inner", None, "outer"),
        P(None, None, "outer"),
        P(),
        P(),
        P(None, "outer"),
        P("outer"),
        P("inner", "outer"),
    )
    out_specs = (P("inner", "outer"), P("inner", None, "outer"), P("inner", "outer"))
    return jax.shard_map(body, mesh=mesh, in_specs=in_specs, out_specs=out_specs, check_vma=False)
```

profile of v0, /device:TPU:1, one launch (start us, length us, event | category | flops | bytes accessed | tf_op | source)
XLA Modules:
  0.0 88.2 jit_solution(717455273740256136)
XLA Ops:
  0.6 0.0 copy-start
  0.6 0.0 copy-start.1
  0.7 0.8 slice.166
  1.4 4.6 %collective-permute-start = (bf16[6,3,256]{2,0,1:T(8,128)(2,1)S(1)}, bf16[6,3,256]{2,0,1:T(8,128)(2,1)S(1)}, u32[]{:S(2)}, u32[]{:S(2)}) collective-permute-start(bf16[6,3,256]{2,0,1:T(8,128)(2,1)S(1)} %slice.166), channel_id=1, source_target_pairs={{0,1},{1,2},{2,3},{3,4},{4,5},{5,6},{6,7},{7,8},{8,9},{9,10},{10,1... | collective-permute-start | bytes 27656 | tf_op jit(solution)/shard_map/ppermute | solution.py:15
  6.0 0.1 convert_multiply_fusion.14
  6.1 0.1 fusion.175
  6.1 0.1 fusion.177
  6.2 0.1 fusion.179
  6.3 0.1 fusion.181
  6.3 0.1 fusion.183
  6.4 0.1 fusion.185
  6.4 0.1 fusion.187
  6.5 0.1 fusion.189
  6.6 0.1 fusion.191
  6.6 0.1 fusion.193
  6.7 0.1 fusion.195
  6.8 0.1 fusion.197
  6.8 0.7 fusion.200
  7.5 1.0 %fusion.199 = (f32[1,3,256]{2,0,1:T(1,128)S(1)}, f32[1,3,256]{2,0,1:T(1,128)S(1)}, f32[1,3,256]{2,0,1:T(1,128)S(1)}, f32[1,3,256]{2,0,1:T(1,128)S(1)}, f32[1,3,2...) fusion(f32[7,3,256]{2,0,1:T(8,128)} %param.8), kind=kLoop, calls=%fused_computation.323 | loop fusion | bytes 43008 | tf_op jit(solution)/shard_map/slice | solution.py:126
  8.6 0.1 stack.34
  8.7 1.1 %fusion.7 = f32[128,64]{0,1:T(8,128)S(1)} fusion(f32[128,33]{0,1:T(8,128)S(1)} %stack.34, f32[33,64]{1,0:T(8,128)} %param.9, f32[64]{0:T(128)} %param.10), kind=kOutput, calls=%fused_computation.19 | convolution fusion | flops 3252224 | bytes 58368 | tf_op jit(solution)/shard_map/dot_general | solution.py:135
  9.8 0.0 copy-done
  9.8 0.3 fusion.6
  10.1 7.4 %collective-permute-done = bf16[6,3,256]{2,0,1:T(8,128)(2,1)S(1)} collective-permute-done((bf16[6,3,256]{2,0,1:T(8,128)(2,1)S(1)}, bf16[6,3,256]{2,0,1:T(8,128)(2,1)S(1)}, u32[]{:S(2)}, u32[]{:S(2)}) %collective-permute-start) | collective-permute-done | bytes 9248 | tf_op jit(solution)/shard_map/ppermute | solution.py:15
  17.5 2.1 %multiply_add_fusion.2 = f32[128,3,256]{2,0,1:T(8,128)S(1)} fusion(bf16[128,3,256]{2,0,1:T(8,128)(2,1)} %param.7, bf16[6,3,256]{2,0,1:T(8,128)(2,1)S(1)} %collective-permute-done, f32[3,256]{1,0:T(4,128)S(1)} %get-tuple-element.35, f32[3,256]{1,0:T(4,128)S(1)} %get-tuple-element.36, f32[3,256]{1,0:T(4,128)S(1)} %get-tuple-element.37, ...), kind=kLoop, calls=%fused_computation.54 | loop fusion | flops 3735552 | bytes 620544 | tf_op jit(solution)/shard_map/add | solution.py:126
  19.6 0.0 copy-done.1
  19.7 1.0 %copy.38 = f32[3,256,1,128]{3,2,0,1:T(1,128)} copy(f32[3,256,1,128]{1,3,0,2:T(8,128)S(1)} %maximum_bitcast_fusion) | data formatting | bytes 786432 | tf_op jit(solution)/shard_map/broadcast_in_dim | solution.py:88
  20.7 7.7 %all-to-all-start = ((f32[3,256,1,128]{3,2,0,1:T(1,128)}), f32[3,256,1,128]{3,2,0,1:T(1,128)S(1)}, u32[]{:S(2)}, u32[]{:S(2)}) async-start(f32[3,256,1,128]{3,2,0,1:T(1,128)} %copy.38), calls=%async_computation | async-start | bytes 786432 | tf_op jit(solution)/shard_map/all_to_all | solution.py:87
  28.4 0.1 multiply_sine_fusion.9
  28.6 0.1 multiply_sine_fusion.8
  28.7 0.3 multiply_cosine_fusion.6
  29.1 13.9 %all-to-all-done = f32[3,256,1,128]{3,2,0,1:T(1,128)S(1)} async-done(((f32[3,256,1,128]{3,2,0,1:T(1,128)}), f32[3,256,1,128]{3,2,0,1:T(1,128)S(1)}, u32[]{:S(2)}, u32[]{:S(2)}) %all-to-all-start) | async-done | bytes 393248 | tf_op jit(solution)/shard_map/all_to_all | solution.py:87
  43.0 0.1 slice_bitcast_fusion.14
  43.1 0.7 fusion.17
  43.9 0.8 fusion.19
  44.7 0.9 %fusion.5 = f32[2,12,64,128]{3,2,1,0:T(8,128)S(1)} fusion(f32[2,12,128,64]{2,3,1,0:T(8,128)S(1)} %fusion.17, f32[1,12,64,128]{3,2,1,0:T(8,128)S(1)} %broadcast_multiply_fusion, f32[1,12,64,128]{3,2,1,0:T(8,128)S(1)} %maximum_bitcast_fusion.1), kind=kOutput, calls=%fused_computation.15 | convolution fusion | flops 151445504 | bytes 2359296 | tf_op jit(solution)/shard_map/ap,hrpj->hraj/dot_general | solution.py:40
  45.7 0.9 %fusion.4 = f32[2,12,64,128]{3,2,1,0:T(8,128)S(1)} fusion(f32[2,12,128,64]{2,3,1,0:T(8,128)S(1)} %fusion.19, f32[1,12,64,128]{3,2,1,0:T(8,128)S(1)} %broadcast_multiply_fusion, f32[1,12,64,128]{3,2,1,0:T(8,128)S(1)} %maximum_bitcast_fusion.1), kind=kOutput, calls=%fused_computation.13 | convolution fusion | flops 151445504 | bytes 2359296 | tf_op jit(solution)/shard_map/ap,hrpj->hraj/dot_general | solution.py:43
  46.6 1.0 %fusion.21 = f32[2,12,64,128]{3,2,1,0:T(8,128)S(1)} fusion(f32[2,12,64,128]{3,2,1,0:T(8,128)S(1)} %fusion.4, f32[2,12,64,128]{3,2,1,0:T(8,128)S(1)} %fusion.5, f32[64,128]{1,0:T(8,128)S(1)} %get-tuple-element.65, f32[64,128]{1,0:T(8,128)S(1)} %get-tuple-element.66), kind=kOutput, calls=%fused_computation.65 | convolution fusion | flops 302809088 | bytes 2424832 | tf_op jit(solution)/shard_map/bj,hraj->hrab/dot_general | solution.py:40
  47.6 1.0 %fusion.22 = f32[2,12,64,128]{3,2,1,0:T(8,128)S(1)} fusion(f32[2,12,64,128]{3,2,1,0:T(8,128)S(1)} %fusion.4, f32[2,12,64,128]{3,2,1,0:T(8,128)S(1)} %fusion.5, f32[64,128]{1,0:T(8,128)S(1)} %get-tuple-element.65, f32[64,128]{1,0:T(8,128)S(1)} %get-tuple-element.66), kind=kOutput, calls=%fused_computation.66 | convolution fusion | flops 302809088 | bytes 2424832 | tf_op jit(solution)/shard_map/bj,hraj->hrab/dot_general | solution.py:43
  48.7 1.0 %fusion.3 = f32[1,2,12,64,128]{4,3,2,1,0:T(8,128)S(1)} fusion(f32[2,12,64,128]{3,2,1,0:T(8,128)S(1)} %fusion.21, f32[2,12,64,128]{3,2,1,0:T(8,128)S(1)} %fusion.4, f32[2,12,64,128]{3,2,1,0:T(8,128)S(1)} %fusion.5, f32[64,128]{1,0:T(8,128)S(1)} %get-tuple-element.65, f32[64,128]{1,0:T(8,128)S(1)} %get-tuple-element.66), kind=kOutput, calls=%fused_computation.11 | convolution fusion | flops 303005696 | bytes 3211264 | tf_op jit(solution)/shard_map/bj,hraj->hrab/dot_general | solution.py:40
  49.7 1.0 %fusion.2 = f32[1,2,12,64,128]{4,3,2,1,0:T(8,128)S(1)} fusion(f32[2,12,64,128]{3,2,1,0:T(8,128)S(1)} %fusion.22, f32[2,12,64,128]{3,2,1,0:T(8,128)S(1)} %fusion.4, f32[2,12,64,128]{3,2,1,0:T(8,128)S(1)} %fusion.5, f32[64,128]{1,0:T(8,128)S(1)} %get-tuple-element.65, f32[64,128]{1,0:T(8,128)S(1)} %get-tuple-element.66), kind=kOutput, calls=%fused_computation.9 | convolution fusion | flops 303005696 | bytes 3211264 | tf_op jit(solution)/shard_map/bj,hraj->hrab/dot_general | solution.py:43
  50.7 0.1 multiply_add_fusion.5
  50.8 0.1 multiply_subtract_fusion.4
  51.0 0.2 maximum_maximum_fusion
  51.2 1.0 %fusion.8 = f32[2,12,64,128]{3,2,1,0:T(8,128)S(1)} fusion(f32[2,2,12,64,128]{4,3,2,1,0:T(8,128)S(1)} %maximum_maximum_fusion), kind=kOutput, calls=%fused_computation.27 | convolution fusion | flops 302219264 | bytes 1572864 | tf_op jit(solution)/shard_map/jb,hrab->hraj/dot_general | solution.py:40
  52.2 1.0 %fusion.9 = f32[2,12,64,128]{3,2,1,0:T(8,128)S(1)} fusion(f32[2,2,12,64,128]{4,3,2,1,0:T(8,128)S(1)} %maximum_maximum_fusion), kind=kOutput, calls=%fused_computation.28 | convolution fusion | flops 302219264 | bytes 1572864 | tf_op jit(solution)/shard_map/jb,hrab->hraj/dot_general | solution.py:43
  53.2 1.0 %convolution_subtract_fusion.1 = f32[2,12,64,128]{3,2,1,0:T(8,128)S(1)} fusion(f32[2,12,64,128]{3,2,1,0:T(8,128)S(1)} %fusion.8, f32[2,2,12,64,128]{4,3,2,1,0:T(8,128)S(1)} %maximum_maximum_fusion), kind=kOutput, calls=%fused_computation.7 | convolution fusion | flops 302415872 | bytes 2359296 | tf_op jit(solution)/shard_map/jb,hrab->hraj/dot_general | solution.py:40
  54.3 1.2 %convolution_add_fusion.1 = f32[2,12,64,128]{3,2,1,0:T(8,128)S(1)} fusion(f32[2,12,64,128]{3,2,1,0:T(8,128)S(1)} %fusion.9, f32[2,2,12,64,128]{4,3,2,1,0:T(8,128)S(1)} %maximum_maximum_fusion), kind=kOutput, calls=%fused_computation.6 | convolution fusion | flops 302415872 | bytes 2359296 | tf_op jit(solution)/shard_map/jb,hrab->hraj/dot_general | solution.py:43
  55.5 1.0 %fusion.23 = f32[2,12,128,64]{2,3,1,0:T(8,128)S(1)} fusion(f32[2,12,64,128]{3,2,1,0:T(8,128)S(1)} %convolution_add_fusion.1, f32[2,12,64,128]{3,2,1,0:T(8,128)S(1)} %convolution_subtract_fusion.1, f32[64,128]{1,0:T(8,128)S(1)} %get-tuple-element.67, f32[64,128]{1,0:T(8,128)S(1)} %get-tuple-element.68), kind=kOutput, calls=%fused_computation.67 | convolution fusion | flops 151642112 | bytes 2424832 | tf_op jit(solution)/shard_map/pa,hraj->hrpj/dot_general | solution.py:40
  56.6 1.0 %fusion.24 = f32[2,12,128,64]{2,3,1,0:T(8,128)S(1)} fusion(f32[2,12,64,128]{3,2,1,0:T(8,128)S(1)} %convolution_add_fusion.1, f32[2,12,64,128]{3,2,1,0:T(8,128)S(1)} %convolution_subtract_fusion.1, f32[64,128]{1,0:T(8,128)S(1)} %get-tuple-element.67, f32[64,128]{1,0:T(8,128)S(1)} %get-tuple-element.68), kind=kOutput, calls=%fused_computation.68 | convolution fusion | flops 151642112 | bytes 2424832 | tf_op jit(solution)/shard_map/pa,hraj->hrpj/dot_general | solution.py:43
  57.6 1.0 %fusion.1 = f32[1,2,12,64,128]{4,3,2,1,0:T(8,128)S(1)} fusion(f32[2,12,128,64]{2,3,1,0:T(8,128)S(1)} %fusion.23, f32[2,12,64,128]{3,2,1,0:T(8,128)S(1)} %convolution_add_fusion.1, f32[2,12,64,128]{3,2,1,0:T(8,128)S(1)} %convolution_subtract_fusion.1, f32[64,128]{1,0:T(8,128)S(1)} %get-tuple-element.67, f32[64,128]{1,0:T(8,128)S(1)} %get-tuple-element.68), kind=kOutput, calls=%fused_computation.5 | convolution fusion | flops 151838720 | bytes 3211264 | tf_op jit(solution)/shard_map/pa,hraj->hrpj/dot_general | solution.py:40
  58.7 1.0 %fusion = f32[1,2,12,64,128]{4,3,2,1,0:T(8,128)S(1)} fusion(f32[2,12,128,64]{2,3,1,0:T(8,128)S(1)} %fusion.24, f32[2,12,64,128]{3,2,1,0:T(8,128)S(1)} %convolution_add_fusion.1, f32[2,12,64,128]{3,2,1,0:T(8,128)S(1)} %convolution_subtract_fusion.1, f32[64,128]{1,0:T(8,128)S(1)} %get-tuple-element.67, f32[64,128]{1,0:T(8,128)S(1)} %get-tuple-element.68), kind=kOutput, calls=%fused_computation.3 | convolution fusion | flops 151838720 | bytes 3211264 | tf_op jit(solution)/shard_map/pa,hraj->hrpj/dot_general | solution.py:43
  59.7 0.2 maximum_multiply_fusion
  59.9 0.1 fusion.198
  60.0 0.1 subtract_multiply_fusion
  60.1 0.3 copy.41
  60.4 20.6 %all_to_all.30 = f32[3,4,64,128]{3,1,0,2:T(4,128)S(1)} all-to-all(f32[3,4,64,128]{3,1,0,2:T(4,128)S(1)} %copy.41), channel_id=1, replica_groups=mesh['outer'=16,'inner'=64] {'inner'}, dimensions={2} | all-to-all | bytes 786432 | tf_op jit(solution)/shard_map/all_to_all | solution.py:93
  81.0 0.1 copy.42
  81.1 0.2 copy.43
  81.3 0.7 fusion.33
  82.0 2.3 %collective-permute-start.1 = (f32[6,3,256]{2,0,1:T(8,128)S(1)}, f32[6,3,256]{2,0,1:T(8,128)S(1)}, u32[]{:S(2)}, u32[]{:S(2)}) collective-permute-start(f32[6,3,256]{2,0,1:T(8,128)S(1)} %slice.234), channel_id=1, source_target_pairs={{1,0},{2,1},{3,2},{4,3},{5,4},{6,5},{7,6},{8,7},{9,8},{10,9},{11,1... | collective-permute-start | bytes 55304 | tf_op jit(solution)/shard_map/ppermute | solution.py:15
  84.3 0.7 fusion.34
  84.9 2.2 %collective-permute-done.1 = f32[6,3,256]{2,0,1:T(8,128)S(1)} collective-permute-done((f32[6,3,256]{2,0,1:T(8,128)S(1)}, f32[6,3,256]{2,0,1:T(8,128)S(1)}, u32[]{:S(2)}, u32[]{:S(2)}) %collective-permute-start.1) | collective-permute-done | bytes 18464 | tf_op jit(solution)/shard_map/ppermute | solution.py:15
  87.1 1.0 %fusion.11 = bf16[128,3,256]{2,0,1:T(8,128)(2,1)} fusion(f32[134,3,256]{2,0,1:T(8,128)S(1)} %pad_maximum_fusion.3, f32[3,256]{1,0:T(4,128)S(1)} %get-tuple-element.35, f32[3,256]{1,0:T(4,128)S(1)} %get-tuple-element.36, f32[3,256]{1,0:T(4,128)S(1)} %get-tuple-element.37, f32[3,256]{1,0:T(4,128)S(1)} %get-tuple-element.38, ...), kind=kLoop, calls=%fused_computation.37 | loop fusion | flops 1572864 | bytes 2970624 | tf_op jit(solution)/shard_map/convert_element_type | solution.py:169
  (17 shorter events, 0.3 us)
Async XLA Ops:
  0.6 9.2 %copy-start = (f32[64,256]{1,0:T(8,128)S(1)}, f32[64,256]{1,0:T(8,128)}, u32[]{:S(2)}) copy-start(f32[64,256]{1,0:T(8,128)} %param.11) | copy-start | bytes 196612
  0.6 19.0 %copy-start.1 = (bf16[128,256]{1,0:T(8,128)(2,1)S(1)}, bf16[128,256]{1,0:T(8,128)(2,1)}, u32[]{:S(2)}) copy-start(bf16[128,256]{1,0:T(8,128)(2,1)} %param.13) | copy-start | bytes 196612
  1.4 16.1 %collective-permute-start = (bf16[6,3,256]{2,0,1:T(8,128)(2,1)S(1)}, bf16[6,3,256]{2,0,1:T(8,128)(2,1)S(1)}, u32[]{:S(2)}, u32[]{:S(2)}) collective-permute-start(bf16[6,3,256]{2,0,1:T(8,128)(2,1)S(1)} %slice.166), channel_id=1, source_target_pairs={{0,1},{1,2},{2,3},{3,4},{4,5},{5,6},{6,7},{7,8},{8,9},{9,10},{10,1... | collective-permute-start | bytes 27656 | tf_op jit(solution)/shard_map/ppermute | solution.py:15
  20.7 22.3 %all-to-all-start = ((f32[3,256,1,128]{3,2,0,1:T(1,128)}), f32[3,256,1,128]{3,2,0,1:T(1,128)S(1)}, u32[]{:S(2)}, u32[]{:S(2)}) async-start(f32[3,256,1,128]{3,2,0,1:T(1,128)} %copy.38), calls=%async_computation | async-start | bytes 786432 | tf_op jit(solution)/shard_map/all_to_all | solution.py:87
  82.0 5.1 %collective-permute-start.1 = (f32[6,3,256]{2,0,1:T(8,128)S(1)}, f32[6,3,256]{2,0,1:T(8,128)S(1)}, u32[]{:S(2)}, u32[]{:S(2)}) collective-permute-start(f32[6,3,256]{2,0,1:T(8,128)S(1)} %slice.234), channel_id=1, source_target_pairs={{1,0},{2,1},{3,2},{4,3},{5,4},{6,5},{7,6},{8,7},{9,8},{10,9},{11,1... | collective-permute-start | bytes 55304 | tf_op jit(solution)/shard_map/ppermute | solution.py:15
where the time goes:
time: 88.6 us; the launch traced here: 88.2 us
  waiting for transfers between devices  23.4 us (26%)
  blocking collectives  20.6 us (23%)
  matrix products  17.3 us (20%)
  starting transfers between devices  14.6 us (16%)
  other arithmetic  7.44 us (8%)
  local copies, waits for them, and re-layouts  3.61 us (4%)
  between operations  1.1 us (1%)
    all_to_all x1, blocking collectives, to_positions(): lax.all_to_all(values, 'inner', split_axis=2, concat_axis=1, tiled=True)  20.6 us
    all_to_all x1, waiting for transfers between devices, to_channels(): lax.all_to_all(jnp.swapaxes(stacked, 1, 2)[:, :, None, :], 'inner', split...  13.9 us
    ppermute x2, waiting for transfers between devices, passed_along(): return lax.ppermute(value, axis, pairs)  9.53 us
    all_to_all x1, starting transfers between devices, to_channels(): lax.all_to_all(jnp.swapaxes(stacked, 1, 2)[:, :, None, :], 'inner', split...  7.73 us
    ppermute x2, starting transfers between devices, passed_along(): return lax.ppermute(value, axis, pairs)  6.89 us
    dot_general x4, matrix products, mix_axis(): jnp.einsum(pattern, sine, values[0], precision=exact_mode)  4.25 us
    dot_general x4, matrix products, mix_axis(): jnp.einsum(pattern, cosine, values[0], precision=exact_mode)  4.02 us
    dot_general x4, matrix products, mix_axis(): jnp.einsum(pattern, sine, values[1], precision=exact_mode)  3.84 us
  transfers between devices with their start and end apart: 3, of which 3 were waited for; matrix products, arithmetic and copies ran while one was open for 6% of the time, Pallas kernels for 0%

commit v1 on v0

--- a/solution.py
+++ b/solution.py
@@ -6,6 +6,7 @@
 from jax.sharding import PartitionSpec as P
 
 exact_mode = lax.Precision.HIGHEST
+transform_mode = lax.Precision.HIGH
 full_turn = 6.283185307179586
 
 
@@ -37,11 +38,11 @@
 def mix_axis(values, count, direction, pattern):
     index = jnp.arange(count, dtype=jnp.int32)
     cosine, sine = turning(index[:, None] * index[None, :], count, direction)
-    real_part = jnp.einsum(pattern, cosine, values[0], precision=exact_mode) - jnp.einsum(
-        pattern, sine, values[1], precision=exact_mode
+    real_part = jnp.einsum(pattern, cosine, values[0], precision=transform_mode) - jnp.einsum(
+        pattern, sine, values[1], precision=transform_mode
     )
-    other_part = jnp.einsum(pattern, cosine, values[1], precision=exact_mode) + jnp.einsum(
-        pattern, sine, values[0], precision=exact_mode
+    other_part = jnp.einsum(pattern, cosine, values[1], precision=transform_mode) + jnp.einsum(
+        pattern, sine, values[0], precision=transform_mode
     )
     return jnp.stack([real_part, other_part])
 

time: 88.6 us -> 83.5 us (0.942)
  matrix products: 17.3 us -> 12 us
    dot_general x16, matrix products: 15.9 us -> 10.6 us  [the longest x4 2.7 us: mix_axis(): jnp.einsum(pattern, sine, values[0], precision=transform_mode)]
where the time goes in v1:
time: 83.5 us; the launch traced here: 83 us
  waiting for transfers between devices  23.4 us (28%)
  blocking collectives  20.6 us (25%)
  starting transfers between devices  14.6 us (17%)
  matrix products  12 us (14%)
  other arithmetic  7.65 us (9%)
  local copies, waits for them, and re-layouts  3.61 us (4%)
  between operations  1.1 us (1%)
    all_to_all x1, blocking collectives, to_positions(): lax.all_to_all(values, 'inner', split_axis=2, concat_axis=1, tiled=True)  20.6 us
    all_to_all x1, waiting for transfers between devices, to_channels(): lax.all_to_all(jnp.swapaxes(stacked, 1, 2)[:, :, None, :], 'inner', split...  13.9 us
    ppermute x2, waiting for transfers between devices, passed_along(): return lax.ppermute(value, axis, pairs)  9.53 us
    all_to_all x1, starting transfers between devices, to_channels(): lax.all_to_all(jnp.swapaxes(stacked, 1, 2)[:, :, None, :], 'inner', split...  7.73 us
    ppermute x2, starting transfers between devices, passed_along(): return lax.ppermute(value, axis, pairs)  6.89 us
    dot_general x4, matrix products, mix_axis(): jnp.einsum(pattern, sine, values[0], precision=transform_mode)  2.7 us
    dot_general x4, matrix products, mix_axis(): jnp.einsum(pattern, cosine, values[0], precision=transform_mode)  2.68 us
    dot_general x4, matrix products, mix_axis(): jnp.einsum(pattern, sine, values[1], precision=transform_mode)  2.6 us
  transfers between devices with their start and end apart: 3, of which 3 were waited for; matrix products, arithmetic and copies ran while one was open for 6% of the time, Pallas kernels for 0%

profile of v1, /device:TPU:1, one launch (start us, length us, event | category | flops | bytes accessed | tf_op | source)
XLA Modules:
  0.0 83.0 jit_solution(4114591728855989843)
XLA Ops:
  0.6 0.0 copy-start
  0.6 0.0 copy-start.1
  0.7 0.8 slice.166
  1.4 4.6 %collective-permute-start = (bf16[6,3,256]{2,0,1:T(8,128)(2,1)S(1)}, bf16[6,3,256]{2,0,1:T(8,128)(2,1)S(1)}, u32[]{:S(2)}, u32[]{:S(2)}) collective-permute-start(bf16[6,3,256]{2,0,1:T(8,128)(2,1)S(1)} %slice.166), channel_id=1, source_target_pairs={{0,1},{1,2},{2,3},{3,4},{4,5},{5,6},{6,7},{7,8},{8,9},{9,10},{10,1... | collective-permute-start | bytes 27656 | tf_op jit(solution)/shard_map/ppermute | solution.py:16
  6.0 0.1 convert_multiply_fusion.14
  6.1 0.1 fusion.175
  6.1 0.1 fusion.177
  6.2 0.1 fusion.179
  6.3 0.1 fusion.181
  6.3 0.1 fusion.183
  6.4 0.1 fusion.185
  6.4 0.1 fusion.187
  6.5 0.1 fusion.189
  6.6 0.1 fusion.191
  6.6 0.1 fusion.193
  6.7 0.1 fusion.195
  6.8 0.1 fusion.197
  6.8 0.7 fusion.200
  7.5 1.0 %fusion.199 = (f32[1,3,256]{2,0,1:T(1,128)S(1)}, f32[1,3,256]{2,0,1:T(1,128)S(1)}, f32[1,3,256]{2,0,1:T(1,128)S(1)}, f32[1,3,256]{2,0,1:T(1,128)S(1)}, f32[1,3,2...) fusion(f32[7,3,256]{2,0,1:T(8,128)} %param.8), kind=kLoop, calls=%fused_computation.323 | loop fusion | bytes 43008 | tf_op jit(solution)/shard_map/slice | solution.py:127
  8.6 0.1 stack.34
  8.7 1.1 %fusion.7 = f32[128,64]{0,1:T(8,128)S(1)} fusion(f32[128,33]{0,1:T(8,128)S(1)} %stack.34, f32[33,64]{1,0:T(8,128)} %param.9, f32[64]{0:T(128)} %param.10), kind=kOutput, calls=%fused_computation.19 | convolution fusion | flops 3252224 | bytes 58368 | tf_op jit(solution)/shard_map/dot_general | solution.py:136
  9.8 0.0 copy-done
  9.8 0.3 fusion.6
  10.1 7.4 %collective-permute-done = bf16[6,3,256]{2,0,1:T(8,128)(2,1)S(1)} collective-permute-done((bf16[6,3,256]{2,0,1:T(8,128)(2,1)S(1)}, bf16[6,3,256]{2,0,1:T(8,128)(2,1)S(1)}, u32[]{:S(2)}, u32[]{:S(2)}) %collective-permute-start) | collective-permute-done | bytes 9248 | tf_op jit(solution)/shard_map/ppermute | solution.py:16
  17.5 2.3 %multiply_add_fusion.2 = f32[128,3,256]{2,0,1:T(8,128)S(1)} fusion(bf16[128,3,256]{2,0,1:T(8,128)(2,1)} %param.7, bf16[6,3,256]{2,0,1:T(8,128)(2,1)S(1)} %collective-permute-done, f32[3,256]{1,0:T(4,128)S(1)} %get-tuple-element.35, f32[3,256]{1,0:T(4,128)S(1)} %get-tuple-element.36, f32[3,256]{1,0:T(4,128)S(1)} %get-tuple-element.37, ...), kind=kLoop, calls=%fused_computation.54 | loop fusion | flops 3735552 | bytes 620544 | tf_op jit(solution)/shard_map/add | solution.py:127
  19.8 0.0 copy-done.1
  19.9 1.0 %copy.38 = f32[3,256,1,128]{3,2,0,1:T(1,128)} copy(f32[3,256,1,128]{1,3,0,2:T(8,128)S(1)} %maximum_bitcast_fusion) | data formatting | bytes 786432 | tf_op jit(solution)/shard_map/broadcast_in_dim | solution.py:89
  20.9 7.7 %all-to-all-start = ((f32[3,256,1,128]{3,2,0,1:T(1,128)}), f32[3,256,1,128]{3,2,0,1:T(1,128)S(1)}, u32[]{:S(2)}, u32[]{:S(2)}) async-start(f32[3,256,1,128]{3,2,0,1:T(1,128)} %copy.38), calls=%async_computation | async-start | bytes 786432 | tf_op jit(solution)/shard_map/all_to_all | solution.py:88
  28.6 0.1 multiply_sine_fusion.9
  28.8 0.1 multiply_sine_fusion.8
  28.9 0.3 multiply_cosine_fusion.6
  29.3 13.9 %all-to-all-done = f32[3,256,1,128]{3,2,0,1:T(1,128)S(1)} async-done(((f32[3,256,1,128]{3,2,0,1:T(1,128)}), f32[3,256,1,128]{3,2,0,1:T(1,128)S(1)}, u32[]{:S(2)}, u32[]{:S(2)}) %all-to-all-start) | async-done | bytes 393248 | tf_op jit(solution)/shard_map/all_to_all | solution.py:88
  43.3 0.1 slice_bitcast_fusion.14
  43.3 0.5 fusion.17
  43.9 0.5 fusion.19
  44.5 0.6 fusion.5
  45.1 0.6 fusion.4
  45.7 0.7 fusion.21
  46.4 0.7 fusion.22
  47.2 0.7 fusion.3
  47.9 0.7 fusion.2
  48.7 0.1 multiply_add_fusion.5
  48.8 0.1 multiply_subtract_fusion.4
  48.9 0.2 maximum_maximum_fusion
  49.1 0.7 fusion.8
  49.8 0.7 fusion.9
  50.6 0.7 convolution_subtract_fusion.1
  51.3 0.7 convolution_add_fusion.1
  52.0 0.6 fusion.23
  52.6 0.6 fusion.24
  53.3 0.6 fusion.1
  53.9 0.6 fusion
  54.6 0.2 maximum_multiply_fusion
  54.8 0.1 fusion.198
  54.8 0.1 subtract_multiply_fusion
  54.9 0.3 copy.41
  55.2 20.6 %all_to_all.30 = f32[3,4,64,128]{3,1,0,2:T(4,128)S(1)} all-to-all(f32[3,4,64,128]{3,1,0,2:T(4,128)S(1)} %copy.41), channel_id=1, replica_groups=mesh['outer'=16,'inner'=64] {'inner'}, dimensions={2} | all-to-all | bytes 786432 | tf_op jit(solution)/shard_map/all_to_all | solution.py:94
  75.8 0.1 copy.42
  75.9 0.2 copy.43
  76.1 0.7 fusion.33
  76.8 2.3 %collective-permute-start.1 = (f32[6,3,256]{2,0,1:T(8,128)S(1)}, f32[6,3,256]{2,0,1:T(8,128)S(1)}, u32[]{:S(2)}, u32[]{:S(2)}) collective-permute-start(f32[6,3,256]{2,0,1:T(8,128)S(1)} %slice.234), channel_id=1, source_target_pairs={{1,0},{2,1},{3,2},{4,3},{5,4},{6,5},{7,6},{8,7},{9,8},{10,9},{11,1... | collective-permute-start | bytes 55304 | tf_op jit(solution)/shard_map/ppermute | solution.py:16
  79.1 0.7 fusion.34
  79.8 2.2 %collective-permute-done.1 = f32[6,3,256]{2,0,1:T(8,128)S(1)} collective-permute-done((f32[6,3,256]{2,0,1:T(8,128)S(1)}, f32[6,3,256]{2,0,1:T(8,128)S(1)}, u32[]{:S(2)}, u32[]{:S(2)}) %collective-permute-start.1) | collective-permute-done | bytes 18464 | tf_op jit(solution)/shard_map/ppermute | solution.py:16
  82.0 1.0 %fusion.11 = bf16[128,3,256]{2,0,1:T(8,128)(2,1)} fusion(f32[134,3,256]{2,0,1:T(8,128)S(1)} %pad_maximum_fusion.3, f32[3,256]{1,0:T(4,128)S(1)} %get-tuple-element.35, f32[3,256]{1,0:T(4,128)S(1)} %get-tuple-element.36, f32[3,256]{1,0:T(4,128)S(1)} %get-tuple-element.37, f32[3,256]{1,0:T(4,128)S(1)} %get-tuple-element.38, ...), kind=kLoop, calls=%fused_computation.37 | loop fusion | flops 1572864 | bytes 2970624 | tf_op jit(solution)/shard_map/convert_element_type | solution.py:170
  (17 shorter events, 0.3 us)
Async XLA Ops:
  0.6 9.2 %copy-start = (f32[64,256]{1,0:T(8,128)S(1)}, f32[64,256]{1,0:T(8,128)}, u32[]{:S(2)}) copy-start(f32[64,256]{1,0:T(8,128)} %param.11) | copy-start | bytes 196612
  0.6 19.2 %copy-start.1 = (bf16[128,256]{1,0:T(8,128)(2,1)S(1)}, bf16[128,256]{1,0:T(8,128)(2,1)}, u32[]{:S(2)}) copy-start(bf16[128,256]{1,0:T(8,128)(2,1)} %param.13) | copy-start | bytes 196612
  1.4 16.1 %collective-permute-start = (bf16[6,3,256]{2,0,1:T(8,128)(2,1)S(1)}, bf16[6,3,256]{2,0,1:T(8,128)(2,1)S(1)}, u32[]{:S(2)}, u32[]{:S(2)}) collective-permute-start(bf16[6,3,256]{2,0,1:T(8,128)(2,1)S(1)} %slice.166), channel_id=1, source_target_pairs={{0,1},{1,2},{2,3},{3,4},{4,5},{5,6},{6,7},{7,8},{8,9},{9,10},{10,1... | collective-permute-start | bytes 27656 | tf_op jit(solution)/shard_map/ppermute | solution.py:16
  20.9 22.3 %all-to-all-start = ((f32[3,256,1,128]{3,2,0,1:T(1,128)}), f32[3,256,1,128]{3,2,0,1:T(1,128)S(1)}, u32[]{:S(2)}, u32[]{:S(2)}) async-start(f32[3,256,1,128]{3,2,0,1:T(1,128)} %copy.38), calls=%async_computation | async-start | bytes 786432 | tf_op jit(solution)/shard_map/all_to_all | solution.py:88
  76.8 5.1 %collective-permute-start.1 = (f32[6,3,256]{2,0,1:T(8,128)S(1)}, f32[6,3,256]{2,0,1:T(8,128)S(1)}, u32[]{:S(2)}, u32[]{:S(2)}) collective-permute-start(f32[6,3,256]{2,0,1:T(8,128)S(1)} %slice.234), channel_id=1, source_target_pairs={{1,0},{2,1},{3,2},{4,3},{5,4},{6,5},{7,6},{8,7},{9,8},{10,9},{11,1... | collective-permute-start | bytes 55304 | tf_op jit(solution)/shard_map/ppermute | solution.py:16

commit v2 on v1

--- a/solution.py
+++ b/solution.py
@@ -71,17 +71,23 @@
 
 
 def inverse_padded(spectrum):
+    half = spectrum.shape[2] // 2
+    first = spectrum[:, :, :half]
+    second = spectrum[:, :, half:]
+    joined = jnp.stack([first[0] - second[1], first[1] + second[0]])
     parts = spectrum.shape[3]
     length = spectrum.shape[4]
     seq_total = parts * length
-    values = mix_axis(spectrum, length, 1.0, "jb,hrab->hraj")
+    values = mix_axis(joined, length, 1.0, "jb,hrab->hraj")
     index_a = jnp.arange(parts, dtype=jnp.int32)[:, None]
     index_j = jnp.arange(length, dtype=jnp.int32)[None, :]
     cosine, sine = turning(index_a * index_j, seq_total, 1.0)
     values = rotate(values, cosine, sine)
     values = mix_axis(values, parts, 1.0, "pa,hraj->hrpj") / seq_total
     cosine, sine = turning(grid_places(parts, length), 2 * seq_total, 1.0)
-    return 0.5 * (values[0, 0] + values[0, 1] * cosine - values[1, 1] * sine)
+    real_part = 0.5 * (values[0, 0] + values[0, 1] * cosine - values[1, 1] * sine)
+    other_part = 0.5 * (values[1, 0] + values[0, 1] * sine + values[1, 1] * cosine)
+    return jnp.concatenate([real_part, other_part], axis=0)
 
 
 def to_channels(stacked):
@@ -154,7 +160,18 @@
         ],
         axis=2,
     )
-    returned = inverse_padded(paired)
+    spread = slices // 2
+    ordered = jnp.concatenate(
+        [paired[:, :, : slices], paired[:, :, 2 * slices : 2 * slices + spread],
+         paired[:, :, slices : 2 * slices], paired[:, :, 2 * slices + spread :]],
+        axis=2,
+    )
+    returned = inverse_padded(ordered)
+    returned = jnp.concatenate(
+        [returned[:slices], returned[slices + spread : 2 * slices + spread],
+         returned[slices : slices + spread], returned[2 * slices + spread :]],
+        axis=0,
+    )
     back = to_positions(returned.reshape(3, slices, parts, length))
     conv = back[0]
     grad_product = back[1]

time: 83.5 us -> 80.3 us (0.962)
  other arithmetic: 7.65 us -> 4.95 us
  matrix products: 12 us -> 10 us
  waiting for transfers between devices: 23.4 us -> 24.7 us
  local copies, waits for them, and re-layouts: 3.61 us -> 4.65 us
  starting transfers between devices: 14.6 us -> 13.7 us
    unnamed x8 -> x18, local copies, waits for them, and re-layouts: 0.03 us -> 2.12 us
    add x1, other arithmetic: 2.31 us -> 0.35 us  [body(): mixed + short_weight[offset] * extended[taps - 1 - offset:taps - 1 - offs...]
    ppermute x2, waiting for transfers between devices: 9.53 us -> 10.6 us  [passed_along(): return lax.ppermute(value, axis, pairs)]
    all_to_all x1, starting transfers between devices: 7.73 us -> 6.67 us  [to_channels(): lax.all_to_all(jnp.swapaxes(stacked, 1, 2)[:, :, None, :], 'inner', split...]
    slice x1, local copies, waits for them, and re-layouts: 1.02 us -> 0.02 us  [body(): short_weight[offset]]
  transfers between devices with their start and end apart: 3 -> 3, of which waited for: 3 -> 3; matrix products, arithmetic and copies ran while one was open for 6% -> 4% of each run, Pallas kernels for 0% -> 0%
where the time goes in v2:
time: 80.3 us; the launch traced here: 79.8 us
  waiting for transfers between devices  24.7 us (31%)
  blocking collectives  20.6 us (26%)
  starting transfers between devices  13.7 us (17%)
  matrix products  10 us (12%)
  other arithmetic  4.95 us (6%)
  local copies, waits for them, and re-layouts  4.65 us (6%)
  between operations  1.17 us (1%)
    all_to_all x1, blocking collectives, to_positions(): lax.all_to_all(values, 'inner', split_axis=2, concat_axis=1, tiled=True)  20.6 us
    all_to_all x1, waiting for transfers between devices, to_channels(): lax.all_to_all(jnp.swapaxes(stacked, 1, 2)[:, :, None, :], 'inner', split...  14.1 us
    ppermute x2, waiting for transfers between devices, passed_along(): return lax.ppermute(value, axis, pairs)  10.6 us
    ppermute x2, starting transfers between devices, passed_along(): return lax.ppermute(value, axis, pairs)  7.02 us
    all_to_all x1, starting transfers between devices, to_channels(): lax.all_to_all(jnp.swapaxes(stacked, 1, 2)[:, :, None, :], 'inner', split...  6.67 us
    dot_general x4, matrix products, mix_axis(): jnp.einsum(pattern, sine, values[0], precision=transform_mode)  2.39 us
    dot_general x4, matrix products, mix_axis(): jnp.einsum(pattern, cosine, values[0], precision=transform_mode)  2.38 us
    dot_general x4, matrix products, mix_axis(): jnp.einsum(pattern, sine, values[1], precision=transform_mode)  2.3 us
  transfers between devices with their start and end apart: 3, of which 3 were waited for; matrix products, arithmetic and copies ran while one was open for 4% of the time, Pallas kernels for 0%

profile of v2, /device:TPU:1, one launch (start us, length us, event | category | flops | bytes accessed | tf_op | source)
XLA Modules:
  0.0 79.8 jit_solution(1830285434718852727)
XLA Ops:
  0.6 0.0 copy-start
  0.6 0.7 slice.199
  1.4 4.7 %collective-permute-start = (bf16[6,3,256]{2,0,1:T(8,128)(2,1)S(1)}, bf16[6,3,256]{2,0,1:T(8,128)(2,1)S(1)}, u32[]{:S(2)}, u32[]{:S(2)}) collective-permute-start(bf16[6,3,256]{2,0,1:T(8,128)(2,1)S(1)} %slice.199), channel_id=1, source_target_pairs={{0,1},{1,2},{2,3},{3,4},{4,5},{5,6},{6,7},{7,8},{8,9},{9,10},{10,1... | collective-permute-start | bytes 27656 | tf_op jit(solution)/shard_map/ppermute | solution.py:16
  6.1 0.1 convert_multiply_fusion.14
  6.2 0.1 fusion.189
  6.2 0.1 fusion.191
  6.3 0.1 fusion.193
  6.4 0.1 fusion.195
  6.4 0.1 fusion.197
  6.5 0.1 fusion.199
  6.6 0.1 fusion.201
  6.6 0.1 fusion.203
  6.7 0.1 fusion.205
  6.8 0.1 fusion.207
  6.8 0.1 fusion.209
  6.9 0.1 fusion.211
  7.0 0.7 copy-done.4
  7.7 0.0 copy-start.5
  7.7 0.0 copy-start.6
  7.7 0.1 stack.34
  7.8 0.6 copy-done.5
  8.5 0.4 fusion.7
  8.8 0.3 fusion.6
  9.1 8.5 %collective-permute-done = bf16[6,3,256]{2,0,1:T(8,128)(2,1)S(1)} collective-permute-done((bf16[6,3,256]{2,0,1:T(8,128)(2,1)S(1)}, bf16[6,3,256]{2,0,1:T(8,128)(2,1)S(1)}, u32[]{:S(2)}, u32[]{:S(2)}) %collective-permute-start) | collective-permute-done | bytes 9248 | tf_op jit(solution)/shard_map/ppermute | solution.py:16
  17.6 0.4 multiply_add_fusion.2
  18.0 0.8 %copy-done.1 = bf16[128,256]{1,0:T(8,128)(2,1)S(1)} copy-done((bf16[128,256]{1,0:T(8,128)(2,1)S(1)}, bf16[128,256]{1,0:T(8,128)(2,1)}, u32[]{:S(2)}) %copy-start.1) | copy-done | bytes 65560
  18.9 1.0 %copy.22 = f32[3,256,1,128]{3,2,0,1:T(1,128)} copy(f32[3,256,1,128]{1,3,0,2:T(8,128)S(1)} %maximum_bitcast_fusion) | data formatting | bytes 786432 | tf_op jit(solution)/shard_map/broadcast_in_dim | solution.py:95
  19.9 6.7 %all-to-all-start = ((f32[3,256,1,128]{3,2,0,1:T(1,128)}), f32[3,256,1,128]{3,2,0,1:T(1,128)S(1)}, u32[]{:S(2)}, u32[]{:S(2)}) async-start(f32[3,256,1,128]{3,2,0,1:T(1,128)} %copy.22), calls=%async_computation | async-start | bytes 786432 | tf_op jit(solution)/shard_map/all_to_all | solution.py:94
  26.6 0.1 multiply_sine_fusion.9
  26.7 0.1 multiply_sine_fusion.8
  26.9 0.3 multiply_cosine_fusion.6
  27.2 14.1 %all-to-all-done = f32[3,256,1,128]{3,2,0,1:T(1,128)S(1)} async-done(((f32[3,256,1,128]{3,2,0,1:T(1,128)}), f32[3,256,1,128]{3,2,0,1:T(1,128)S(1)}, u32[]{:S(2)}, u32[]{:S(2)}) %all-to-all-start) | async-done | bytes 393248 | tf_op jit(solution)/shard_map/all_to_all | solution.py:94
  41.3 0.1 slice_bitcast_fusion.12
  41.4 0.5 fusion.18
  41.9 0.5 fusion.20
  42.5 0.6 fusion.3
  43.2 0.6 fusion.2
  43.8 0.7 fusion.23
  44.5 0.7 fusion.24
  45.2 0.7 fusion.1
  46.0 0.7 fusion
  46.7 0.1 multiply_add_fusion.5
  46.9 0.2 multiply_subtract_fusion.4
  47.1 0.1 fusion.8
  47.2 0.1 pad_maximum_fusion.1
  47.2 0.6 fusion.42
  47.8 0.6 fusion.44
  48.4 0.6 convolution_subtract_fusion.3
  48.9 0.6 convolution_add_fusion.3
  49.5 0.5 fusion.49
  50.0 0.5 fusion.50
  50.5 0.5 fusion.5
  51.0 0.5 fusion.4
  51.5 0.1 maximum_multiply_fusion
  51.6 0.1 fusion.35
  51.7 0.3 copy.25
  52.0 20.6 %all_to_all.30 = f32[3,4,64,128]{3,1,0,2:T(4,128)S(1)} all-to-all(f32[3,4,64,128]{3,1,0,2:T(4,128)S(1)} %copy.25), channel_id=1, replica_groups=mesh['outer'=16,'inner'=64] {'inner'}, dimensions={2} | all-to-all | bytes 786432 | tf_op jit(solution)/shard_map/all_to_all | solution.py:100
  72.6 0.1 copy.26
  72.7 0.2 copy.27
  72.9 0.7 fusion.39
  73.6 2.3 %collective-permute-start.1 = (f32[6,3,256]{2,0,1:T(8,128)S(1)}, f32[6,3,256]{2,0,1:T(8,128)S(1)}, u32[]{:S(2)}, u32[]{:S(2)}) collective-permute-start(f32[6,3,256]{2,0,1:T(8,128)S(1)} %slice.285), channel_id=1, source_target_pairs={{1,0},{2,1},{3,2},{4,3},{5,4},{6,5},{7,6},{8,7},{9,8},{10,9},{11,1... | collective-permute-start | bytes 55304 | tf_op jit(solution)/shard_map/ppermute | solution.py:16
  75.9 0.7 fusion.40
  76.6 2.2 %collective-permute-done.1 = f32[6,3,256]{2,0,1:T(8,128)S(1)} collective-permute-done((f32[6,3,256]{2,0,1:T(8,128)S(1)}, f32[6,3,256]{2,0,1:T(8,128)S(1)}, u32[]{:S(2)}, u32[]{:S(2)}) %collective-permute-start.1) | collective-permute-done | bytes 18464 | tf_op jit(solution)/shard_map/ppermute | solution.py:16
  78.8 1.0 %fusion.10 = bf16[128,3,256]{2,0,1:T(8,128)(2,1)} fusion(f32[134,3,256]{2,0,1:T(8,128)S(1)} %pad_maximum_fusion.4, f32[3,256]{1,0:T(4,128)S(1)} %get-tuple-element.34, f32[3,256]{1,0:T(4,128)S(1)} %get-tuple-element.35, f32[3,256]{1,0:T(4,128)S(1)} %get-tuple-element.36, f32[3,256]{1,0:T(4,128)S(1)} %get-tuple-element.37, ...), kind=kLoop, calls=%fused_computation.36 | loop fusion | flops 1572864 | bytes 2970624 | tf_op jit(solution)/shard_map/convert_element_type | solution.py:187
  (33 shorter events, 0.4 us)
Async XLA Ops:
  0.6 8.2 %copy-start = (f32[64,256]{1,0:T(8,128)S(1)}, f32[64,256]{1,0:T(8,128)}, u32[]{:S(2)}) copy-start(f32[64,256]{1,0:T(8,128)} %param.11) | copy-start | bytes 196612
  1.4 6.3 %copy-start.3 = (f32[7,3,256]{2,0,1:T(8,128)S(1)}, f32[7,3,256]{2,0,1:T(8,128)}, u32[]{:S(2)}) copy-start(f32[7,3,256]{2,0,1:T(8,128)} %param.8) | copy-start | bytes 64516
  1.4 16.2 %collective-permute-start = (bf16[6,3,256]{2,0,1:T(8,128)(2,1)S(1)}, bf16[6,3,256]{2,0,1:T(8,128)(2,1)S(1)}, u32[]{:S(2)}, u32[]{:S(2)}) collective-permute-start(bf16[6,3,256]{2,0,1:T(8,128)(2,1)S(1)} %slice.199), channel_id=1, source_target_pairs={{0,1},{1,2},{2,3},{3,4},{4,5},{5,6},{6,7},{7,8},{8,9},{9,10},{10,1... | collective-permute-start | bytes 27656 | tf_op jit(solution)/shard_map/ppermute | solution.py:16
  6.9 0.7 copy-start.4
  7.7 0.7 copy-start.5
  7.7 0.7 copy-start.6
  8.4 9.2 %copy-start.2 = (bf16[128,3,256]{2,0,1:T(8,128)(2,1)S(1)}, bf16[128,3,256]{2,0,1:T(8,128)(2,1)}, u32[]{:S(2)}) copy-start(bf16[128,3,256]{2,0,1:T(8,128)(2,1)} %param.7) | copy-start | bytes 589828
  18.0 0.8 %copy-start.1 = (bf16[128,256]{1,0:T(8,128)(2,1)S(1)}, bf16[128,256]{1,0:T(8,128)(2,1)}, u32[]{:S(2)}) copy-start(bf16[128,256]{1,0:T(8,128)(2,1)} %param.13) | copy-start | bytes 196612
  19.9 21.4 %all-to-all-start = ((f32[3,256,1,128]{3,2,0,1:T(1,128)}), f32[3,256,1,128]{3,2,0,1:T(1,128)S(1)}, u32[]{:S(2)}, u32[]{:S(2)}) async-start(f32[3,256,1,128]{3,2,0,1:T(1,128)} %copy.22), calls=%async_computation | async-start | bytes 786432 | tf_op jit(solution)/shard_map/all_to_all | solution.py:94
  73.6 5.1 %collective-permute-start.1 = (f32[6,3,256]{2,0,1:T(8,128)S(1)}, f32[6,3,256]{2,0,1:T(8,128)S(1)}, u32[]{:S(2)}, u32[]{:S(2)}) collective-permute-start(f32[6,3,256]{2,0,1:T(8,128)S(1)} %slice.285), channel_id=1, source_target_pairs={{1,0},{2,1},{3,2},{4,3},{5,4},{6,5},{7,6},{8,7},{9,8},{10,9},{11,1... | collective-permute-start | bytes 55304 | tf_op jit(solution)/shard_map/ppermute | solution.py:16

commit v3 on v2

--- a/solution.py
+++ b/solution.py
@@ -54,20 +54,32 @@
     )
 
 
-def forward_padded(signal):
-    parts = signal.shape[1]
-    length = signal.shape[2]
+def forward_padded(first, second):
+    parts = first.shape[1]
+    length = first.shape[2]
     seq_total = parts * length
     cosine, sine = turning(grid_places(parts, length), 2 * seq_total, -1.0)
     values = jnp.stack(
-        [jnp.stack([signal, signal * cosine]), jnp.stack([jnp.zeros_like(signal), signal * sine])]
+        [
+            jnp.stack([first, first * cosine - second * sine]),
+            jnp.stack([second, first * sine + second * cosine]),
+        ]
     )
     values = mix_axis(values, parts, -1.0, "ap,hrpj->hraj")
     index_a = jnp.arange(parts, dtype=jnp.int32)[:, None]
     index_j = jnp.arange(length, dtype=jnp.int32)[None, :]
     cosine, sine = turning(index_a * index_j, seq_total, -1.0)
     values = rotate(values, cosine, sine)
-    return mix_axis(values, length, -1.0, "bj,hraj->hrab")
+    spectrum = mix_axis(values, length, -1.0, "bj,hraj->hrab")
+    flipped = jnp.flip(spectrum[:, 0], axis=3)
+    even_back = jnp.concatenate(
+        [jnp.roll(flipped[:, :, :1], 1, axis=3), jnp.flip(flipped[:, :, 1:], axis=2)], axis=2
+    )
+    odd_back = jnp.flip(spectrum[:, 1], axis=(2, 3))
+    mirrored = jnp.stack([even_back, odd_back], axis=1)
+    first_spec = 0.5 * jnp.stack([spectrum[0] + mirrored[0], spectrum[1] - mirrored[1]])
+    second_spec = 0.5 * jnp.stack([spectrum[1] + mirrored[1], mirrored[0] - spectrum[0]])
+    return first_spec, second_spec
 
 
 def inverse_padded(spectrum):
@@ -148,10 +160,14 @@
     signal_rows = moved[0]
     filter_rows = moved[1]
     grad_rows = moved[2]
-    spectra = forward_padded(jnp.concatenate([signal_rows, filter_rows, grad_rows], axis=0))
-    signal_spec = spectra[:, :, :slices]
-    filter_spec = spectra[:, :, slices : 2 * slices]
-    grad_spec = spectra[:, :, 2 * slices :]
+    spread = slices // 2
+    first_spec, second_spec = forward_padded(
+        jnp.concatenate([signal_rows, filter_rows[:spread]], axis=0),
+        jnp.concatenate([grad_rows, filter_rows[spread:]], axis=0),
+    )
+    signal_spec = first_spec[:, :, :slices]
+    filter_spec = jnp.concatenate([first_spec[:, :, slices:], second_spec[:, :, slices:]], axis=2)
+    grad_spec = second_spec[:, :, :slices]
     paired = jnp.concatenate(
         [
             times_complex(signal_spec, filter_spec),
@@ -160,7 +176,6 @@
         ],
         axis=2,
     )
-    spread = slices // 2
     ordered = jnp.concatenate(
         [paired[:, :, : slices], paired[:, :, 2 * slices : 2 * slices + spread],
          paired[:, :, slices : 2 * slices], paired[:, :, 2 * slices + spread :]],

time: 80.3 us -> 80.5 us (level)
  matrix products: 10 us -> 8.92 us
where the time goes in v3:
time: 80.5 us; the launch traced here: 80 us
  waiting for transfers between devices  24.7 us (31%)
  blocking collectives  20.6 us (26%)
  starting transfers between devices  13.7 us (17%)
  matrix products  8.92 us (11%)
  local copies, waits for them, and re-layouts  5.43 us (7%)
  other arithmetic  5.41 us (7%)
  between operations  1.27 us (2%)
    all_to_all x1, blocking collectives, to_positions(): lax.all_to_all(values, 'inner', split_axis=2, concat_axis=1, tiled=True)  20.6 us
    all_to_all x1, waiting for transfers between devices, to_channels(): lax.all_to_all(jnp.swapaxes(stacked, 1, 2)[:, :, None, :], 'inner', split...  14.1 us
    ppermute x2, waiting for transfers between devices, passed_along(): return lax.ppermute(value, axis, pairs)  10.6 us
    ppermute x2, starting transfers between devices, passed_along(): return lax.ppermute(value, axis, pairs)  7.02 us
    all_to_all x1, starting transfers between devices, to_channels(): lax.all_to_all(jnp.swapaxes(stacked, 1, 2)[:, :, None, :], 'inner', split...  6.67 us
    unnamed x18, local copies, waits for them, and re-layouts  2.12 us
    dot_general x4, matrix products, mix_axis(): jnp.einsum(pattern, sine, values[0], precision=transform_mode)  2.07 us
    dot_general x4, matrix products, mix_axis(): jnp.einsum(pattern, sine, values[1], precision=transform_mode)  2.07 us
  transfers between devices with their start and end apart: 3, of which 3 were waited for; matrix products, arithmetic and copies ran while one was open for 4% of the time, Pallas kernels for 0%

profile of v3, /device:TPU:1, one launch (start us, length us, event | category | flops | bytes accessed | tf_op | source)
XLA Modules:
  0.0 80.0 jit_solution(17342715137676859652)
XLA Ops:
  0.6 0.7 slice.242
  1.4 4.7 %collective-permute-start = (bf16[6,3,256]{2,0,1:T(8,128)(2,1)S(1)}, bf16[6,3,256]{2,0,1:T(8,128)(2,1)S(1)}, u32[]{:S(2)}, u32[]{:S(2)}) collective-permute-start(bf16[6,3,256]{2,0,1:T(8,128)(2,1)S(1)} %slice.242), channel_id=1, source_target_pairs={{0,1},{1,2},{2,3},{3,4},{4,5},{5,6},{6,7},{7,8},{8,9},{9,10},{10,1... | collective-permute-start | bytes 27656 | tf_op jit(solution)/shard_map/ppermute | solution.py:16
  6.2 0.1 fusion.190
  6.2 0.1 fusion.192
  6.3 0.1 fusion.194
  6.4 0.1 fusion.196
  6.4 0.1 fusion.198
  6.5 0.1 fusion.200
  6.6 0.1 fusion.202
  6.6 0.1 fusion.204
  6.7 0.1 fusion.206
  6.8 0.1 fusion.208
  6.8 0.1 fusion.210
  7.0 0.7 copy-done.4
  7.7 0.1 stack.56
  7.8 0.6 copy-done.5
  8.5 0.4 fusion.5
  8.8 0.3 fusion.4
  9.1 8.5 %collective-permute-done = bf16[6,3,256]{2,0,1:T(8,128)(2,1)S(1)} collective-permute-done((bf16[6,3,256]{2,0,1:T(8,128)(2,1)S(1)}, bf16[6,3,256]{2,0,1:T(8,128)(2,1)S(1)}, u32[]{:S(2)}, u32[]{:S(2)}) %collective-permute-start) | collective-permute-done | bytes 9248 | tf_op jit(solution)/shard_map/ppermute | solution.py:16
  17.6 0.4 multiply_add_fusion.2
  18.0 0.8 %copy-done.1 = bf16[128,256]{1,0:T(8,128)(2,1)S(1)} copy-done((bf16[128,256]{1,0:T(8,128)(2,1)S(1)}, bf16[128,256]{1,0:T(8,128)(2,1)}, u32[]{:S(2)}) %copy-start.1) | copy-done | bytes 65560
  18.9 1.0 %copy.25 = f32[3,256,1,128]{3,2,0,1:T(1,128)} copy(f32[3,256,1,128]{1,3,0,2:T(8,128)S(1)} %maximum_bitcast_fusion) | data formatting | bytes 786432 | tf_op jit(solution)/shard_map/broadcast_in_dim | solution.py:107
  19.9 6.7 %all-to-all-start = ((f32[3,256,1,128]{3,2,0,1:T(1,128)}), f32[3,256,1,128]{3,2,0,1:T(1,128)S(1)}, u32[]{:S(2)}, u32[]{:S(2)}) async-start(f32[3,256,1,128]{3,2,0,1:T(1,128)} %copy.25), calls=%async_computation | async-start | bytes 786432 | tf_op jit(solution)/shard_map/all_to_all | solution.py:106
  26.6 0.1 multiply_sine_fusion.9
  26.7 0.1 multiply_sine_fusion.8
  26.9 0.3 multiply_cosine_fusion.6
  27.2 14.1 %all-to-all-done = f32[3,256,1,128]{3,2,0,1:T(1,128)S(1)} async-done(((f32[3,256,1,128]{3,2,0,1:T(1,128)}), f32[3,256,1,128]{3,2,0,1:T(1,128)S(1)}, u32[]{:S(2)}, u32[]{:S(2)}) %all-to-all-start) | async-done | bytes 393248 | tf_op jit(solution)/shard_map/all_to_all | solution.py:106
  41.5 0.5 fusion.23
  42.0 0.5 fusion.22
  42.5 0.5 fusion.3
  42.9 0.5 fusion.2
  43.4 0.6 fusion.49
  44.0 0.6 fusion.48
  44.5 0.6 convolution_add_fusion.2
  45.1 0.6 convolution_subtract_fusion.2
  45.7 0.1 fusion.10
  45.8 0.1 slice.323
  45.9 0.4 rev.10
  46.2 0.1 slice.266
  46.3 0.2 rev.11
  46.5 0.1 maximum_bitcast_fusion.1
  46.6 0.2 add_bitcast_fusion.1
  46.8 0.1 maximum_multiply_fusion
  47.0 0.1 multiply_subtract_fusion.4
  47.0 0.3 multiply_subtract_fusion.3
  47.5 0.6 fusion.41
  48.0 0.6 fusion.43
  48.6 0.6 convolution_subtract_fusion.1
  49.2 0.6 convolution_add_fusion.1
  49.7 0.5 fusion.50
  50.2 0.5 fusion.51
  50.7 0.5 fusion.1
  51.2 0.5 fusion
  51.7 0.1 maximum_multiply_fusion.2
  51.8 0.1 fusion.36
  52.0 0.3 copy.29
  52.2 20.6 %all_to_all.30 = f32[3,4,64,128]{3,1,0,2:T(4,128)S(1)} all-to-all(f32[3,4,64,128]{3,1,0,2:T(4,128)S(1)} %copy.29), channel_id=1, replica_groups=mesh['outer'=16,'inner'=64] {'inner'}, dimensions={2} | all-to-all | bytes 786432 | tf_op jit(solution)/shard_map/all_to_all | solution.py:112
  72.9 0.1 copy.30
  72.9 0.2 copy.31
  73.1 0.7 fusion.38
  73.8 2.3 %collective-permute-start.1 = (f32[6,3,256]{2,0,1:T(8,128)S(1)}, f32[6,3,256]{2,0,1:T(8,128)S(1)}, u32[]{:S(2)}, u32[]{:S(2)}) collective-permute-start(f32[6,3,256]{2,0,1:T(8,128)S(1)} %slice.351), channel_id=1, source_target_pairs={{1,0},{2,1},{3,2},{4,3},{5,4},{6,5},{7,6},{8,7},{9,8},{10,9},{11,1... | collective-permute-start | bytes 55304 | tf_op jit(solution)/shard_map/ppermute | solution.py:16
  76.1 0.7 fusion.39
  76.8 2.2 %collective-permute-done.1 = f32[6,3,256]{2,0,1:T(8,128)S(1)} collective-permute-done((f32[6,3,256]{2,0,1:T(8,128)S(1)}, f32[6,3,256]{2,0,1:T(8,128)S(1)}, u32[]{:S(2)}, u32[]{:S(2)}) %collective-permute-start.1) | collective-permute-done | bytes 18464 | tf_op jit(solution)/shard_map/ppermute | solution.py:16
  79.0 1.0 %fusion.12 = bf16[128,3,256]{2,0,1:T(8,128)(2,1)} fusion(f32[134,3,256]{2,0,1:T(8,128)S(1)} %pad_maximum_fusion.1, f32[3,256]{1,0:T(4,128)S(1)} %get-tuple-element.50, f32[3,256]{1,0:T(4,128)S(1)} %get-tuple-element.51, f32[3,256]{1,0:T(4,128)S(1)} %get-tuple-element.52, f32[3,256]{1,0:T(4,128)S(1)} %get-tuple-element.53, ...), kind=kLoop, calls=%fused_computation.43 | loop fusion | flops 1572864 | bytes 2970624 | tf_op jit(solution)/shard_map/convert_element_type | solution.py:202
  (48 shorter events, 0.9 us)
Async XLA Ops:
  0.6 8.2 %copy-start = (f32[64,256]{1,0:T(8,128)S(1)}, f32[64,256]{1,0:T(8,128)}, u32[]{:S(2)}) copy-start(f32[64,256]{1,0:T(8,128)} %param.11) | copy-start | bytes 196612
  1.4 6.3 %copy-start.3 = (f32[7,3,256]{2,0,1:T(8,128)S(1)}, f32[7,3,256]{2,0,1:T(8,128)}, u32[]{:S(2)}) copy-start(f32[7,3,256]{2,0,1:T(8,128)} %param.8) | copy-start | bytes 64516
  1.4 16.2 %collective-permute-start = (bf16[6,3,256]{2,0,1:T(8,128)(2,1)S(1)}, bf16[6,3,256]{2,0,1:T(8,128)(2,1)S(1)}, u32[]{:S(2)}, u32[]{:S(2)}) collective-permute-start(bf16[6,3,256]{2,0,1:T(8,128)(2,1)S(1)} %slice.242), channel_id=1, source_target_pairs={{0,1},{1,2},{2,3},{3,4},{4,5},{5,6},{6,7},{7,8},{8,9},{9,10},{10,1... | collective-permute-start | bytes 27656 | tf_op jit(solution)/shard_map/ppermute | solution.py:16
  6.9 0.7 copy-start.4
  7.7 0.7 copy-start.5
  7.7 0.7 copy-start.6
  8.4 9.2 %copy-start.2 = (bf16[128,3,256]{2,0,1:T(8,128)(2,1)S(1)}, bf16[128,3,256]{2,0,1:T(8,128)(2,1)}, u32[]{:S(2)}) copy-start(bf16[128,3,256]{2,0,1:T(8,128)(2,1)} %param.7) | copy-start | bytes 589828
  18.0 0.8 %copy-start.1 = (bf16[128,256]{1,0:T(8,128)(2,1)S(1)}, bf16[128,256]{1,0:T(8,128)(2,1)}, u32[]{:S(2)}) copy-start(bf16[128,256]{1,0:T(8,128)(2,1)} %param.13) | copy-start | bytes 196612
  19.9 21.4 %all-to-all-start = ((f32[3,256,1,128]{3,2,0,1:T(1,128)}), f32[3,256,1,128]{3,2,0,1:T(1,128)S(1)}, u32[]{:S(2)}, u32[]{:S(2)}) async-start(f32[3,256,1,128]{3,2,0,1:T(1,128)} %copy.25), calls=%async_computation | async-start | bytes 786432 | tf_op jit(solution)/shard_map/all_to_all | solution.py:106
  73.8 5.1 %collective-permute-start.1 = (f32[6,3,256]{2,0,1:T(8,128)S(1)}, f32[6,3,256]{2,0,1:T(8,128)S(1)}, u32[]{:S(2)}, u32[]{:S(2)}) collective-permute-start(f32[6,3,256]{2,0,1:T(8,128)S(1)} %slice.351), channel_id=1, source_target_pairs={{1,0},{2,1},{3,2},{4,3},{5,4},{6,5},{7,6},{8,7},{9,8},{10,9},{11,1... | collective-permute-start | bytes 55304 | tf_op jit(solution)/shard_map/ppermute | solution.py:16

commit v4 on v2

--- a/solution.py
+++ b/solution.py
@@ -38,13 +38,11 @@
 def mix_axis(values, count, direction, pattern):
     index = jnp.arange(count, dtype=jnp.int32)
     cosine, sine = turning(index[:, None] * index[None, :], count, direction)
-    real_part = jnp.einsum(pattern, cosine, values[0], precision=transform_mode) - jnp.einsum(
-        pattern, sine, values[1], precision=transform_mode
-    )
-    other_part = jnp.einsum(pattern, cosine, values[1], precision=transform_mode) + jnp.einsum(
-        pattern, sine, values[0], precision=transform_mode
-    )
-    return jnp.stack([real_part, other_part])
+    matrix = jnp.stack([jnp.stack([cosine, -sine]), jnp.stack([sine, cosine])])
+    pair, result = pattern.split("->")
+    table, operand = pair.split(",")
+    joined = "zy" + table + ",y" + operand + "->z" + result
+    return jnp.einsum(joined, matrix, values, precision=transform_mode)
 
 
 def grid_places(parts, length):

time: 80.3 us -> 78 us (0.971)
  matrix products: 10 us -> 4.07 us
  other arithmetic: 4.95 us -> 9.81 us
  waiting for transfers between devices: 24.7 us -> 21.8 us
  starting transfers between devices: 13.7 us -> 16.4 us
  local copies, waits for them, and re-layouts: 4.65 us -> 3.63 us
    dot_general x16 -> x4, matrix products: 9.35 us -> 2.68 us  [mix_axis(): return jnp.einsum(joined, matrix, values, precision=transform_mode)]
    ppermute x2, waiting for transfers between devices: 10.6 us -> 7.56 us  [passed_along(): return lax.ppermute(value, axis, pairs)]
    all_to_all x1, starting transfers between devices: 6.67 us -> 9.53 us  [to_channels(): lax.all_to_all(jnp.swapaxes(stacked, 1, 2)[:, :, None, :], 'inner', split...]
    unnamed x18 -> x8, local copies, waits for them, and re-layouts: 2.12 us -> 0.03 us
    add x1, other arithmetic: 0.35 us -> 2.31 us  [body(): mixed + short_weight[offset] * extended[taps - 1 - offset:taps - 1 - offs...]
    slice x1, local copies, waits for them, and re-layouts: 0.02 us -> 1.02 us  [body(): short_weight[offset]]
    sin x2 -> x6, other arithmetic: 0.29 us -> 1.13 us  [turning(): return (jnp.cos(angles), jnp.sin(angles))]
    neg x0 -> x4, other arithmetic: none -> 0.81 us  [mix_axis(): matrix = jnp.stack([jnp.stack([cosine, -sine]), jnp.stack([sine, cosine])])]
  transfers between devices with their start and end apart: 3 -> 3, of which waited for: 3 -> 3; matrix products, arithmetic and copies ran while one was open for 4% -> 9% of each run, Pallas kernels for 0% -> 0%
where the time goes in v4:
time: 78 us; the launch traced here: 77.5 us
  waiting for transfers between devices  21.8 us (28%)
  blocking collectives  20.6 us (26%)
  starting transfers between devices  16.4 us (21%)
  other arithmetic  9.81 us (13%)
  matrix products  4.07 us (5%)
  local copies, waits for them, and re-layouts  3.63 us (5%)
  between operations  1.14 us (1%)
    all_to_all x1, blocking collectives, to_positions(): lax.all_to_all(values, 'inner', split_axis=2, concat_axis=1, tiled=True)  20.6 us
    all_to_all x1, waiting for transfers between devices, to_channels(): lax.all_to_all(jnp.swapaxes(stacked, 1, 2)[:, :, None, :], 'inner', split...  14.3 us
    all_to_all x1, starting transfers between devices, to_channels(): lax.all_to_all(jnp.swapaxes(stacked, 1, 2)[:, :, None, :], 'inner', split...  9.53 us
    ppermute x2, waiting for transfers between devices, passed_along(): return lax.ppermute(value, axis, pairs)  7.56 us
    ppermute x2, starting transfers between devices, passed_along(): return lax.ppermute(value, axis, pairs)  6.89 us
    dot_general x4, matrix products, mix_axis(): return jnp.einsum(joined, matrix, values, precision=transform_mode)  2.68 us
    add x1, other arithmetic, body(): mixed + short_weight[offset] * extended[taps - 1 - offset:taps - 1 - offs...  2.31 us
  transfers between devices with their start and end apart: 3, of which 3 were waited for; matrix products, arithmetic and copies ran while one was open for 9% of the time, Pallas kernels for 0%

profile of v4, /device:TPU:1, one launch (start us, length us, event | category | flops | bytes accessed | tf_op | source)
XLA Modules:
  0.0 77.5 jit_solution(521624422874675821)
XLA Ops:
  0.6 0.0 copy-start
  0.6 0.0 copy-start.1
  0.7 0.8 slice.209
  1.4 4.6 %collective-permute-start = (bf16[6,3,256]{2,0,1:T(8,128)(2,1)S(1)}, bf16[6,3,256]{2,0,1:T(8,128)(2,1)S(1)}, u32[]{:S(2)}, u32[]{:S(2)}) collective-permute-start(bf16[6,3,256]{2,0,1:T(8,128)(2,1)S(1)} %slice.209), channel_id=1, source_target_pairs={{0,1},{1,2},{2,3},{3,4},{4,5},{5,6},{6,7},{7,8},{8,9},{9,10},{10,1... | collective-permute-start | bytes 27656 | tf_op jit(solution)/shard_map/ppermute | solution.py:16
  6.0 0.1 convert_multiply_fusion.14
  6.1 0.1 fusion.81
  6.1 0.1 fusion.83
  6.2 0.1 fusion.85
  6.3 0.1 fusion.87
  6.3 0.1 fusion.89
  6.4 0.1 fusion.91
  6.4 0.1 fusion.93
  6.5 0.1 fusion.95
  6.6 0.1 fusion.97
  6.6 0.1 fusion.99
  6.7 0.1 fusion.101
  6.8 0.1 fusion.103
  6.8 0.1 fusion.73
  7.0 0.1 multiply_sine_fusion.6
  7.1 0.1 multiply_sine_fusion.5
  7.3 0.3 fusion.71
  7.6 0.3 multiply_sine_fusion.1
  7.8 0.3 fusion.72
  8.1 0.3 multiply_sine_fusion
  8.4 0.1 multiply_sine_fusion.4
  8.5 0.1 multiply_sine_fusion.3
  8.7 1.0 %fusion.104 = (f32[1,3,256]{2,0,1:T(1,128)S(1)}, f32[1,3,256]{2,0,1:T(1,128)S(1)}, f32[1,3,256]{2,0,1:T(1,128)S(1)}, f32[1,3,256]{2,0,1:T(1,128)S(1)}, f32[1,3,2...) fusion(f32[7,3,256]{2,0,1:T(8,128)} %param.8), kind=kLoop, calls=%fused_computation.261 | loop fusion | bytes 43008 | tf_op jit(solution)/shard_map/slice | solution.py:131
  9.7 0.7 fusion.105
  10.4 0.1 stack.76
  10.5 1.1 %fusion.11 = f32[128,64]{0,1:T(8,128)S(1)} fusion(f32[128,33]{0,1:T(8,128)S(1)} %stack.76, f32[33,64]{1,0:T(8,128)} %param.9, f32[64]{0:T(128)} %param.10), kind=kOutput, calls=%fused_computation.17 | convolution fusion | flops 3252224 | bytes 58368 | tf_op jit(solution)/shard_map/dot_general | solution.py:140
  11.6 0.0 copy-done
  11.6 0.3 fusion.10
  11.9 0.1 fusion.74
  12.1 5.4 %collective-permute-done = bf16[6,3,256]{2,0,1:T(8,128)(2,1)S(1)} collective-permute-done((bf16[6,3,256]{2,0,1:T(8,128)(2,1)S(1)}, bf16[6,3,256]{2,0,1:T(8,128)(2,1)S(1)}, u32[]{:S(2)}, u32[]{:S(2)}) %collective-permute-start) | collective-permute-done | bytes 9248 | tf_op jit(solution)/shard_map/ppermute | solution.py:16
  17.5 2.3 %multiply_add_fusion.2 = f32[128,3,256]{2,0,1:T(8,128)S(1)} fusion(bf16[128,3,256]{2,0,1:T(8,128)(2,1)} %param.7, bf16[6,3,256]{2,0,1:T(8,128)(2,1)S(1)} %collective-permute-done, f32[3,256]{1,0:T(4,128)S(1)} %get-tuple-element.50, f32[3,256]{1,0:T(4,128)S(1)} %get-tuple-element.51, f32[3,256]{1,0:T(4,128)S(1)} %get-tuple-element.52, ...), kind=kLoop, calls=%fused_computation.63 | loop fusion | flops 3735552 | bytes 620544 | tf_op jit(solution)/shard_map/add | solution.py:131
  19.9 1.0 %copy.34 = f32[3,256,1,128]{3,2,0,1:T(1,128)} copy(f32[3,256,1,128]{1,3,0,2:T(8,128)S(1)} %maximum_bitcast_fusion.13) | data formatting | bytes 786432 | tf_op jit(solution)/shard_map/broadcast_in_dim | solution.py:93
  20.9 9.5 %all-to-all-start = ((f32[3,256,1,128]{3,2,0,1:T(1,128)}), f32[3,256,1,128]{3,2,0,1:T(1,128)S(1)}, u32[]{:S(2)}, u32[]{:S(2)}) async-start(f32[3,256,1,128]{3,2,0,1:T(1,128)} %copy.34), calls=%async_computation | async-start | bytes 786432 | tf_op jit(solution)/shard_map/all_to_all | solution.py:92
  30.5 0.3 multiply_cosine_fusion.2
  30.9 14.3 %all-to-all-done = f32[3,256,1,128]{3,2,0,1:T(1,128)S(1)} async-done(((f32[3,256,1,128]{3,2,0,1:T(1,128)}), f32[3,256,1,128]{3,2,0,1:T(1,128)S(1)}, u32[]{:S(2)}, u32[]{:S(2)}) %all-to-all-start) | async-done | bytes 393248 | tf_op jit(solution)/shard_map/all_to_all | solution.py:92
  45.2 0.1 slice_bitcast_fusion.12
  45.3 0.1 fusion.25
  45.4 0.1 pad_bitcast_fusion
  45.5 0.1 maximum_bitcast_fusion.8
  45.6 0.8 %fusion.7 = f32[2,2,12,64,128]{4,3,0,2,1:T(8,128)S(1)} fusion(f32[1,2,12,64,128]{4,3,0,2,1:T(8,128)S(1)} %pad_bitcast_fusion, f32[1,2,12,64,128]{4,3,0,2,1:T(8,128)S(1)} %maximum_bitcast_fusion.8, f32[1,2,64,64]{3,2,1,0:T(8,128)S(1)} %get-tuple-element.36, f32[1,2,64,64]{3,2,1,0:T(8,128)S(1)} %get-tuple-element.35), kind=kOutput, calls=%fused_computation.9 | convolution fusion | flops 302399488 | bytes 3211264 | tf_op jit(solution)/shard_map/zyap,yhrpj->zhraj/dot_general | solution.py:45
  46.4 0.3 multiply_subtract_fusion
  46.7 0.8 %fusion.6 = f32[2,2,12,64,128]{4,3,0,2,1:T(8,128)S(1)} fusion(f32[1,2,12,64,128]{4,3,0,2,1:T(8,128)S(1)} %get-tuple-element.4, f32[1,2,12,64,128]{4,3,0,2,1:T(8,128)S(1)} %get-tuple-element.3, f32[1,2,128,128]{3,2,1,0:T(8,128)S(1)} %get-tuple-element.32, f32[1,2,128,128]{3,2,1,0:T(8,128)S(1)} %get-tuple-element.31), kind=kOutput, calls=%fused_computation.8 | convolution fusion | flops 604438528 | bytes 3407872 | tf_op jit(solution)/shard_map/zybj,yhraj->zhrab/dot_general | solution.py:45
  47.6 0.2 multiply_subtract_fusion.4
  47.8 0.1 multiply_subtract_fusion.2
  47.9 0.1 fusion.12
  47.9 0.1 pad_maximum_fusion
  48.0 0.1 slice_subtract_fusion
  48.1 0.5 convolution_bitcast_fusion.1
  48.6 0.1 multiply_subtract_fusion.1
  48.8 0.5 fusion.9
  49.3 0.1 fusion.41
  49.5 0.3 copy.41
  49.7 20.6 %all_to_all.30 = f32[3,4,64,128]{3,1,0,2:T(4,128)S(1)} all-to-all(f32[3,4,64,128]{3,1,0,2:T(4,128)S(1)} %copy.41), channel_id=1, replica_groups=mesh['outer'=16,'inner'=64] {'inner'}, dimensions={2} | all-to-all | bytes 786432 | tf_op jit(solution)/shard_map/all_to_all | solution.py:98
  70.4 0.1 copy.42
  70.4 0.2 copy.43
  70.6 0.7 fusion.43
  71.3 2.3 %collective-permute-start.1 = (f32[6,3,256]{2,0,1:T(8,128)S(1)}, f32[6,3,256]{2,0,1:T(8,128)S(1)}, u32[]{:S(2)}, u32[]{:S(2)}) collective-permute-start(f32[6,3,256]{2,0,1:T(8,128)S(1)} %slice.303), channel_id=1, source_target_pairs={{1,0},{2,1},{3,2},{4,3},{5,4},{6,5},{7,6},{8,7},{9,8},{10,9},{11,1... | collective-permute-start | bytes 55304 | tf_op jit(solution)/shard_map/ppermute | solution.py:16
  73.6 0.7 fusion.44
  74.3 2.2 %collective-permute-done.1 = f32[6,3,256]{2,0,1:T(8,128)S(1)} collective-permute-done((f32[6,3,256]{2,0,1:T(8,128)S(1)}, f32[6,3,256]{2,0,1:T(8,128)S(1)}, u32[]{:S(2)}, u32[]{:S(2)}) %collective-permute-start.1) | collective-permute-done | bytes 18464 | tf_op jit(solution)/shard_map/ppermute | solution.py:16
  76.5 1.0 %fusion.18 = bf16[128,3,256]{2,0,1:T(8,128)(2,1)} fusion(f32[134,3,256]{2,0,1:T(8,128)S(1)} %pad_maximum_fusion.1, f32[3,256]{1,0:T(4,128)S(1)} %get-tuple-element.50, f32[3,256]{1,0:T(4,128)S(1)} %get-tuple-element.51, f32[3,256]{1,0:T(4,128)S(1)} %get-tuple-element.52, f32[3,256]{1,0:T(4,128)S(1)} %get-tuple-element.53, ...), kind=kLoop, calls=%fused_computation.42 | loop fusion | flops 1572864 | bytes 2970624 | tf_op jit(solution)/shard_map/convert_element_type | solution.py:185
  (27 shorter events, 0.4 us)
Async XLA Ops:
  0.6 11.0 %copy-start = (f32[64,256]{1,0:T(8,128)S(1)}, f32[64,256]{1,0:T(8,128)}, u32[]{:S(2)}) copy-start(f32[64,256]{1,0:T(8,128)} %param.11) | copy-start | bytes 196612
  0.6 19.2 %copy-start.1 = (bf16[128,256]{1,0:T(8,128)(2,1)S(1)}, bf16[128,256]{1,0:T(8,128)(2,1)}, u32[]{:S(2)}) copy-start(bf16[128,256]{1,0:T(8,128)(2,1)} %param.13) | copy-start | bytes 196612
  1.4 16.1 %collective-permute-start = (bf16[6,3,256]{2,0,1:T(8,128)(2,1)S(1)}, bf16[6,3,256]{2,0,1:T(8,128)(2,1)S(1)}, u32[]{:S(2)}, u32[]{:S(2)}) collective-permute-start(bf16[6,3,256]{2,0,1:T(8,128)(2,1)S(1)} %slice.209), channel_id=1, source_target_pairs={{0,1},{1,2},{2,3},{3,4},{4,5},{5,6},{6,7},{7,8},{8,9},{9,10},{10,1... | collective-permute-start | bytes 27656 | tf_op jit(solution)/shard_map/ppermute | solution.py:16
  20.9 24.3 %all-to-all-start = ((f32[3,256,1,128]{3,2,0,1:T(1,128)}), f32[3,256,1,128]{3,2,0,1:T(1,128)S(1)}, u32[]{:S(2)}, u32[]{:S(2)}) async-start(f32[3,256,1,128]{3,2,0,1:T(1,128)} %copy.34), calls=%async_computation | async-start | bytes 786432 | tf_op jit(solution)/shard_map/all_to_all | solution.py:92
  71.3 5.1 %collective-permute-start.1 = (f32[6,3,256]{2,0,1:T(8,128)S(1)}, f32[6,3,256]{2,0,1:T(8,128)S(1)}, u32[]{:S(2)}, u32[]{:S(2)}) collective-permute-start(f32[6,3,256]{2,0,1:T(8,128)S(1)} %slice.303), channel_id=1, source_target_pairs={{1,0},{2,1},{3,2},{4,3},{5,4},{6,5},{7,6},{8,7},{9,8},{10,9},{11,1... | collective-permute-start | bytes 55304 | tf_op jit(solution)/shard_map/ppermute | solution.py:16

commit v5 on v4

--- a/solution.py
+++ b/solution.py
@@ -1,6 +1,7 @@
 import math
 
 import jax
+import numpy as np
 import jax.numpy as jnp
 from jax import lax
 from jax.sharding import PartitionSpec as P
@@ -17,8 +18,8 @@
 
 
 def turning(numbers, period, direction):
-    angles = direction * full_turn / period * (numbers % period).astype(jnp.float32)
-    return (jnp.cos(angles), jnp.sin(angles))
+    angles = direction * full_turn / period * (numbers % period).astype(np.float64)
+    return (jnp.asarray(np.cos(angles), jnp.float32), jnp.asarray(np.sin(angles), jnp.float32))
 
 
 def rotate(values, cosine, sine):
@@ -36,7 +37,7 @@
 
 
 def mix_axis(values, count, direction, pattern):
-    index = jnp.arange(count, dtype=jnp.int32)
+    index = np.arange(count, dtype=np.int64)
     cosine, sine = turning(index[:, None] * index[None, :], count, direction)
     matrix = jnp.stack([jnp.stack([cosine, -sine]), jnp.stack([sine, cosine])])
     pair, result = pattern.split("->")
@@ -47,8 +48,8 @@
 
 def grid_places(parts, length):
     return (
-        jnp.arange(parts, dtype=jnp.int32)[:, None] * length
-        + jnp.arange(length, dtype=jnp.int32)[None, :]
+        np.arange(parts, dtype=np.int64)[:, None] * length
+        + np.arange(length, dtype=np.int64)[None, :]
     )
 
 
@@ -61,8 +62,8 @@
         [jnp.stack([signal, signal * cosine]), jnp.stack([jnp.zeros_like(signal), signal * sine])]
     )
     values = mix_axis(values, parts, -1.0, "ap,hrpj->hraj")
-    index_a = jnp.arange(parts, dtype=jnp.int32)[:, None]
-    index_j = jnp.arange(length, dtype=jnp.int32)[None, :]
+    index_a = np.arange(parts, dtype=np.int64)[:, None]
+    index_j = np.arange(length, dtype=np.int64)[None, :]
     cosine, sine = turning(index_a * index_j, seq_total, -1.0)
     values = rotate(values, cosine, sine)
     return mix_axis(values, length, -1.0, "bj,hraj->hrab")
@@ -77,8 +78,8 @@
     length = spectrum.shape[4]
     seq_total = parts * length
     values = mix_axis(joined, length, 1.0, "jb,hrab->hraj")
-    index_a = jnp.arange(parts, dtype=jnp.int32)[:, None]
-    index_j = jnp.arange(length, dtype=jnp.int32)[None, :]
+    index_a = np.arange(parts, dtype=np.int64)[:, None]
+    index_j = np.arange(length, dtype=np.int64)[None, :]
     cosine, sine = turning(index_a * index_j, seq_total, 1.0)
     values = rotate(values, cosine, sine)
     values = mix_axis(values, parts, 1.0, "pa,hraj->hrpj") / seq_total

time: 78 us -> 77.8 us (level)
  blocking collectives: 20.6 us -> 42.1 us
  waiting for transfers between devices: 21.8 us -> 9.53 us
  starting transfers between devices: 16.4 us -> 6.89 us
  local copies, waits for them, and re-layouts: 3.63 us -> 6.08 us
  other arithmetic: 9.81 us -> 7.47 us
    all_to_all x0 -> x1, blocking collectives: none -> 21.5 us  [to_channels(): lax.all_to_all(jnp.swapaxes(stacked, 1, 2)[:, :, None, :], 'inner', split...]
    all_to_all x1 -> x0, waiting for transfers between devices: 14.3 us -> none  [to_channels(): lax.all_to_all(jnp.swapaxes(stacked, 1, 2)[:, :, None, :], 'inner', split...]
    all_to_all x1 -> x0, starting transfers between devices: 9.53 us -> none  [to_channels(): lax.all_to_all(jnp.swapaxes(stacked, 1, 2)[:, :, None, :], 'inner', split...]
    unnamed x8 -> x28, local copies, waits for them, and re-layouts: 0.03 us -> 3.09 us
    ppermute x2, waiting for transfers between devices: 7.56 us -> 9.53 us  [passed_along(): return lax.ppermute(value, axis, pairs)]
    sin x6 -> x0, other arithmetic: 1.13 us -> none  [turning(): return (jnp.cos(angles), jnp.sin(angles))]
    neg x4 -> x0, other arithmetic: 0.81 us -> none  [mix_axis(): matrix = jnp.stack([jnp.stack([cosine, -sine]), jnp.stack([sine, cosine])])]
  transfers between devices with their start and end apart: 3 -> 2, of which waited for: 3 -> 2; matrix products, arithmetic and copies ran while one was open for 9% -> 6% of each run, Pallas kernels for 0% -> 0%
where the time goes in v5:
time: 77.8 us; the launch traced here: 77.2 us
  blocking collectives  42.1 us (54%)
  waiting for transfers between devices  9.53 us (12%)
  other arithmetic  7.47 us (10%)
  starting transfers between devices  6.89 us (9%)
  local copies, waits for them, and re-layouts  6.08 us (8%)
  matrix products  4.06 us (5%)
  between operations  1.13 us (1%)
    all_to_all x1, blocking collectives, to_channels(): lax.all_to_all(jnp.swapaxes(stacked, 1, 2)[:, :, None, :], 'inner', split...  21.5 us
    all_to_all x1, blocking collectives, to_positions(): lax.all_to_all(values, 'inner', split_axis=2, concat_axis=1, tiled=True)  20.6 us
    ppermute x2, waiting for transfers between devices, passed_along(): return lax.ppermute(value, axis, pairs)  9.53 us
    ppermute x2, starting transfers between devices, passed_along(): return lax.ppermute(value, axis, pairs)  6.89 us
    unnamed x28, local copies, waits for them, and re-layouts  3.09 us
    dot_general x4, matrix products, mix_axis(): return jnp.einsum(joined, matrix, values, precision=transform_mode)  2.67 us
    add x1, other arithmetic, body(): mixed + short_weight[offset] * extended[taps - 1 - offset:taps - 1 - offs...  2.31 us
  transfers between devices with their start and end apart: 2, of which 2 were waited for; matrix products, arithmetic and copies ran while one was open for 6% of the time, Pallas kernels for 0%

profile of v5, /device:TPU:1, one launch (start us, length us, event | category | flops | bytes accessed | tf_op | source)
XLA Modules:
  0.0 77.2 jit_solution(13216592622881801056)
XLA Ops:
  0.6 0.0 copy-start
  0.6 0.0 copy-start.2
  0.7 0.8 slice.209
  1.4 4.6 %collective-permute-start = (bf16[6,3,256]{2,0,1:T(8,128)(2,1)S(1)}, bf16[6,3,256]{2,0,1:T(8,128)(2,1)S(1)}, u32[]{:S(2)}, u32[]{:S(2)}) collective-permute-start(bf16[6,3,256]{2,0,1:T(8,128)(2,1)S(1)} %slice.209), channel_id=1, source_target_pairs={{0,1},{1,2},{2,3},{3,4},{4,5},{5,6},{6,7},{7,8},{8,9},{9,10},{10,1... | collective-permute-start | bytes 27656 | tf_op jit(solution)/shard_map/ppermute | solution.py:17
  6.0 0.1 fusion.71
  6.1 0.1 fusion.53
  6.1 0.1 fusion.55
  6.2 0.1 fusion.57
  6.3 0.1 fusion.59
  6.3 0.1 fusion.61
  6.4 0.1 fusion.63
  6.5 0.1 fusion.65
  6.5 0.1 fusion.67
  6.6 0.1 fusion.69
  6.7 0.1 fusion.49
  6.7 0.1 fusion.51
  6.8 0.1 convert_multiply_fusion.14
  6.8 0.7 fusion.73
  7.5 1.0 %fusion.72 = (f32[1,3,256]{2,0,1:T(1,128)S(1)}, f32[1,3,256]{2,0,1:T(1,128)S(1)}, f32[1,3,256]{2,0,1:T(1,128)S(1)}, f32[1,3,256]{2,0,1:T(1,128)S(1)}, f32[1,3,25...) fusion(f32[7,3,256]{2,0,1:T(8,128)} %param.24), kind=kLoop, calls=%fused_computation.188 | loop fusion | bytes 43008 | tf_op jit(solution)/shard_map/slice | solution.py:132
  8.6 0.1 stack.100
  8.7 1.1 %fusion.11 = f32[128,64]{0,1:T(8,128)S(1)} fusion(f32[128,33]{0,1:T(8,128)S(1)} %stack.100, f32[33,64]{1,0:T(8,128)} %param.25, f32[64]{0:T(128)} %param.26), kind=kOutput, calls=%fused_computation.17 | convolution fusion | flops 3252224 | bytes 58368 | tf_op jit(solution)/shard_map/dot_general | solution.py:141
  9.8 0.0 copy-done
  9.8 0.3 fusion.10
  10.1 7.4 %collective-permute-done = bf16[6,3,256]{2,0,1:T(8,128)(2,1)S(1)} collective-permute-done((bf16[6,3,256]{2,0,1:T(8,128)(2,1)S(1)}, bf16[6,3,256]{2,0,1:T(8,128)(2,1)S(1)}, u32[]{:S(2)}, u32[]{:S(2)}) %collective-permute-start) | collective-permute-done | bytes 9248 | tf_op jit(solution)/shard_map/ppermute | solution.py:17
  17.5 2.3 %multiply_add_fusion.2 = f32[128,3,256]{2,0,1:T(8,128)S(1)} fusion(bf16[128,3,256]{2,0,1:T(8,128)(2,1)} %param.23, bf16[6,3,256]{2,0,1:T(8,128)(2,1)S(1)} %collective-permute-done, f32[3,256]{1,0:T(4,128)S(1)} %get-tuple-element.38, f32[3,256]{1,0:T(4,128)S(1)} %get-tuple-element.39, f32[3,256]{1,0:T(4,128)S(1)} %get-tuple-element.40, ...), kind=kLoop, calls=%fused_computation.63 | loop fusion | flops 3735552 | bytes 620544 | tf_op jit(solution)/shard_map/add | solution.py:132
  19.8 0.0 copy-done.2
  19.9 0.4 copy.50
  20.3 21.5 %all_to_all.30 = f32[3,256,1,128]{3,2,0,1:T(1,128)S(1)} all-to-all(f32[3,256,1,128]{3,2,0,1:T(1,128)S(1)} %copy.50), channel_id=1, replica_groups=mesh['outer'=16,'inner'=64] {'inner'}, dimensions={1} | all-to-all | bytes 786432 | tf_op jit(solution)/shard_map/all_to_all | solution.py:93
  41.8 0.1 slice_bitcast_fusion.12
  41.9 0.6 copy-done.6
  42.5 0.0 copy-done.11
  42.5 0.1 fusion.25
  42.6 0.0 copy-start.5
  42.6 0.1 pad_bitcast_fusion
  42.7 0.1 maximum_bitcast_fusion.8
  42.8 0.7 copy-done.5
  43.5 0.8 %fusion.7 = f32[2,2,12,64,128]{4,3,0,2,1:T(8,128)S(1)} fusion(f32[2,2,64,64,1,1]{3,2,1,0,5,4:T(8,128)S(1)} %copy-done.5, f32[1,2,12,64,128]{4,3,0,2,1:T(8,128)S(1)} %pad_bitcast_fusion, f32[1,2,12,64,128]{4,3,0,2,1:T(8,128)S(1)} %maximum_bitcast_fusion.8), kind=kOutput, calls=%fused_computation.9 | convolution fusion | flops 302383104 | bytes 3211264 | tf_op jit(solution)/shard_map/zyap,yhrpj->zhraj/dot_general | solution.py:46
  44.4 0.0 copy-start.3
  44.4 0.3 multiply_subtract_fusion
  44.7 0.6 copy-done.3
  45.3 0.8 %fusion.6 = f32[2,2,12,64,128]{4,3,0,2,1:T(8,128)S(1)} fusion(f32[2,2,128,128,1,1]{3,2,1,0,5,4:T(8,128)S(1)} %copy-done.3, f32[1,2,12,64,128]{4,3,0,2,1:T(8,128)S(1)} %get-tuple-element.4, f32[1,2,12,64,128]{4,3,0,2,1:T(8,128)S(1)} %get-tuple-element.3), kind=kOutput, calls=%fused_computation.8 | convolution fusion | flops 604372992 | bytes 3407872 | tf_op jit(solution)/shard_map/zybj,yhraj->zhrab/dot_general | solution.py:46
  46.1 0.1 multiply_subtract_fusion.2
  46.2 0.2 multiply_subtract_fusion.4
  46.5 0.1 fusion.12
  46.5 0.1 pad_maximum_fusion
  46.6 0.0 copy-start.1
  46.6 0.0 copy-start.10
  46.6 0.1 slice_subtract_fusion
  46.7 0.8 %copy-done.1 = f32[2,2,128,128,1,1]{3,2,1,0,5,4:T(8,128)S(1)} copy-done((f32[2,2,128,128,1,1]{3,2,1,0,5,4:T(8,128)S(1)}, f32[2,2,128,128,1,1]{3,2,1,0,5,4:T(8,128)}, u32[]{:S(2)}) %copy-start.1) | copy-done | bytes 262168
  47.6 0.5 convolution_bitcast_fusion.1
  48.1 0.0 copy-start.9
  48.1 0.1 multiply_subtract_fusion.1
  48.2 0.2 copy-done.7
  48.5 0.5 fusion.9
  49.0 0.1 fusion.37
  49.2 0.3 copy.57
  49.4 20.6 %all_to_all.31 = f32[3,4,64,128]{3,1,0,2:T(4,128)S(1)} all-to-all(f32[3,4,64,128]{3,1,0,2:T(4,128)S(1)} %copy.57), channel_id=1, replica_groups=mesh['outer'=16,'inner'=64] {'inner'}, dimensions={2} | all-to-all | bytes 786432 | tf_op jit(solution)/shard_map/all_to_all | solution.py:99
  70.1 0.1 copy.58
  70.1 0.2 copy.59
  70.3 0.7 fusion.39
  71.0 2.3 %collective-permute-start.1 = (f32[6,3,256]{2,0,1:T(8,128)S(1)}, f32[6,3,256]{2,0,1:T(8,128)S(1)}, u32[]{:S(2)}, u32[]{:S(2)}) collective-permute-start(f32[6,3,256]{2,0,1:T(8,128)S(1)} %slice.303), channel_id=1, source_target_pairs={{1,0},{2,1},{3,2},{4,3},{5,4},{6,5},{7,6},{8,7},{9,8},{10,9},{11,1... | collective-permute-start | bytes 55304 | tf_op jit(solution)/shard_map/ppermute | solution.py:17
  73.3 0.7 fusion.40
  74.0 2.2 %collective-permute-done.1 = f32[6,3,256]{2,0,1:T(8,128)S(1)} collective-permute-done((f32[6,3,256]{2,0,1:T(8,128)S(1)}, f32[6,3,256]{2,0,1:T(8,128)S(1)}, u32[]{:S(2)}, u32[]{:S(2)}) %collective-permute-start.1) | collective-permute-done | bytes 18464 | tf_op jit(solution)/shard_map/ppermute | solution.py:17
  76.2 1.0 %fusion.18 = bf16[128,3,256]{2,0,1:T(8,128)(2,1)} fusion(f32[134,3,256]{2,0,1:T(8,128)S(1)} %pad_maximum_fusion.1, f32[3,256]{1,0:T(4,128)S(1)} %get-tuple-element.38, f32[3,256]{1,0:T(4,128)S(1)} %get-tuple-element.39, f32[3,256]{1,0:T(4,128)S(1)} %get-tuple-element.40, f32[3,256]{1,0:T(4,128)S(1)} %get-tuple-element.41, ...), kind=kLoop, calls=%fused_computation.42 | loop fusion | flops 1572864 | bytes 2970624 | tf_op jit(solution)/shard_map/convert_element_type | solution.py:186
  (30 shorter events, 0.4 us)
Async XLA Ops:
  0.6 9.2 %copy-start = (f32[64,256]{1,0:T(8,128)S(1)}, f32[64,256]{1,0:T(8,128)}, u32[]{:S(2)}) copy-start(f32[64,256]{1,0:T(8,128)} %param.27) | copy-start | bytes 196612
  0.6 19.2 %copy-start.2 = (bf16[128,256]{1,0:T(8,128)(2,1)S(1)}, bf16[128,256]{1,0:T(8,128)(2,1)}, u32[]{:S(2)}) copy-start(bf16[128,256]{1,0:T(8,128)(2,1)} %param.29) | copy-start | bytes 196612
  1.4 16.1 %collective-permute-start = (bf16[6,3,256]{2,0,1:T(8,128)(2,1)S(1)}, bf16[6,3,256]{2,0,1:T(8,128)(2,1)S(1)}, u32[]{:S(2)}, u32[]{:S(2)}) collective-permute-start(bf16[6,3,256]{2,0,1:T(8,128)(2,1)S(1)} %slice.209), channel_id=1, source_target_pairs={{0,1},{1,2},{2,3},{3,4},{4,5},{5,6},{6,7},{7,8},{8,9},{9,10},{10,1... | collective-permute-start | bytes 27656 | tf_op jit(solution)/shard_map/ppermute | solution.py:17
  41.7 0.8 copy-start.6
  41.7 0.8 copy-start.11
  42.6 0.9 %copy-start.5 = (f32[2,2,64,64,1,1]{3,2,1,0,5,4:T(8,128)S(1)}, f32[2,2,64,64,1,1]{3,2,1,0,5,4:T(8,128)}, u32[]{:S(2)}) copy-start(f32[2,2,64,64,1,1]{3,2,1,0,5,4:T(8,128)} %constant.252) | copy-start | bytes 196612
  43.5 0.8 %copy-start.4 = (f32[64,128]{1,0:T(8,128)S(1)}, f32[64,128]{1,0:T(8,128)}, u32[]{:S(2)}) copy-start(f32[64,128]{1,0:T(8,128)} %constant.208.clone) | copy-start | bytes 98308
  43.5 0.8 %copy-start.8 = (f32[64,128]{1,0:T(8,128)S(1)}, f32[64,128]{1,0:T(8,128)}, u32[]{:S(2)}) copy-start(f32[64,128]{1,0:T(8,128)} %constant.209.clone) | copy-start | bytes 98308
  44.4 1.0 %copy-start.3 = (f32[2,2,128,128,1,1]{3,2,1,0,5,4:T(8,128)S(1)}, f32[2,2,128,128,1,1]{3,2,1,0,5,4:T(8,128)}, u32[]{:S(2)}) copy-start(f32[2,2,128,128,1,1]{3,2,1,0,5,4:T(8,128)} %constant.253) | copy-start | bytes 786436
  46.6 1.0 %copy-start.1 = (f32[2,2,128,128,1,1]{3,2,1,0,5,4:T(8,128)S(1)}, f32[2,2,128,128,1,1]{3,2,1,0,5,4:T(8,128)}, u32[]{:S(2)}) copy-start(f32[2,2,128,128,1,1]{3,2,1,0,5,4:T(8,128)} %constant.254) | copy-start | bytes 786436
  46.6 1.5 %copy-start.10 = (f32[64,128]{1,0:T(8,128)S(1)}, f32[64,128]{1,0:T(8,128)}, u32[]{:S(2)}) copy-start(f32[64,128]{1,0:T(8,128)} %constant.213.clone) | copy-start | bytes 98308
  47.6 0.9 %copy-start.7 = (f32[2,2,64,64,1,1]{3,2,1,0,5,4:T(8,128)S(1)}, f32[2,2,64,64,1,1]{3,2,1,0,5,4:T(8,128)}, u32[]{:S(2)}) copy-start(f32[2,2,64,64,1,1]{3,2,1,0,5,4:T(8,128)} %constant.255) | copy-start | bytes 196612
  48.1 0.9 %copy-start.9 = (f32[64,128]{1,0:T(8,128)S(1)}, f32[64,128]{1,0:T(8,128)}, u32[]{:S(2)}) copy-start(f32[64,128]{1,0:T(8,128)} %constant.215.clone) | copy-start | bytes 98308
  71.0 5.1 %collective-permute-start.1 = (f32[6,3,256]{2,0,1:T(8,128)S(1)}, f32[6,3,256]{2,0,1:T(8,128)S(1)}, u32[]{:S(2)}, u32[]{:S(2)}) collective-permute-start(f32[6,3,256]{2,0,1:T(8,128)S(1)} %slice.303), channel_id=1, source_target_pairs={{1,0},{2,1},{3,2},{4,3},{5,4},{6,5},{7,6},{8,7},{9,8},{10,9},{11,1... | collective-permute-start | bytes 55304 | tf_op jit(solution)/shard_map/ppermute | solution.py:17

commit v6 on v5

--- a/solution.py
+++ b/solution.py
@@ -115,6 +115,11 @@
     return jnp.exp(-rates * places.astype(jnp.float32)) * jnp.sqrt(-jnp.expm1(-2.0 * rates))
 
 
+def split_wide(values):
+    rounded = lax.reduce_precision(values, exponent_bits=8, mantissa_bits=7)
+    return rounded.astype(jnp.bfloat16), (values - rounded).astype(jnp.bfloat16)
+
+
 def body(projected, short_weight, filter_in, filter_bias, filter_out, filter_decay, cotangent):
     parts = lax.axis_size("inner")
     inner_id = lax.axis_index("inner")
@@ -124,18 +129,6 @@
     bands = (filter_in.shape[0] - 1) // 2
     seq_total = parts * length
     slices = chans // parts
-    earlier = passed_along(projected[length - taps + 1 :], "inner", 1)
-    extended = jnp.concatenate([earlier, projected], axis=0)
-    mixed = jnp.zeros((length, 3, chans), jnp.float32)
-    for offset in range(taps):
-        mixed = (
-            mixed + short_weight[offset] * extended[taps - 1 - offset : taps - 1 - offset + length]
-        )
-    query = mixed[:, 0]
-    key_part = mixed[:, 1]
-    value_part = mixed[:, 2]
-    product = key_part * value_part
-    grad_conv = cotangent * query
     places = inner_id * length + jnp.arange(length, dtype=jnp.int32)
     activity = jnp.sin(
         jnp.dot(filter_features(places, seq_total, bands), filter_in, precision=exact_mode)
@@ -143,10 +136,29 @@
     )
     shaped = jnp.dot(activity, filter_out, precision=exact_mode)
     long_filter = shaped * decay_window(filter_decay[None, :], places[:, None])
-    moved = to_channels(jnp.stack([product, long_filter, grad_conv]))
-    signal_rows = moved[0]
-    filter_rows = moved[1]
-    grad_rows = moved[2]
+    filter_upper, filter_lower = split_wide(long_filter)
+    outgoing = jnp.stack(
+        [projected[:, 0], projected[:, 1], projected[:, 2], cotangent, filter_upper, filter_lower]
+    )
+    moved = to_channels(outgoing).reshape(6, slices, seq_total)
+    first = inner_id * slices
+    weights = lax.dynamic_slice_in_dim(short_weight, first, slices, axis=2)[:, :, :, None]
+    mixed = []
+    for group in range(3):
+        padded = jnp.pad(moved[group], ((0, 0), (taps - 1, 0)))
+        total = jnp.zeros((slices, seq_total), jnp.float32)
+        for offset in range(taps):
+            total = total + weights[offset, group] * padded[
+                :, taps - 1 - offset : taps - 1 - offset + seq_total
+            ]
+        mixed.append(total)
+    query, key_part, value_part = mixed
+    product = key_part * value_part
+    grad_conv = moved[3] * query
+    long_rows = moved[4].astype(jnp.float32) + moved[5].astype(jnp.float32)
+    signal_rows = product.reshape(slices, parts, length)
+    filter_rows = long_rows.reshape(slices, parts, length)
+    grad_rows = grad_conv.reshape(slices, parts, length)
     spectra = forward_padded(jnp.concatenate([signal_rows, filter_rows, grad_rows], axis=0))
     signal_spec = spectra[:, :, :slices]
     filter_spec = spectra[:, :, slices : 2 * slices]
@@ -170,20 +182,27 @@
         [returned[:slices], returned[slices + spread : 2 * slices + spread],
          returned[slices : slices + spread], returned[2 * slices + spread :]],
         axis=0,
-    )
-    back = to_positions(returned.reshape(3, slices, parts, length))
-    conv = back[0]
-    grad_product = back[1]
-    grad_filter = back[2] / math.sqrt(seq_total)
+    ).reshape(3, slices, seq_total)
+    conv = returned[0]
+    grad_product = returned[1]
+    grad_filter = returned[2] / math.sqrt(seq_total)
     operator_out = (query * conv).astype(jnp.bfloat16)
-    grad_query = cotangent * conv
-    grad_mixed = jnp.stack([grad_query, grad_product * value_part, grad_product * key_part], axis=1)
-    later = passed_along(grad_mixed[: taps - 1], "inner", -1)
-    tailed = jnp.concatenate([grad_mixed, later], axis=0)
-    grad_projected = jnp.zeros((length, 3, chans), jnp.float32)
-    for offset in range(taps):
-        grad_projected = grad_projected + short_weight[offset] * tailed[offset : offset + length]
-    return (operator_out, grad_projected.astype(jnp.bfloat16), grad_filter)
+    grad_mixed = [moved[3] * conv, grad_product * value_part, grad_product * key_part]
+    grad_projected = []
+    for group in range(3):
+        padded = jnp.pad(grad_mixed[group], ((0, 0), (0, taps - 1)))
+        total = jnp.zeros((slices, seq_total), jnp.float32)
+        for offset in range(taps):
+            total = total + weights[offset, group] * padded[:, offset : offset + seq_total]
+        grad_projected.append(total.astype(jnp.bfloat16))
+    grad_upper, grad_lower = split_wide(grad_filter)
+    back = to_positions(
+        jnp.stack([operator_out] + grad_projected + [grad_upper, grad_lower]).reshape(
+            6, slices, parts, length
+        )
+    )
+    grad_out = back[4].astype(jnp.float32) + back[5].astype(jnp.float32)
+    return (back[0], jnp.stack([back[1], back[2], back[3]], axis=1), grad_out)
 
 
 def solution(mesh):

time: 77.8 us -> 78.1 us (level)
  blocking collectives: 42.1 us -> 20.8 us
  starting transfers between devices: 6.89 us -> 18.2 us
  waiting for transfers between devices: 9.53 us -> 16.5 us
  local copies, waits for them, and re-layouts: 6.08 us -> 11.2 us
  other arithmetic: 7.47 us -> 5.59 us
    all_to_all x1 -> x0, blocking collectives: 21.5 us -> none  [to_channels(): lax.all_to_all(jnp.swapaxes(stacked, 1, 2)[:, :, None, :], 'inner', split...]
    all_to_all x0 -> x1, starting transfers between devices: none -> 18.2 us  [to_channels(): lax.all_to_all(jnp.swapaxes(stacked, 1, 2)[:, :, None, :], 'inner', split...]
    all_to_all x0 -> x1, waiting for transfers between devices: none -> 16.5 us  [to_channels(): lax.all_to_all(jnp.swapaxes(stacked, 1, 2)[:, :, None, :], 'inner', split...]
    ppermute x2 -> x0, waiting for transfers between devices: 9.53 us -> none  [passed_along(): return lax.ppermute(value, axis, pairs)]
    ppermute x2 -> x0, starting transfers between devices: 6.89 us -> none  [passed_along(): return lax.ppermute(value, axis, pairs)]
    unnamed x28 -> x42, local copies, waits for them, and re-layouts: 3.09 us -> 8.47 us
    unnamed x0 -> x7, other arithmetic: none -> 2.49 us
    add x1 -> x2, other arithmetic: 2.31 us -> 0.04 us  [the longest x1 0.02 us: body(): long_rows = moved[4].astype(jnp.float32) + moved[5].astype(jnp.float32)]
  transfers between devices with their start and end apart: 2 -> 1, of which waited for: 2 -> 1; matrix products, arithmetic and copies ran while one was open for 6% -> 1% of each run, Pallas kernels for 0% -> 0%
where the time goes in v6:
time: 78.1 us; the launch traced here: 77.5 us
  blocking collectives  20.8 us (27%)
  starting transfers between devices  18.2 us (23%)
  waiting for transfers between devices  16.5 us (21%)
  local copies, waits for them, and re-layouts  11.2 us (14%)
  other arithmetic  5.59 us (7%)
  matrix products  4.06 us (5%)
  between operations  1.17 us (1%)
    all_to_all x1, blocking collectives, to_positions(): lax.all_to_all(values, 'inner', split_axis=2, concat_axis=1, tiled=True)  20.8 us
    all_to_all x1, starting transfers between devices, to_channels(): lax.all_to_all(jnp.swapaxes(stacked, 1, 2)[:, :, None, :], 'inner', split...  18.2 us
    all_to_all x1, waiting for transfers between devices, to_channels(): lax.all_to_all(jnp.swapaxes(stacked, 1, 2)[:, :, None, :], 'inner', split...  16.5 us
    unnamed x42, local copies, waits for them, and re-layouts  8.47 us
    dot_general x4, matrix products, mix_axis(): return jnp.einsum(joined, matrix, values, precision=transform_mode)  2.67 us
    unnamed x7, other arithmetic  2.49 us
  transfers between devices with their start and end apart: 1, of which 1 were waited for; matrix products, arithmetic and copies ran while one was open for 1% of the time, Pallas kernels for 0%

profile of v6, /device:TPU:1, one launch (start us, length us, event | category | flops | bytes accessed | tf_op | source)
XLA Modules:
  0.0 77.5 jit_solution(15915147382945632049)
XLA Ops:
  0.7 0.1 fusion.69
  0.7 0.1 fusion.51
  0.8 0.1 fusion.53
  0.8 0.1 fusion.55
  0.9 0.1 fusion.57
  1.0 0.1 fusion.59
  1.0 0.1 fusion.61
  1.1 0.1 fusion.63
  1.2 0.1 fusion.65
  1.2 0.1 fusion.67
  1.3 0.1 fusion.47
  1.4 0.1 fusion.49
  1.4 0.1 convert_multiply_fusion.12
  1.5 0.7 fusion.70
  2.2 0.9 %bitcast_dynamic-update-slice_fusion.7 = bf16[6,128,256]{2,1,0:T(8,128)(2,1)S(1)} fusion(bf16[128,3,256]{2,0,1:T(8,128)(2,1)} %param.23), kind=kLoop, calls=%fused_computation.118 | loop fusion | bytes 131072
  3.0 0.8 %bitcast_dynamic-update-slice_fusion.6 = bf16[6,128,256]{2,1,0:T(8,128)(2,1)S(1)} fusion(bf16[6,128,256]{2,1,0:T(8,128)(2,1)S(1)} %bitcast_dynamic-update-slice_fusion.7, bf16[128,3,256]{2,0,1:T(8,128)(2,1)} %param.23), kind=kLoop, calls=%fused_computation.117 | loop fusion | bytes 131072
  3.9 0.8 %bitcast_dynamic-update-slice_fusion.5 = bf16[6,128,256]{2,1,0:T(8,128)(2,1)S(1)} fusion(bf16[6,128,256]{2,1,0:T(8,128)(2,1)S(1)} %bitcast_dynamic-update-slice_fusion.6, bf16[128,3,256]{2,0,1:T(8,128)(2,1)} %param.23), kind=kLoop, calls=%fused_computation.116 | loop fusion | bytes 131072
  4.7 0.8 %bitcast_dynamic-update-slice_fusion.4 = bf16[6,128,256]{2,1,0:T(8,128)(2,1)S(1)} fusion(bf16[6,128,256]{2,1,0:T(8,128)(2,1)S(1)} %bitcast_dynamic-update-slice_fusion.5, bf16[128,256]{1,0:T(8,128)(2,1)} %param.29), kind=kLoop, calls=%fused_computation.115 | loop fusion | bytes 131072
  5.6 0.1 stack.219
  5.7 1.1 %fusion.10 = f32[128,64]{0,1:T(8,128)S(1)} fusion(f32[128,33]{0,1:T(8,128)S(1)} %stack.219, f32[33,64]{1,0:T(8,128)} %param.25, f32[64]{0:T(128)} %param.26), kind=kOutput, calls=%fused_computation.16 | convolution fusion | flops 3252224 | bytes 58368 | tf_op jit(solution)/shard_map/dot_general | solution.py:134
  6.8 0.3 fusion.36
  7.1 1.1 %copy.44 = bf16[6,256,1,128]{3,0,2,1:T(8,128)(2,1)} copy(bf16[6,256,1,128]{1,3,0,2:T(8,128)(2,1)S(1)} %bitcast.248) | data formatting | bytes 786432 | tf_op jit(solution)/shard_map/broadcast_in_dim | solution.py:94
  8.2 18.2 %all-to-all-start = ((bf16[6,256,1,128]{3,0,2,1:T(8,128)(2,1)}), bf16[6,256,1,128]{3,0,2,1:T(8,128)(2,1)S(1)}, u32[]{:S(2)}, u32[]{:S(2)}) async-start(bf16[6,256,1,128]{3,0,2,1:T(8,128)(2,1)} %copy.44), calls=%async_computation | async-start | bytes 1048576 | tf_op jit(solution)/shard_map/all_to_all | solution.py:93
  26.4 0.1 constant_dynamic-slice_fusion
  26.5 0.1 copy.43
  26.6 0.2 slice_reduce_fusion.20
  26.8 0.5 slice_reduce_fusion.6
  27.3 16.5 %all-to-all-done = bf16[6,256,1,128]{3,0,2,1:T(8,128)(2,1)S(1)} async-done(((bf16[6,256,1,128]{3,0,2,1:T(8,128)(2,1)}), bf16[6,256,1,128]{3,0,2,1:T(8,128)(2,1)S(1)}, u32[]{:S(2)}, u32[]{:S(2)}) %all-to-all-start) | async-done | bytes 393248 | tf_op jit(solution)/shard_map/all_to_all | solution.py:93
  43.8 0.2 copy.107
  44.0 0.1 copy.111
  44.1 0.1 copy.110
  44.2 0.1 copy.112
  44.2 0.4 fusion.28
  44.6 0.6 multiply_bitcast_fusion
  45.3 0.1 fusion.17
  45.4 0.1 pad_bitcast_fusion
  45.5 0.1 maximum_bitcast_fusion.8
  45.5 0.7 copy-done.4
  46.3 0.8 %fusion.7 = f32[2,2,12,64,128]{4,3,0,2,1:T(8,128)S(1)} fusion(f32[2,2,64,64,1,1]{3,2,1,0,5,4:T(8,128)S(1)} %copy-done.4, f32[1,2,12,64,128]{4,3,0,2,1:T(8,128)S(1)} %pad_bitcast_fusion, f32[1,2,12,64,128]{4,3,0,2,1:T(8,128)S(1)} %maximum_bitcast_fusion.8), kind=kOutput, calls=%fused_computation.9 | convolution fusion | flops 302383104 | bytes 3211264 | tf_op jit(solution)/shard_map/zyap,yhrpj->zhraj/dot_general | solution.py:46
  47.1 0.3 multiply_subtract_fusion
  47.4 0.6 copy-done.2
  48.1 0.8 %fusion.6 = f32[2,2,12,64,128]{4,3,0,2,1:T(8,128)S(1)} fusion(f32[2,2,128,128,1,1]{3,2,1,0,5,4:T(8,128)S(1)} %copy-done.2, f32[1,2,12,64,128]{4,3,0,2,1:T(8,128)S(1)} %get-tuple-element.36, f32[1,2,12,64,128]{4,3,0,2,1:T(8,128)S(1)} %get-tuple-element.35), kind=kOutput, calls=%fused_computation.8 | convolution fusion | flops 604372992 | bytes 3407872 | tf_op jit(solution)/shard_map/zybj,yhraj->zhrab/dot_general | solution.py:46
  48.9 0.1 multiply_subtract_fusion.2
  49.0 0.2 multiply_subtract_fusion.4
  49.2 0.1 fusion.11
  49.3 0.1 pad_maximum_fusion
  49.4 0.1 slice_subtract_fusion
  49.5 0.8 %copy-done.1 = f32[2,2,128,128,1,1]{3,2,1,0,5,4:T(8,128)S(1)} copy-done((f32[2,2,128,128,1,1]{3,2,1,0,5,4:T(8,128)S(1)}, f32[2,2,128,128,1,1]{3,2,1,0,5,4:T(8,128)}, u32[]{:S(2)}) %copy-start.1) | copy-done | bytes 262168
  50.3 0.5 convolution_bitcast_fusion.1
  50.9 0.1 multiply_subtract_fusion.1
  51.0 0.2 copy-done.6
  51.2 0.5 fusion.9
  51.7 0.1 fusion.21
  51.9 0.1 bitcast_multiply_fusion
  52.0 0.5 fusion.40
  52.5 0.5 fusion.39
  53.0 0.2 bitcast_multiply_fusion.2
  53.2 0.5 fusion.38
  53.9 0.3 copy.51
  54.2 20.8 %all_to_all.30 = bf16[6,4,64,128]{3,1,0,2:T(4,128)(2,1)S(1)} all-to-all(bf16[6,4,64,128]{3,1,0,2:T(4,128)(2,1)S(1)} %copy.51), channel_id=1, replica_groups=mesh['outer'=16,'inner'=64] {'inner'}, dimensions={2} | all-to-all | bytes 786432 | tf_op jit(solution)/shard_map/all_to_all | solution.py:99
  74.9 0.1 copy.52
  75.2 0.8 %copy.54 = bf16[128,3,256]{2,0,1:T(8,128)(2,1)} copy(bf16[128,3,256]{0,2,1:T(8,128)(2,1)S(1)} %pad_maximum_fusion.2) | data formatting | bytes 393216
  76.0 0.8 copy.55
  76.7 0.7 copy.53
  (41 shorter events, 0.4 us)
Async XLA Ops:
  0.6 6.1 %copy-start = (f32[64,256]{1,0:T(8,128)S(1)}, f32[64,256]{1,0:T(8,128)}, u32[]{:S(2)}) copy-start(f32[64,256]{1,0:T(8,128)} %param.27) | copy-start | bytes 196612
  2.2 24.3 %copy-start.11 = (f32[7,3,256]{2,0,1:T(8,128)S(1)}, f32[7,3,256]{2,0,1:T(8,128)}, u32[]{:S(2)}) copy-start(f32[7,3,256]{2,0,1:T(8,128)} %param.24) | copy-start | bytes 64516
  8.2 35.6 %all-to-all-start = ((bf16[6,256,1,128]{3,0,2,1:T(8,128)(2,1)}), bf16[6,256,1,128]{3,0,2,1:T(8,128)(2,1)S(1)}, u32[]{:S(2)}, u32[]{:S(2)}) async-start(bf16[6,256,1,128]{3,0,2,1:T(8,128)(2,1)} %copy.44), calls=%async_computation | async-start | bytes 1048576 | tf_op jit(solution)/shard_map/all_to_all | solution.py:93
  43.9 1.3 %copy-start.5 = (f32[64,128]{1,0:T(8,128)S(1)}, f32[64,128]{1,0:T(8,128)}, u32[]{:S(2)}) copy-start(f32[64,128]{1,0:T(8,128)} %constant.208.clone) | copy-start | bytes 98308
  44.0 1.3 %copy-start.10 = (f32[64,128]{1,0:T(8,128)S(1)}, f32[64,128]{1,0:T(8,128)}, u32[]{:S(2)}) copy-start(f32[64,128]{1,0:T(8,128)} %constant.209.clone) | copy-start | bytes 98308
  45.4 0.9 %copy-start.4 = (f32[2,2,64,64,1,1]{3,2,1,0,5,4:T(8,128)S(1)}, f32[2,2,64,64,1,1]{3,2,1,0,5,4:T(8,128)}, u32[]{:S(2)}) copy-start(f32[2,2,64,64,1,1]{3,2,1,0,5,4:T(8,128)} %constant.268) | copy-start | bytes 196612
  46.3 0.8 %copy-start.3 = (f32[64,128]{1,0:T(8,128)S(1)}, f32[64,128]{1,0:T(8,128)}, u32[]{:S(2)}) copy-start(f32[64,128]{1,0:T(8,128)} %constant.212.clone) | copy-start | bytes 98308
  46.3 0.8 %copy-start.7 = (f32[64,128]{1,0:T(8,128)S(1)}, f32[64,128]{1,0:T(8,128)}, u32[]{:S(2)}) copy-start(f32[64,128]{1,0:T(8,128)} %constant.213.clone) | copy-start | bytes 98308
  47.1 1.0 %copy-start.2 = (f32[2,2,128,128,1,1]{3,2,1,0,5,4:T(8,128)S(1)}, f32[2,2,128,128,1,1]{3,2,1,0,5,4:T(8,128)}, u32[]{:S(2)}) copy-start(f32[2,2,128,128,1,1]{3,2,1,0,5,4:T(8,128)} %constant.269) | copy-start | bytes 786436
  49.4 1.0 %copy-start.1 = (f32[2,2,128,128,1,1]{3,2,1,0,5,4:T(8,128)S(1)}, f32[2,2,128,128,1,1]{3,2,1,0,5,4:T(8,128)}, u32[]{:S(2)}) copy-start(f32[2,2,128,128,1,1]{3,2,1,0,5,4:T(8,128)} %constant.270) | copy-start | bytes 786436
  49.4 1.5 %copy-start.9 = (f32[64,128]{1,0:T(8,128)S(1)}, f32[64,128]{1,0:T(8,128)}, u32[]{:S(2)}) copy-start(f32[64,128]{1,0:T(8,128)} %constant.217.clone) | copy-start | bytes 98308
  50.3 0.9 %copy-start.6 = (f32[2,2,64,64,1,1]{3,2,1,0,5,4:T(8,128)S(1)}, f32[2,2,64,64,1,1]{3,2,1,0,5,4:T(8,128)}, u32[]{:S(2)}) copy-start(f32[2,2,64,64,1,1]{3,2,1,0,5,4:T(8,128)} %constant.271) | copy-start | bytes 196612
  50.8 0.9 %copy-start.8 = (f32[64,128]{1,0:T(8,128)S(1)}, f32[64,128]{1,0:T(8,128)}, u32[]{:S(2)}) copy-start(f32[64,128]{1,0:T(8,128)} %constant.219.clone) | copy-start | bytes 98308

commit v7 on v6

--- a/solution.py
+++ b/solution.py
@@ -137,10 +137,13 @@
     shaped = jnp.dot(activity, filter_out, precision=exact_mode)
     long_filter = shaped * decay_window(filter_decay[None, :], places[:, None])
     filter_upper, filter_lower = split_wide(long_filter)
-    outgoing = jnp.stack(
-        [projected[:, 0], projected[:, 1], projected[:, 2], cotangent, filter_upper, filter_lower]
-    )
-    moved = to_channels(outgoing).reshape(6, slices, seq_total)
+    outgoing = jnp.concatenate(
+        [projected, cotangent[:, None], filter_upper[:, None], filter_lower[:, None]], axis=1
+    )
+    arrived = lax.all_to_all(
+        outgoing.reshape(length, 6, parts, slices), "inner", split_axis=2, concat_axis=0, tiled=True
+    )
+    moved = jnp.transpose(arrived.reshape(seq_total, 6, slices), (1, 2, 0))
     first = inner_id * slices
     weights = lax.dynamic_slice_in_dim(short_weight, first, slices, axis=2)[:, :, :, None]
     mixed = []
@@ -196,13 +199,14 @@
             total = total + weights[offset, group] * padded[:, offset : offset + seq_total]
         grad_projected.append(total.astype(jnp.bfloat16))
     grad_upper, grad_lower = split_wide(grad_filter)
-    back = to_positions(
-        jnp.stack([operator_out] + grad_projected + [grad_upper, grad_lower]).reshape(
-            6, slices, parts, length
-        )
-    )
-    grad_out = back[4].astype(jnp.float32) + back[5].astype(jnp.float32)
-    return (back[0], jnp.stack([back[1], back[2], back[3]], axis=1), grad_out)
+    leaving = jnp.transpose(
+        jnp.stack([operator_out] + grad_projected + [grad_upper, grad_lower]), (2, 0, 1)
+    )
+    back = lax.all_to_all(
+        leaving.reshape(parts, length, 6, 1, slices), "inner", split_axis=0, concat_axis=3, tiled=True
+    ).reshape(length, 6, chans)
+    grad_out = back[:, 4].astype(jnp.float32) + back[:, 5].astype(jnp.float32)
+    return (back[:, 0], back[:, 1:4], grad_out)
 
 
 def solution(mesh):

time: 78.1 us -> 74.6 us (0.955)
  waiting for transfers between devices: 16.5 us -> 13.8 us
  local copies, waits for them, and re-layouts: 11.2 us -> 10.2 us
    all_to_all x1, waiting for transfers between devices: 16.5 us -> 13.8 us  [body(): lax.all_to_all(outgoing.reshape(length, 6, parts, slices), 'inner', split...]
    unnamed x42 -> x31, local copies, waits for them, and re-layouts: 8.47 us -> 6.86 us
    broadcast_in_dim x1 -> x0, local copies, waits for them, and re-layouts: 1.08 us -> none  [to_channels(): jnp.swapaxes(stacked, 1, 2)[:, :, None, :]]
    reshape x0 -> x5, local copies, waits for them, and re-layouts: none -> 0.86 us  [the longest x2 0.72 us: body(): leaving.reshape(parts, length, 6, 1, slices)]
    concatenate x2 -> x1, local copies, waits for them, and re-layouts: 0.01 us -> 0.87 us  [body(): jnp.concatenate([projected, cotangent[:, None], filter_upper[:, None], fi...]
    unnamed x7 -> x8, other arithmetic: 2.49 us -> 2.68 us
where the time goes in v7:
time: 74.6 us; the launch traced here: 74.2 us
  blocking collectives  20.6 us (28%)
  starting transfers between devices  18.2 us (24%)
  waiting for transfers between devices  13.8 us (18%)
  local copies, waits for them, and re-layouts  10.2 us (14%)
  other arithmetic  6.02 us (8%)
  matrix products  4.08 us (5%)
  between operations  1.2 us (2%)
    all_to_all x1, blocking collectives, body(): lax.all_to_all(leaving.reshape(parts, length, 6, 1, slices), 'inner', spl...  20.6 us
    all_to_all x1, starting transfers between devices, body(): lax.all_to_all(outgoing.reshape(length, 6, parts, slices), 'inner', split...  18.2 us
    all_to_all x1, waiting for transfers between devices, body(): lax.all_to_all(outgoing.reshape(length, 6, parts, slices), 'inner', split...  13.8 us
    unnamed x31, local copies, waits for them, and re-layouts  6.86 us
    unnamed x8, other arithmetic  2.68 us
    dot_general x4, matrix products, mix_axis(): return jnp.einsum(joined, matrix, values, precision=transform_mode)  2.67 us
  transfers between devices with their start and end apart: 1, of which 1 were waited for; matrix products, arithmetic and copies ran while one was open for 1% of the time, Pallas kernels for 0%

profile of v7, /device:TPU:1, one launch (start us, length us, event | category | flops | bytes accessed | tf_op | source)
XLA Modules:
  0.0 74.2 jit_solution(12327660471752090802)
XLA Ops:
  0.7 0.1 fusion.41
  0.8 0.1 fusion.43
  0.8 0.1 fusion.45
  0.9 0.1 fusion.47
  1.0 0.1 fusion.49
  1.0 0.1 fusion.51
  1.1 0.1 fusion.53
  1.2 0.1 fusion.55
  1.2 0.1 fusion.57
  1.3 0.1 fusion.37
  1.4 0.1 fusion.39
  1.5 0.7 fusion.60
  2.2 1.0 %copy.61 = bf16[128,256]{0,1:T(8,128)(2,1)S(1)} copy(bf16[128,256]{1,0:T(8,128)(2,1)} %param.29) | data formatting | bytes 131072 | tf_op args[6]
  3.1 0.1 stack.100
  3.2 1.1 %fusion.10 = f32[128,64]{0,1:T(8,128)S(1)} fusion(f32[128,33]{0,1:T(8,128)S(1)} %stack.100, f32[33,64]{1,0:T(8,128)} %param.25, f32[64]{0:T(128)} %param.26), kind=kOutput, calls=%fused_computation.16 | convolution fusion | flops 3252224 | bytes 58368 | tf_op jit(solution)/shard_map/dot_general | solution.py:134
  4.4 0.3 reduce-precision_convert_fusion
  4.7 0.1 copy.62
  4.8 0.1 copy.63
  4.9 1.1 %copy.60 = bf16[128,3,256]{0,2,1:T(8,128)(2,1)S(1)} copy(bf16[128,3,256]{2,0,1:T(8,128)(2,1)} %param.23) | data formatting | bytes 393216 | tf_op args[0]
  6.0 0.3 pad_maximum_fusion.1
  6.4 0.9 %copy.64 = bf16[128,6,64,4]{0,3,1,2:T(4,128)(2,1)} copy(bf16[128,6,64,4]{0,3,2,1:T(4,128)(2,1)S(1)} %pad_maximum_fusion.1) | data formatting | bytes 786432 | tf_op jit(solution)/shard_map/concatenate | solution.py:140
  7.3 18.2 %all-to-all-start = ((bf16[128,6,64,4]{0,3,1,2:T(4,128)(2,1)}), bf16[128,6,64,4]{0,3,1,2:T(4,128)(2,1)S(1)}, u32[]{:S(2)}, u32[]{:S(2)}) async-start(bf16[128,6,64,4]{0,3,1,2:T(4,128)(2,1)} %copy.64), calls=%async_computation | async-start | bytes 786432 | tf_op jit(solution)/shard_map/all_to_all | solution.py:143
  25.5 0.1 constant_dynamic-slice_fusion
  25.6 0.1 copy.59
  25.7 0.2 slice_reduce_fusion.20
  25.9 0.5 slice_reduce_fusion.6
  26.4 13.8 %all-to-all-done = bf16[128,6,64,4]{0,3,1,2:T(4,128)(2,1)S(1)} async-done(((bf16[128,6,64,4]{0,3,1,2:T(4,128)(2,1)}), bf16[128,6,64,4]{0,3,1,2:T(4,128)(2,1)S(1)}, u32[]{:S(2)}, u32[]{:S(2)}) %all-to-all-start) | async-done | bytes 393248 | tf_op jit(solution)/shard_map/all_to_all | solution.py:143
  40.2 0.1 copy.65
  40.3 0.1 reshape.756
  40.5 0.1 slice_bitcast_fusion.9
  40.5 0.6 multiply_bitcast_fusion
  41.2 0.3 fusion.23
  41.6 0.1 broadcast_multiply_fusion.1
  41.7 0.1 pad_bitcast_fusion
  41.8 0.1 maximum_bitcast_fusion.8
  41.9 0.7 copy-done.4
  42.6 0.8 %fusion.7 = f32[2,2,12,64,128]{4,3,0,2,1:T(8,128)S(1)} fusion(f32[2,2,64,64,1,1]{3,2,1,0,5,4:T(8,128)S(1)} %copy-done.4, f32[1,2,12,64,128]{4,3,0,2,1:T(8,128)S(1)} %pad_bitcast_fusion, f32[1,2,12,64,128]{4,3,0,2,1:T(8,128)S(1)} %maximum_bitcast_fusion.8), kind=kOutput, calls=%fused_computation.9 | convolution fusion | flops 302383104 | bytes 3211264 | tf_op jit(solution)/shard_map/zyap,yhrpj->zhraj/dot_general | solution.py:46
  43.5 0.3 multiply_subtract_fusion
  43.8 0.6 copy-done.2
  44.4 0.8 %fusion.6 = f32[2,2,12,64,128]{4,3,0,2,1:T(8,128)S(1)} fusion(f32[2,2,128,128,1,1]{3,2,1,0,5,4:T(8,128)S(1)} %copy-done.2, f32[1,2,12,64,128]{4,3,0,2,1:T(8,128)S(1)} %get-tuple-element.39, f32[1,2,12,64,128]{4,3,0,2,1:T(8,128)S(1)} %get-tuple-element.38), kind=kOutput, calls=%fused_computation.8 | convolution fusion | flops 604372992 | bytes 3407872 | tf_op jit(solution)/shard_map/zybj,yhraj->zhrab/dot_general | solution.py:46
  45.3 0.1 multiply_subtract_fusion.2
  45.4 0.2 multiply_subtract_fusion.4
  45.6 0.1 fusion.11
  45.6 0.1 pad_maximum_fusion
  45.7 0.1 slice_subtract_fusion
  45.9 0.8 %copy-done.1 = f32[2,2,128,128,1,1]{3,2,1,0,5,4:T(8,128)S(1)} copy-done((f32[2,2,128,128,1,1]{3,2,1,0,5,4:T(8,128)S(1)}, f32[2,2,128,128,1,1]{3,2,1,0,5,4:T(8,128)}, u32[]{:S(2)}) %copy-start.1) | copy-done | bytes 262168
  46.7 0.5 convolution_bitcast_fusion.1
  47.2 0.1 multiply_subtract_fusion.1
  47.3 0.2 copy-done.6
  47.6 0.5 fusion.9
  48.1 0.1 fusion.19
  48.3 0.1 convert_multiply_fusion
  48.5 0.1 fusion.28
  48.6 0.5 bitcast_dynamic-update-slice_fusion.5
  49.1 0.1 bitcast_multiply_fusion
  49.2 0.5 bitcast_dynamic-update-slice_fusion.4
  49.7 0.5 bitcast_dynamic-update-slice_fusion.3
  50.3 0.4 reshape.759
  50.7 0.3 copy.70
  51.1 20.6 %all_to_all.30 = bf16[64,128,6,1,4]{1,4,2,3,0:T(4,128)(2,1)S(1)} all-to-all(bf16[64,128,6,1,4]{1,4,2,3,0:T(4,128)(2,1)S(1)} %copy.70), channel_id=1, replica_groups=mesh['outer'=16,'inner'=64] {'inner'}, dimensions={0} | all-to-all | bytes 786432 | tf_op jit(solution)/shard_map/all_to_all | solution.py:205
  71.7 0.1 copy.71
  71.9 0.7 %copy.72 = bf16[128,256]{1,0:T(8,128)(2,1)} copy(bf16[128,256]{0,1:T(8,128)(2,1)S(1)} %slice_bitcast_fusion.6) | data formatting | bytes 131072
  72.6 0.8 %copy.73 = bf16[128,3,256]{2,0,1:T(8,128)(2,1)} copy(bf16[128,3,256]{0,2,1:T(8,128)(2,1)S(1)} %slice.486) | data formatting | bytes 393216
  73.4 0.8 %copy.74 = f32[128,256]{1,0:T(8,128)} copy(f32[128,256]{0,1:T(8,128)S(1)} %add_bitcast_fusion) | data formatting | bytes 262144
  (40 shorter events, 0.5 us)
Async XLA Ops:
  0.6 3.7 %copy-start = (f32[64,256]{1,0:T(8,128)S(1)}, f32[64,256]{1,0:T(8,128)}, u32[]{:S(2)}) copy-start(f32[64,256]{1,0:T(8,128)} %param.27) | copy-start | bytes 196612
  4.7 20.8 %copy-start.11 = (f32[7,3,256]{2,0,1:T(8,128)S(1)}, f32[7,3,256]{2,0,1:T(8,128)}, u32[]{:S(2)}) copy-start(f32[7,3,256]{2,0,1:T(8,128)} %param.24) | copy-start | bytes 64516
  7.3 32.9 %all-to-all-start = ((bf16[128,6,64,4]{0,3,1,2:T(4,128)(2,1)}), bf16[128,6,64,4]{0,3,1,2:T(4,128)(2,1)S(1)}, u32[]{:S(2)}, u32[]{:S(2)}) async-start(bf16[128,6,64,4]{0,3,1,2:T(4,128)(2,1)} %copy.64), calls=%async_computation | async-start | bytes 786432 | tf_op jit(solution)/shard_map/all_to_all | solution.py:143
  40.4 1.2 %copy-start.5 = (f32[64,128]{1,0:T(8,128)S(1)}, f32[64,128]{1,0:T(8,128)}, u32[]{:S(2)}) copy-start(f32[64,128]{1,0:T(8,128)} %constant.208.clone) | copy-start | bytes 98308
  40.4 1.2 %copy-start.10 = (f32[64,128]{1,0:T(8,128)S(1)}, f32[64,128]{1,0:T(8,128)}, u32[]{:S(2)}) copy-start(f32[64,128]{1,0:T(8,128)} %constant.209.clone) | copy-start | bytes 98308
  41.7 0.9 %copy-start.4 = (f32[2,2,64,64,1,1]{3,2,1,0,5,4:T(8,128)S(1)}, f32[2,2,64,64,1,1]{3,2,1,0,5,4:T(8,128)}, u32[]{:S(2)}) copy-start(f32[2,2,64,64,1,1]{3,2,1,0,5,4:T(8,128)} %constant.268) | copy-start | bytes 196612
  42.6 0.8 %copy-start.3 = (f32[64,128]{1,0:T(8,128)S(1)}, f32[64,128]{1,0:T(8,128)}, u32[]{:S(2)}) copy-start(f32[64,128]{1,0:T(8,128)} %constant.212.clone) | copy-start | bytes 98308
  42.6 0.8 %copy-start.7 = (f32[64,128]{1,0:T(8,128)S(1)}, f32[64,128]{1,0:T(8,128)}, u32[]{:S(2)}) copy-start(f32[64,128]{1,0:T(8,128)} %constant.213.clone) | copy-start | bytes 98308
  43.5 1.0 %copy-start.2 = (f32[2,2,128,128,1,1]{3,2,1,0,5,4:T(8,128)S(1)}, f32[2,2,128,128,1,1]{3,2,1,0,5,4:T(8,128)}, u32[]{:S(2)}) copy-start(f32[2,2,128,128,1,1]{3,2,1,0,5,4:T(8,128)} %constant.269) | copy-start | bytes 786436
  45.7 1.0 %copy-start.1 = (f32[2,2,128,128,1,1]{3,2,1,0,5,4:T(8,128)S(1)}, f32[2,2,128,128,1,1]{3,2,1,0,5,4:T(8,128)}, u32[]{:S(2)}) copy-start(f32[2,2,128,128,1,1]{3,2,1,0,5,4:T(8,128)} %constant.270) | copy-start | bytes 786436
  45.7 1.5 %copy-start.9 = (f32[64,128]{1,0:T(8,128)S(1)}, f32[64,128]{1,0:T(8,128)}, u32[]{:S(2)}) copy-start(f32[64,128]{1,0:T(8,128)} %constant.217.clone) | copy-start | bytes 98308
  46.7 0.9 %copy-start.6 = (f32[2,2,64,64,1,1]{3,2,1,0,5,4:T(8,128)S(1)}, f32[2,2,64,64,1,1]{3,2,1,0,5,4:T(8,128)}, u32[]{:S(2)}) copy-start(f32[2,2,64,64,1,1]{3,2,1,0,5,4:T(8,128)} %constant.271) | copy-start | bytes 196612
  47.2 0.9 %copy-start.8 = (f32[64,128]{1,0:T(8,128)S(1)}, f32[64,128]{1,0:T(8,128)}, u32[]{:S(2)}) copy-start(f32[64,128]{1,0:T(8,128)} %constant.219.clone) | copy-start | bytes 98308

commit v8 on v7

--- a/solution.py
+++ b/solution.py
@@ -38,11 +38,13 @@
 
 def mix_axis(values, count, direction, pattern):
     index = np.arange(count, dtype=np.int64)
-    cosine, sine = turning(index[:, None] * index[None, :], count, direction)
-    matrix = jnp.stack([jnp.stack([cosine, -sine]), jnp.stack([sine, cosine])])
+    angles = -full_turn / count * ((index[:, None] * index[None, :]) % count).astype(np.float64)
+    cosine, sine = np.cos(angles), np.sin(angles)
+    matrix = jnp.asarray(np.stack([np.stack([cosine, -sine]), np.stack([sine, cosine])]), jnp.float32)
     pair, result = pattern.split("->")
     table, operand = pair.split(",")
-    joined = "zy" + table + ",y" + operand + "->z" + result
+    order = "zy" if direction < 0 else "yz"
+    joined = order + table + ",y" + operand + "->z" + result
     return jnp.einsum(joined, matrix, values, precision=transform_mode)
 
 
@@ -80,12 +82,14 @@
     values = mix_axis(joined, length, 1.0, "jb,hrab->hraj")
     index_a = np.arange(parts, dtype=np.int64)[:, None]
     index_j = np.arange(length, dtype=np.int64)[None, :]
-    cosine, sine = turning(index_a * index_j, seq_total, 1.0)
-    values = rotate(values, cosine, sine)
+    cosine, sine = turning(index_a * index_j, seq_total, -1.0)
+    values = jnp.stack(
+        [values[0] * cosine + values[1] * sine, values[1] * cosine - values[0] * sine]
+    )
     values = mix_axis(values, parts, 1.0, "pa,hraj->hrpj") / seq_total
-    cosine, sine = turning(grid_places(parts, length), 2 * seq_total, 1.0)
-    real_part = 0.5 * (values[0, 0] + values[0, 1] * cosine - values[1, 1] * sine)
-    other_part = 0.5 * (values[1, 0] + values[0, 1] * sine + values[1, 1] * cosine)
+    cosine, sine = turning(grid_places(parts, length), 2 * seq_total, -1.0)
+    real_part = 0.5 * (values[0, 0] + values[0, 1] * cosine + values[1, 1] * sine)
+    other_part = 0.5 * (values[1, 0] - values[0, 1] * sine + values[1, 1] * cosine)
     return jnp.concatenate([real_part, other_part], axis=0)
 
 

time: 74.6 us -> 74.6 us (level)
    unnamed x31 -> x27, local copies, waits for them, and re-layouts: 6.86 us -> 6.88 us
where the time goes in v8:
time: 74.6 us; the launch traced here: 74.2 us
  blocking collectives  20.6 us (28%)
  starting transfers between devices  18.2 us (24%)
  waiting for transfers between devices  13.8 us (18%)
  local copies, waits for them, and re-layouts  10.3 us (14%)
  other arithmetic  6.02 us (8%)
  matrix products  4.08 us (5%)
  between operations  1.16 us (2%)
    all_to_all x1, blocking collectives, body(): lax.all_to_all(leaving.reshape(parts, length, 6, 1, slices), 'inner', spl...  20.6 us
    all_to_all x1, starting transfers between devices, body(): lax.all_to_all(outgoing.reshape(length, 6, parts, slices), 'inner', split...  18.2 us
    all_to_all x1, waiting for transfers between devices, body(): lax.all_to_all(outgoing.reshape(length, 6, parts, slices), 'inner', split...  13.8 us
    unnamed x27, local copies, waits for them, and re-layouts  6.88 us
    unnamed x8, other arithmetic  2.68 us
    dot_general x4, matrix products, mix_axis(): return jnp.einsum(joined, matrix, values, precision=transform_mode)  2.67 us
  transfers between devices with their start and end apart: 1, of which 1 were waited for; matrix products, arithmetic and copies ran while one was open for 1% of the time, Pallas kernels for 0%

profile of v8, /device:TPU:1, one launch (start us, length us, event | category | flops | bytes accessed | tf_op | source)
XLA Modules:
  0.0 74.2 jit_solution(3004149364714616867)
XLA Ops:
  0.7 0.1 fusion.41
  0.8 0.1 fusion.43
  0.8 0.1 fusion.45
  0.9 0.1 fusion.47
  1.0 0.1 fusion.49
  1.0 0.1 fusion.51
  1.1 0.1 fusion.53
  1.2 0.1 fusion.55
  1.2 0.1 fusion.57
  1.3 0.1 fusion.37
  1.4 0.1 fusion.39
  1.5 0.7 fusion.60
  2.2 1.0 %copy.63 = bf16[128,256]{0,1:T(8,128)(2,1)S(1)} copy(bf16[128,256]{1,0:T(8,128)(2,1)} %param.25) | data formatting | bytes 131072 | tf_op args[6]
  3.1 0.1 stack.36
  3.2 1.1 %fusion.10 = f32[128,64]{0,1:T(8,128)S(1)} fusion(f32[128,33]{0,1:T(8,128)S(1)} %stack.36, f32[33,64]{1,0:T(8,128)} %param.21, f32[64]{0:T(128)} %param.22), kind=kOutput, calls=%fused_computation.16 | convolution fusion | flops 3252224 | bytes 58368 | tf_op jit(solution)/shard_map/dot_general | solution.py:138
  4.4 0.3 reduce-precision_convert_fusion
  4.7 0.1 copy.64
  4.8 0.1 copy.65
  4.9 1.1 %copy.62 = bf16[128,3,256]{0,2,1:T(8,128)(2,1)S(1)} copy(bf16[128,3,256]{2,0,1:T(8,128)(2,1)} %param.19) | data formatting | bytes 393216 | tf_op args[0]
  6.0 0.3 pad_maximum_fusion.1
  6.4 0.9 %copy.66 = bf16[128,6,64,4]{0,3,1,2:T(4,128)(2,1)} copy(bf16[128,6,64,4]{0,3,2,1:T(4,128)(2,1)S(1)} %pad_maximum_fusion.1) | data formatting | bytes 786432 | tf_op jit(solution)/shard_map/concatenate | solution.py:144
  7.3 18.2 %all-to-all-start = ((bf16[128,6,64,4]{0,3,1,2:T(4,128)(2,1)}), bf16[128,6,64,4]{0,3,1,2:T(4,128)(2,1)S(1)}, u32[]{:S(2)}, u32[]{:S(2)}) async-start(bf16[128,6,64,4]{0,3,1,2:T(4,128)(2,1)} %copy.66), calls=%async_computation | async-start | bytes 786432 | tf_op jit(solution)/shard_map/all_to_all | solution.py:147
  25.5 0.1 constant_dynamic-slice_fusion
  25.6 0.1 copy.61
  25.7 0.2 slice_reduce_fusion.20
  25.9 0.5 slice_reduce_fusion.6
  26.4 13.8 %all-to-all-done = bf16[128,6,64,4]{0,3,1,2:T(4,128)(2,1)S(1)} async-done(((bf16[128,6,64,4]{0,3,1,2:T(4,128)(2,1)}), bf16[128,6,64,4]{0,3,1,2:T(4,128)(2,1)S(1)}, u32[]{:S(2)}, u32[]{:S(2)}) %all-to-all-start) | async-done | bytes 393248 | tf_op jit(solution)/shard_map/all_to_all | solution.py:147
  40.2 0.1 copy.67
  40.3 0.1 reshape.756
  40.5 0.1 slice_bitcast_fusion.9
  40.5 0.6 multiply_bitcast_fusion
  41.2 0.3 fusion.23
  41.6 0.1 broadcast_multiply_fusion.1
  41.7 0.1 pad_bitcast_fusion
  41.8 0.1 maximum_bitcast_fusion.8
  41.9 0.7 copy-done.5
  42.6 0.8 %fusion.7 = f32[2,2,12,64,128]{4,3,0,2,1:T(8,128)S(1)} fusion(f32[2,2,64,64,1,1]{3,2,1,0,5,4:T(8,128)S(1)} %copy-done.5, f32[1,2,12,64,128]{4,3,0,2,1:T(8,128)S(1)} %pad_bitcast_fusion, f32[1,2,12,64,128]{4,3,0,2,1:T(8,128)S(1)} %maximum_bitcast_fusion.8), kind=kOutput, calls=%fused_computation.9 | convolution fusion | flops 302383104 | bytes 3211264 | tf_op jit(solution)/shard_map/zyap,yhrpj->zhraj/dot_general | solution.py:48
  43.5 0.3 multiply_subtract_fusion
  43.8 0.6 copy-done.2
  44.4 0.8 %fusion.6 = f32[2,2,12,64,128]{4,3,0,2,1:T(8,128)S(1)} fusion(f32[2,2,128,128,1,1]{3,2,1,0,5,4:T(8,128)S(1)} %copy-done.2, f32[1,2,12,64,128]{4,3,0,2,1:T(8,128)S(1)} %get-tuple-element.39, f32[1,2,12,64,128]{4,3,0,2,1:T(8,128)S(1)} %get-tuple-element.38), kind=kOutput, calls=%fused_computation.8 | convolution fusion | flops 604372992 | bytes 3407872 | tf_op jit(solution)/shard_map/zybj,yhraj->zhrab/dot_general | solution.py:48
  45.3 0.1 multiply_subtract_fusion.2
  45.4 0.2 multiply_subtract_fusion.4
  45.6 0.1 fusion.11
  45.6 0.1 pad_maximum_fusion
  45.7 0.1 slice_subtract_fusion
  45.8 0.8 %copy-done.1 = f32[2,2,128,128,1,1]{3,2,0,1,5,4:T(8,128)S(1)} copy-done((f32[2,2,128,128,1,1]{3,2,0,1,5,4:T(8,128)S(1)}, f32[2,2,128,128,1,1]{3,2,0,1,5,4:T(8,128)}, u32[]{:S(2)}) %copy-start.1) | copy-done | bytes 262168
  46.7 0.5 convolution_bitcast_fusion.1
  47.2 0.1 multiply_add_fusion.1
  47.3 0.3 copy-done.8
  47.6 0.5 fusion.9
  48.1 0.1 fusion.19
  48.2 0.1 convert_multiply_fusion
  48.4 0.1 fusion.28
  48.6 0.5 bitcast_dynamic-update-slice_fusion.5
  49.1 0.1 bitcast_multiply_fusion
  49.2 0.5 bitcast_dynamic-update-slice_fusion.4
  49.7 0.5 bitcast_dynamic-update-slice_fusion.3
  50.3 0.4 reshape.759
  50.7 0.3 copy.74
  51.0 20.6 %all_to_all.30 = bf16[64,128,6,1,4]{1,4,2,3,0:T(4,128)(2,1)S(1)} all-to-all(bf16[64,128,6,1,4]{1,4,2,3,0:T(4,128)(2,1)S(1)} %copy.74), channel_id=1, replica_groups=mesh['outer'=16,'inner'=64] {'inner'}, dimensions={0} | all-to-all | bytes 786432 | tf_op jit(solution)/shard_map/all_to_all | solution.py:209
  71.7 0.1 copy.75
  71.9 0.7 %copy.76 = bf16[128,256]{1,0:T(8,128)(2,1)} copy(bf16[128,256]{0,1:T(8,128)(2,1)S(1)} %slice_bitcast_fusion.6) | data formatting | bytes 131072
  72.6 0.8 %copy.77 = bf16[128,3,256]{2,0,1:T(8,128)(2,1)} copy(bf16[128,3,256]{0,2,1:T(8,128)(2,1)S(1)} %slice.486) | data formatting | bytes 393216
  73.4 0.8 %copy.78 = f32[128,256]{1,0:T(8,128)} copy(f32[128,256]{0,1:T(8,128)S(1)} %add_bitcast_fusion) | data formatting | bytes 262144
  (36 shorter events, 0.5 us)
Async XLA Ops:
  0.6 3.7 %copy-start = (f32[64,256]{1,0:T(8,128)S(1)}, f32[64,256]{1,0:T(8,128)}, u32[]{:S(2)}) copy-start(f32[64,256]{1,0:T(8,128)} %param.23) | copy-start | bytes 196612
  4.7 20.8 %copy-start.9 = (f32[7,3,256]{2,0,1:T(8,128)S(1)}, f32[7,3,256]{2,0,1:T(8,128)}, u32[]{:S(2)}) copy-start(f32[7,3,256]{2,0,1:T(8,128)} %param.20) | copy-start | bytes 64516
  7.3 32.9 %all-to-all-start = ((bf16[128,6,64,4]{0,3,1,2:T(4,128)(2,1)}), bf16[128,6,64,4]{0,3,1,2:T(4,128)(2,1)S(1)}, u32[]{:S(2)}, u32[]{:S(2)}) async-start(bf16[128,6,64,4]{0,3,1,2:T(4,128)(2,1)} %copy.66), calls=%async_computation | async-start | bytes 786432 | tf_op jit(solution)/shard_map/all_to_all | solution.py:147
  40.4 1.2 %copy-start.6 = (f32[64,128]{1,0:T(8,128)S(1)}, f32[64,128]{1,0:T(8,128)}, u32[]{:S(2)}) copy-start(f32[64,128]{1,0:T(8,128)} %constant.197.clone) | copy-start | bytes 98308
  40.4 1.2 %copy-start.7 = (f32[64,128]{1,0:T(8,128)S(1)}, f32[64,128]{1,0:T(8,128)}, u32[]{:S(2)}) copy-start(f32[64,128]{1,0:T(8,128)} %constant.196.clone) | copy-start | bytes 98308
  41.7 0.9 %copy-start.5 = (f32[2,2,64,64,1,1]{3,2,1,0,5,4:T(8,128)S(1)}, f32[2,2,64,64,1,1]{3,2,1,0,5,4:T(8,128)}, u32[]{:S(2)}) copy-start(f32[2,2,64,64,1,1]{3,2,1,0,5,4:T(8,128)} %constant.216) | copy-start | bytes 196612
  42.6 0.8 %copy-start.3 = (f32[64,128]{1,0:T(8,128)S(1)}, f32[64,128]{1,0:T(8,128)}, u32[]{:S(2)}) copy-start(f32[64,128]{1,0:T(8,128)} %constant.200.clone) | copy-start | bytes 98308
  42.6 0.8 %copy-start.4 = (f32[64,128]{1,0:T(8,128)S(1)}, f32[64,128]{1,0:T(8,128)}, u32[]{:S(2)}) copy-start(f32[64,128]{1,0:T(8,128)} %constant.199.clone) | copy-start | bytes 98308
  43.5 1.0 %copy-start.2 = (f32[2,2,128,128,1,1]{3,2,1,0,5,4:T(8,128)S(1)}, f32[2,2,128,128,1,1]{3,2,1,0,5,4:T(8,128)}, u32[]{:S(2)}) copy-start(f32[2,2,128,128,1,1]{3,2,1,0,5,4:T(8,128)} %constant.217) | copy-start | bytes 786436
  45.7 1.0 %copy-start.1 = (f32[2,2,128,128,1,1]{3,2,0,1,5,4:T(8,128)S(1)}, f32[2,2,128,128,1,1]{3,2,0,1,5,4:T(8,128)}, u32[]{:S(2)}) copy-start(f32[2,2,128,128,1,1]{3,2,0,1,5,4:T(8,128)} %constant.218) | copy-start | bytes 786436
  46.7 0.9 %copy-start.8 = (f32[2,2,64,64,1,1]{3,2,0,1,5,4:T(8,128)S(1)}, f32[2,2,64,64,1,1]{3,2,0,1,5,4:T(8,128)}, u32[]{:S(2)}) copy-start(f32[2,2,64,64,1,1]{3,2,0,1,5,4:T(8,128)} %constant.219) | copy-start | bytes 196612

commit v9 on v8

--- a/solution.py
+++ b/solution.py
@@ -144,6 +144,7 @@
     outgoing = jnp.concatenate(
         [projected, cotangent[:, None], filter_upper[:, None], filter_lower[:, None]], axis=1
     )
+    outgoing = lax.optimization_barrier(outgoing)
     arrived = lax.all_to_all(
         outgoing.reshape(length, 6, parts, slices), "inner", split_axis=2, concat_axis=0, tiled=True
     )

time: 74.6 us -> 74.4 us (level)
    concatenate x1 -> x0, local copies, waits for them, and re-layouts: 0.87 us -> none  [body(): jnp.concatenate([projected, cotangent[:, None], filter_upper[:, None], fi...]
    reshape x0 -> x1, local copies, waits for them, and re-layouts: none -> 0.87 us  [body(): outgoing.reshape(length, 6, parts, slices)]
where the time goes in v9:
time: 74.4 us; the launch traced here: 73.9 us
  blocking collectives  20.6 us (28%)
  starting transfers between devices  18.2 us (24%)
  waiting for transfers between devices  13.8 us (19%)
  local copies, waits for them, and re-layouts  10.3 us (14%)
  other arithmetic  5.73 us (8%)
  matrix products  4.08 us (5%)
  between operations  1.16 us (2%)
    all_to_all x1, blocking collectives, body(): lax.all_to_all(leaving.reshape(parts, length, 6, 1, slices), 'inner', spl...  20.6 us
    all_to_all x1, starting transfers between devices, body(): lax.all_to_all(outgoing.reshape(length, 6, parts, slices), 'inner', split...  18.2 us
    all_to_all x1, waiting for transfers between devices, body(): lax.all_to_all(outgoing.reshape(length, 6, parts, slices), 'inner', split...  13.8 us
    unnamed x27, local copies, waits for them, and re-layouts  6.88 us
    unnamed x8, other arithmetic  2.68 us
    dot_general x4, matrix products, mix_axis(): return jnp.einsum(joined, matrix, values, precision=transform_mode)  2.67 us
  transfers between devices with their start and end apart: 1, of which 1 were waited for; matrix products, arithmetic and copies ran while one was open for 1% of the time, Pallas kernels for 0%

profile of v9, /device:TPU:1, one launch (start us, length us, event | category | flops | bytes accessed | tf_op | source)
XLA Modules:
  0.0 73.9 jit_solution(10043421240787413203)
XLA Ops:
  0.7 0.1 fusion.43
  0.8 0.1 fusion.45
  0.8 0.1 fusion.47
  0.9 0.1 fusion.49
  1.0 0.1 fusion.51
  1.0 0.1 fusion.53
  1.1 0.1 fusion.55
  1.2 0.1 fusion.57
  1.2 0.1 fusion.59
  1.3 0.1 fusion.39
  1.4 0.1 fusion.41
  1.5 0.7 fusion.62
  2.2 1.0 %copy.62 = bf16[128,256]{0,1:T(8,128)(2,1)S(1)} copy(bf16[128,256]{1,0:T(8,128)(2,1)} %param.25) | data formatting | bytes 131072 | tf_op args[6]
  3.1 0.1 stack.36
  3.2 1.1 %fusion.10 = f32[128,64]{0,1:T(8,128)S(1)} fusion(f32[128,33]{0,1:T(8,128)S(1)} %stack.36, f32[33,64]{1,0:T(8,128)} %param.21, f32[64]{0:T(128)} %param.22), kind=kOutput, calls=%fused_computation.16 | convolution fusion | flops 3252224 | bytes 58368 | tf_op jit(solution)/shard_map/dot_general | solution.py:138
  4.4 0.3 fusion.32
  4.7 0.1 copy.64
  4.8 0.1 copy.65
  4.9 1.1 %copy.63 = bf16[128,3,256]{0,2,1:T(8,128)(2,1)S(1)} copy(bf16[128,3,256]{2,0,1:T(8,128)(2,1)} %param.19) | data formatting | bytes 393216 | tf_op args[0]
  6.0 0.1 pad_maximum_fusion.1
  6.1 0.9 %copy.66 = bf16[128,6,64,4]{0,3,1,2:T(4,128)(2,1)} copy(bf16[128,6,64,4]{0,3,2,1:T(4,128)(2,1)S(1)} %bitcast.202) | data formatting | bytes 786432 | tf_op jit(solution)/shard_map/reshape | solution.py:149
  7.0 18.2 %all-to-all-start = ((bf16[128,6,64,4]{0,3,1,2:T(4,128)(2,1)}), bf16[128,6,64,4]{0,3,1,2:T(4,128)(2,1)S(1)}, u32[]{:S(2)}, u32[]{:S(2)}) async-start(bf16[128,6,64,4]{0,3,1,2:T(4,128)(2,1)} %copy.66), calls=%async_computation | async-start | bytes 786432 | tf_op jit(solution)/shard_map/all_to_all | solution.py:148
  25.2 0.1 constant_dynamic-slice_fusion
  25.3 0.1 copy.61
  25.4 0.2 slice_reduce_fusion.20
  25.6 0.5 slice_reduce_fusion.6
  26.1 13.8 %all-to-all-done = bf16[128,6,64,4]{0,3,1,2:T(4,128)(2,1)S(1)} async-done(((bf16[128,6,64,4]{0,3,1,2:T(4,128)(2,1)}), bf16[128,6,64,4]{0,3,1,2:T(4,128)(2,1)S(1)}, u32[]{:S(2)}, u32[]{:S(2)}) %all-to-all-start) | async-done | bytes 393248 | tf_op jit(solution)/shard_map/all_to_all | solution.py:148
  39.9 0.1 copy.67
  40.0 0.1 reshape.752
  40.2 0.1 slice_bitcast_fusion.9
  40.3 0.6 multiply_bitcast_fusion
  40.9 0.3 fusion.23
  41.3 0.1 broadcast_multiply_fusion.1
  41.4 0.1 pad_bitcast_fusion
  41.5 0.1 maximum_bitcast_fusion.8
  41.6 0.7 copy-done.5
  42.3 0.8 %fusion.7 = f32[2,2,12,64,128]{4,3,0,2,1:T(8,128)S(1)} fusion(f32[2,2,64,64,1,1]{3,2,1,0,5,4:T(8,128)S(1)} %copy-done.5, f32[1,2,12,64,128]{4,3,0,2,1:T(8,128)S(1)} %pad_bitcast_fusion, f32[1,2,12,64,128]{4,3,0,2,1:T(8,128)S(1)} %maximum_bitcast_fusion.8), kind=kOutput, calls=%fused_computation.9 | convolution fusion | flops 302383104 | bytes 3211264 | tf_op jit(solution)/shard_map/zyap,yhrpj->zhraj/dot_general | solution.py:48
  43.2 0.3 multiply_subtract_fusion
  43.5 0.6 copy-done.2
  44.1 0.8 %fusion.6 = f32[2,2,12,64,128]{4,3,0,2,1:T(8,128)S(1)} fusion(f32[2,2,128,128,1,1]{3,2,1,0,5,4:T(8,128)S(1)} %copy-done.2, f32[1,2,12,64,128]{4,3,0,2,1:T(8,128)S(1)} %get-tuple-element.39, f32[1,2,12,64,128]{4,3,0,2,1:T(8,128)S(1)} %get-tuple-element.38), kind=kOutput, calls=%fused_computation.8 | convolution fusion | flops 604372992 | bytes 3407872 | tf_op jit(solution)/shard_map/zybj,yhraj->zhrab/dot_general | solution.py:48
  45.0 0.1 multiply_subtract_fusion.2
  45.1 0.2 multiply_subtract_fusion.4
  45.3 0.1 fusion.11
  45.4 0.1 pad_maximum_fusion
  45.4 0.1 slice_subtract_fusion
  45.6 0.8 %copy-done.1 = f32[2,2,128,128,1,1]{3,2,0,1,5,4:T(8,128)S(1)} copy-done((f32[2,2,128,128,1,1]{3,2,0,1,5,4:T(8,128)S(1)}, f32[2,2,128,128,1,1]{3,2,0,1,5,4:T(8,128)}, u32[]{:S(2)}) %copy-start.1) | copy-done | bytes 262168
  46.4 0.5 convolution_bitcast_fusion.1
  46.9 0.1 multiply_add_fusion.1
  47.0 0.3 copy-done.8
  47.3 0.5 fusion.9
  47.8 0.1 fusion.19
  48.0 0.1 convert_multiply_fusion
  48.1 0.1 fusion.28
  48.3 0.5 bitcast_dynamic-update-slice_fusion.5
  48.8 0.1 bitcast_multiply_fusion
  48.9 0.5 bitcast_dynamic-update-slice_fusion.4
  49.4 0.5 bitcast_dynamic-update-slice_fusion.3
  50.0 0.4 reshape.755
  50.4 0.3 copy.74
  50.8 20.6 %all_to_all.30 = bf16[64,128,6,1,4]{1,4,2,3,0:T(4,128)(2,1)S(1)} all-to-all(bf16[64,128,6,1,4]{1,4,2,3,0:T(4,128)(2,1)S(1)} %copy.74), channel_id=1, replica_groups=mesh['outer'=16,'inner'=64] {'inner'}, dimensions={0} | all-to-all | bytes 786432 | tf_op jit(solution)/shard_map/all_to_all | solution.py:210
  71.4 0.1 copy.75
  71.6 0.7 %copy.76 = bf16[128,256]{1,0:T(8,128)(2,1)} copy(bf16[128,256]{0,1:T(8,128)(2,1)S(1)} %slice_bitcast_fusion.6) | data formatting | bytes 131072
  72.3 0.8 %copy.77 = bf16[128,3,256]{2,0,1:T(8,128)(2,1)} copy(bf16[128,3,256]{0,2,1:T(8,128)(2,1)S(1)} %slice.486) | data formatting | bytes 393216
  73.1 0.8 %copy.78 = f32[128,256]{1,0:T(8,128)} copy(f32[128,256]{0,1:T(8,128)S(1)} %add_bitcast_fusion) | data formatting | bytes 262144
  (36 shorter events, 0.5 us)
Async XLA Ops:
  0.6 3.7 %copy-start = (f32[64,256]{1,0:T(8,128)S(1)}, f32[64,256]{1,0:T(8,128)}, u32[]{:S(2)}) copy-start(f32[64,256]{1,0:T(8,128)} %param.23) | copy-start | bytes 196612
  4.7 20.5 %copy-start.9 = (f32[7,3,256]{2,0,1:T(8,128)S(1)}, f32[7,3,256]{2,0,1:T(8,128)}, u32[]{:S(2)}) copy-start(f32[7,3,256]{2,0,1:T(8,128)} %param.20) | copy-start | bytes 64516
  7.0 32.9 %all-to-all-start = ((bf16[128,6,64,4]{0,3,1,2:T(4,128)(2,1)}), bf16[128,6,64,4]{0,3,1,2:T(4,128)(2,1)S(1)}, u32[]{:S(2)}, u32[]{:S(2)}) async-start(bf16[128,6,64,4]{0,3,1,2:T(4,128)(2,1)} %copy.66), calls=%async_computation | async-start | bytes 786432 | tf_op jit(solution)/shard_map/all_to_all | solution.py:148
  40.1 1.2 %copy-start.6 = (f32[64,128]{1,0:T(8,128)S(1)}, f32[64,128]{1,0:T(8,128)}, u32[]{:S(2)}) copy-start(f32[64,128]{1,0:T(8,128)} %constant.197.clone) | copy-start | bytes 98308
  40.1 1.2 %copy-start.7 = (f32[64,128]{1,0:T(8,128)S(1)}, f32[64,128]{1,0:T(8,128)}, u32[]{:S(2)}) copy-start(f32[64,128]{1,0:T(8,128)} %constant.196.clone) | copy-start | bytes 98308
  41.4 0.9 %copy-start.5 = (f32[2,2,64,64,1,1]{3,2,1,0,5,4:T(8,128)S(1)}, f32[2,2,64,64,1,1]{3,2,1,0,5,4:T(8,128)}, u32[]{:S(2)}) copy-start(f32[2,2,64,64,1,1]{3,2,1,0,5,4:T(8,128)} %constant.216) | copy-start | bytes 196612
  42.3 0.8 %copy-start.3 = (f32[64,128]{1,0:T(8,128)S(1)}, f32[64,128]{1,0:T(8,128)}, u32[]{:S(2)}) copy-start(f32[64,128]{1,0:T(8,128)} %constant.200.clone) | copy-start | bytes 98308
  42.3 0.8 %copy-start.4 = (f32[64,128]{1,0:T(8,128)S(1)}, f32[64,128]{1,0:T(8,128)}, u32[]{:S(2)}) copy-start(f32[64,128]{1,0:T(8,128)} %constant.199.clone) | copy-start | bytes 98308
  43.2 1.0 %copy-start.2 = (f32[2,2,128,128,1,1]{3,2,1,0,5,4:T(8,128)S(1)}, f32[2,2,128,128,1,1]{3,2,1,0,5,4:T(8,128)}, u32[]{:S(2)}) copy-start(f32[2,2,128,128,1,1]{3,2,1,0,5,4:T(8,128)} %constant.217) | copy-start | bytes 786436
  45.4 1.0 %copy-start.1 = (f32[2,2,128,128,1,1]{3,2,0,1,5,4:T(8,128)S(1)}, f32[2,2,128,128,1,1]{3,2,0,1,5,4:T(8,128)}, u32[]{:S(2)}) copy-start(f32[2,2,128,128,1,1]{3,2,0,1,5,4:T(8,128)} %constant.218) | copy-start | bytes 786436
  46.4 0.9 %copy-start.8 = (f32[2,2,64,64,1,1]{3,2,0,1,5,4:T(8,128)S(1)}, f32[2,2,64,64,1,1]{3,2,0,1,5,4:T(8,128)}, u32[]{:S(2)}) copy-start(f32[2,2,64,64,1,1]{3,2,0,1,5,4:T(8,128)} %constant.219) | copy-start | bytes 196612

commit v10 on v9

--- a/solution.py
+++ b/solution.py
@@ -104,15 +104,16 @@
     return jnp.swapaxes(moved[:, :, 0, :], 1, 2)
 
 
-def filter_features(places, seq_total, bands):
-    columns = [places.astype(jnp.float32) / seq_total]
+def filter_features(seq_total, bands):
+    places = np.arange(seq_total, dtype=np.int64)
+    columns = [places.astype(np.float32) / np.float32(seq_total)]
     for band in range(bands):
         stride = min(2**band, seq_total // 4)
         phases = places % (seq_total // stride) * stride
-        angles = full_turn / seq_total * phases.astype(jnp.float32)
-        columns.append(jnp.cos(angles))
-        columns.append(jnp.sin(angles))
-    return jnp.stack(columns, axis=1)
+        angles = np.float32(full_turn / seq_total) * phases.astype(np.float32)
+        columns.append(np.cos(angles))
+        columns.append(np.sin(angles))
+    return jnp.asarray(np.stack(columns, axis=0), jnp.float32)
 
 
 def decay_window(rates, places):
@@ -135,7 +136,13 @@
     slices = chans // parts
     places = inner_id * length + jnp.arange(length, dtype=jnp.int32)
     activity = jnp.sin(
-        jnp.dot(filter_features(places, seq_total, bands), filter_in, precision=exact_mode)
+        jnp.dot(
+            jnp.transpose(
+                lax.dynamic_slice_in_dim(filter_features(seq_total, bands), inner_id * length, length, 1)
+            ),
+            filter_in,
+            precision=exact_mode,
+        )
         + filter_bias
     )
     shaped = jnp.dot(activity, filter_out, precision=exact_mode)

time: 74.4 us -> 73.5 us (0.988)
  no operation moved by 1% of the time
where the time goes in v10:
time: 73.5 us; the launch traced here: 73.1 us
  blocking collectives  20.6 us (28%)
  starting transfers between devices  18.2 us (25%)
  waiting for transfers between devices  13.8 us (19%)
  local copies, waits for them, and re-layouts  10.1 us (14%)
  other arithmetic  5.07 us (7%)
  matrix products  4.09 us (6%)
  between operations  1.11 us (2%)
    all_to_all x1, blocking collectives, body(): lax.all_to_all(leaving.reshape(parts, length, 6, 1, slices), 'inner', spl...  20.6 us
    all_to_all x1, starting transfers between devices, body(): lax.all_to_all(outgoing.reshape(length, 6, parts, slices), 'inner', split...  18.2 us
    all_to_all x1, waiting for transfers between devices, body(): lax.all_to_all(outgoing.reshape(length, 6, parts, slices), 'inner', split...  13.8 us
    unnamed x27, local copies, waits for them, and re-layouts  6.89 us
    unnamed x8, other arithmetic  2.68 us
    dot_general x4, matrix products, mix_axis(): return jnp.einsum(joined, matrix, values, precision=transform_mode)  2.67 us
  transfers between devices with their start and end apart: 1, of which 1 were waited for; matrix products, arithmetic and copies ran while one was open for 1% of the time, Pallas kernels for 0%

profile of v10, /device:TPU:1, one launch (start us, length us, event | category | flops | bytes accessed | tf_op | source)
XLA Modules:
  0.0 73.1 jit_solution(163182357785831342)
XLA Ops:
  0.6 0.0 copy-start
  0.7 0.7 fusion.39
  1.4 1.0 %copy.63 = bf16[128,256]{0,1:T(8,128)(2,1)S(1)} copy(bf16[128,256]{1,0:T(8,128)(2,1)} %param.26) | data formatting | bytes 131072 | tf_op args[6]
  2.3 1.1 %fusion.10 = f32[128,64]{0,1:T(8,128)S(1)} fusion(f32[33,64]{1,0:T(8,128)} %param.22, f32[33,8192]{1,0:T(8,128)} %constant.43.clone, s32[]{:T(128)S(6)} %select_n.7, f32[64]{0:T(128)} %param.23), kind=kOutput, calls=%fused_computation.16 | convolution fusion | flops 3252224 | bytes 74244 | tf_op jit(solution)/shard_map/dot_general | solution.py:139
  3.5 0.0 copy-done
  3.5 0.3 fusion.32
  3.8 0.0 copy-start.9
  3.8 0.1 copy.65
  3.9 0.1 copy.66
  4.0 1.1 %copy.64 = bf16[128,3,256]{0,2,1:T(8,128)(2,1)S(1)} copy(bf16[128,3,256]{2,0,1:T(8,128)(2,1)} %param.20) | data formatting | bytes 393216 | tf_op args[0]
  5.1 0.1 pad_maximum_fusion.1
  5.2 0.9 %copy.67 = bf16[128,6,64,4]{0,3,1,2:T(4,128)(2,1)} copy(bf16[128,6,64,4]{0,3,2,1:T(4,128)(2,1)S(1)} %bitcast.201) | data formatting | bytes 786432 | tf_op jit(solution)/shard_map/reshape | solution.py:156
  6.1 18.2 %all-to-all-start = ((bf16[128,6,64,4]{0,3,1,2:T(4,128)(2,1)}), bf16[128,6,64,4]{0,3,1,2:T(4,128)(2,1)S(1)}, u32[]{:S(2)}, u32[]{:S(2)}) async-start(bf16[128,6,64,4]{0,3,1,2:T(4,128)(2,1)} %copy.67), calls=%async_computation | async-start | bytes 786432 | tf_op jit(solution)/shard_map/all_to_all | solution.py:155
  24.3 0.0 copy-done.9
  24.3 0.1 constant_dynamic-slice_fusion
  24.4 0.1 copy.62
  24.5 0.2 slice_reduce_fusion.20
  24.7 0.5 slice_reduce_fusion.6
  25.2 13.8 %all-to-all-done = bf16[128,6,64,4]{0,3,1,2:T(4,128)(2,1)S(1)} async-done(((bf16[128,6,64,4]{0,3,1,2:T(4,128)(2,1)}), bf16[128,6,64,4]{0,3,1,2:T(4,128)(2,1)S(1)}, u32[]{:S(2)}, u32[]{:S(2)}) %all-to-all-start) | async-done | bytes 393248 | tf_op jit(solution)/shard_map/all_to_all | solution.py:155
  39.0 0.1 copy.68
  39.1 0.1 reshape.211
  39.3 0.1 slice_bitcast_fusion.9
  39.3 0.0 copy-start.6
  39.4 0.0 copy-start.7
  39.4 0.6 multiply_bitcast_fusion
  40.1 0.3 fusion.23
  40.5 0.0 copy-done.6
  40.5 0.0 copy-done.7
  40.5 0.1 broadcast_multiply_fusion.1
  40.6 0.0 copy-start.5
  40.6 0.2 maximum_bitcast_fusion.8
  40.8 0.7 copy-done.5
  41.5 0.8 %fusion.7 = f32[2,2,12,64,128]{4,3,0,2,1:T(8,128)S(1)} fusion(f32[2,2,64,64,1,1]{3,2,1,0,5,4:T(8,128)S(1)} %copy-done.5, f32[1,2,12,64,128]{4,3,0,2,1:T(8,128)S(1)} %get-tuple-element.70, f32[1,2,12,64,128]{4,3,0,2,1:T(8,128)S(1)} %get-tuple-element.69), kind=kOutput, calls=%fused_computation.9 | convolution fusion | flops 302383104 | bytes 3211264 | tf_op jit(solution)/shard_map/zyap,yhrpj->zhraj/dot_general | solution.py:48
  42.3 0.0 copy-done.3
  42.3 0.0 copy-done.4
  42.3 0.0 copy-start.2
  42.4 0.3 multiply_subtract_fusion
  42.7 0.6 copy-done.2
  43.3 0.8 %fusion.6 = f32[2,2,12,64,128]{4,3,0,2,1:T(8,128)S(1)} fusion(f32[2,2,128,128,1,1]{3,2,1,0,5,4:T(8,128)S(1)} %copy-done.2, f32[1,2,12,64,128]{4,3,0,2,1:T(8,128)S(1)} %get-tuple-element.39, f32[1,2,12,64,128]{4,3,0,2,1:T(8,128)S(1)} %get-tuple-element.38), kind=kOutput, calls=%fused_computation.8 | convolution fusion | flops 604372992 | bytes 3407872 | tf_op jit(solution)/shard_map/zybj,yhraj->zhrab/dot_general | solution.py:48
  44.1 0.1 multiply_subtract_fusion.2
  44.2 0.2 multiply_subtract_fusion.4
  44.5 0.1 fusion.11
  44.5 0.1 pad_maximum_fusion
  44.6 0.0 copy-start.1
  44.6 0.1 slice_subtract_fusion
  44.7 0.8 %copy-done.1 = f32[2,2,128,128,1,1]{3,2,0,1,5,4:T(8,128)S(1)} copy-done((f32[2,2,128,128,1,1]{3,2,0,1,5,4:T(8,128)S(1)}, f32[2,2,128,128,1,1]{3,2,0,1,5,4:T(8,128)}, u32[]{:S(2)}) %copy-start.1) | copy-done | bytes 262168
  45.5 0.5 convolution_bitcast_fusion.1
  46.1 0.1 multiply_add_fusion.1
  46.2 0.3 copy-done.8
  46.4 0.5 fusion.9
  47.0 0.1 fusion.19
  47.1 0.1 convert_multiply_fusion
  47.3 0.1 fusion.28
  47.4 0.5 bitcast_dynamic-update-slice_fusion.5
  47.9 0.1 bitcast_multiply_fusion
  48.1 0.5 bitcast_dynamic-update-slice_fusion.4
  48.6 0.5 bitcast_dynamic-update-slice_fusion.3
  49.2 0.4 reshape.214
  49.6 0.3 copy.75
  49.9 20.6 %all_to_all.30 = bf16[64,128,6,1,4]{1,4,2,3,0:T(4,128)(2,1)S(1)} all-to-all(bf16[64,128,6,1,4]{1,4,2,3,0:T(4,128)(2,1)S(1)} %copy.75), channel_id=1, replica_groups=mesh['outer'=16,'inner'=64] {'inner'}, dimensions={0} | all-to-all | bytes 786432 | tf_op jit(solution)/shard_map/all_to_all | solution.py:217
  70.5 0.1 copy.76
  70.7 0.7 %copy.77 = bf16[128,256]{1,0:T(8,128)(2,1)} copy(bf16[128,256]{0,1:T(8,128)(2,1)S(1)} %slice_bitcast_fusion.6) | data formatting | bytes 131072
  71.5 0.8 %copy.78 = bf16[128,3,256]{2,0,1:T(8,128)(2,1)} copy(bf16[128,3,256]{0,2,1:T(8,128)(2,1)S(1)} %slice.486) | data formatting | bytes 393216
  72.3 0.8 %copy.79 = f32[128,256]{1,0:T(8,128)} copy(f32[128,256]{0,1:T(8,128)S(1)} %add_bitcast_fusion) | data formatting | bytes 262144
  (21 shorter events, 0.4 us)
Async XLA Ops:
  0.6 2.8 %copy-start = (f32[64,256]{1,0:T(8,128)S(1)}, f32[64,256]{1,0:T(8,128)}, u32[]{:S(2)}) copy-start(f32[64,256]{1,0:T(8,128)} %param.24) | copy-start | bytes 196612
  3.8 20.5 %copy-start.9 = (f32[7,3,256]{2,0,1:T(8,128)S(1)}, f32[7,3,256]{2,0,1:T(8,128)}, u32[]{:S(2)}) copy-start(f32[7,3,256]{2,0,1:T(8,128)} %param.21) | copy-start | bytes 64516
  6.1 32.9 %all-to-all-start = ((bf16[128,6,64,4]{0,3,1,2:T(4,128)(2,1)}), bf16[128,6,64,4]{0,3,1,2:T(4,128)(2,1)S(1)}, u32[]{:S(2)}, u32[]{:S(2)}) async-start(bf16[128,6,64,4]{0,3,1,2:T(4,128)(2,1)} %copy.67), calls=%async_computation | async-start | bytes 786432 | tf_op jit(solution)/shard_map/all_to_all | solution.py:155
  39.3 1.1 %copy-start.6 = (f32[64,128]{1,0:T(8,128)S(1)}, f32[64,128]{1,0:T(8,128)}, u32[]{:S(2)}) copy-start(f32[64,128]{1,0:T(8,128)} %constant.45.clone) | copy-start | bytes 98308
  39.4 1.1 %copy-start.7 = (f32[64,128]{1,0:T(8,128)S(1)}, f32[64,128]{1,0:T(8,128)}, u32[]{:S(2)}) copy-start(f32[64,128]{1,0:T(8,128)} %constant.44.clone) | copy-start | bytes 98308
  40.6 0.9 %copy-start.5 = (f32[2,2,64,64,1,1]{3,2,1,0,5,4:T(8,128)S(1)}, f32[2,2,64,64,1,1]{3,2,1,0,5,4:T(8,128)}, u32[]{:S(2)}) copy-start(f32[2,2,64,64,1,1]{3,2,1,0,5,4:T(8,128)} %constant.64) | copy-start | bytes 196612
  41.5 0.8 %copy-start.3 = (f32[64,128]{1,0:T(8,128)S(1)}, f32[64,128]{1,0:T(8,128)}, u32[]{:S(2)}) copy-start(f32[64,128]{1,0:T(8,128)} %constant.48.clone) | copy-start | bytes 98308
  41.5 0.8 %copy-start.4 = (f32[64,128]{1,0:T(8,128)S(1)}, f32[64,128]{1,0:T(8,128)}, u32[]{:S(2)}) copy-start(f32[64,128]{1,0:T(8,128)} %constant.47.clone) | copy-start | bytes 98308
  42.3 1.0 %copy-start.2 = (f32[2,2,128,128,1,1]{3,2,1,0,5,4:T(8,128)S(1)}, f32[2,2,128,128,1,1]{3,2,1,0,5,4:T(8,128)}, u32[]{:S(2)}) copy-start(f32[2,2,128,128,1,1]{3,2,1,0,5,4:T(8,128)} %constant.65) | copy-start | bytes 786436
  44.6 1.0 %copy-start.1 = (f32[2,2,128,128,1,1]{3,2,0,1,5,4:T(8,128)S(1)}, f32[2,2,128,128,1,1]{3,2,0,1,5,4:T(8,128)}, u32[]{:S(2)}) copy-start(f32[2,2,128,128,1,1]{3,2,0,1,5,4:T(8,128)} %constant.66) | copy-start | bytes 786436
  45.5 0.9 %copy-start.8 = (f32[2,2,64,64,1,1]{3,2,0,1,5,4:T(8,128)S(1)}, f32[2,2,64,64,1,1]{3,2,0,1,5,4:T(8,128)}, u32[]{:S(2)}) copy-start(f32[2,2,64,64,1,1]{3,2,0,1,5,4:T(8,128)} %constant.67) | copy-start | bytes 196612

commit v11 on v10

--- a/solution.py
+++ b/solution.py
@@ -36,11 +36,26 @@
     return jnp.stack([values[0], -values[1]])
 
 
-def mix_axis(values, count, direction, pattern):
+def block_matrix(count):
     index = np.arange(count, dtype=np.int64)
     angles = -full_turn / count * ((index[:, None] * index[None, :]) % count).astype(np.float64)
     cosine, sine = np.cos(angles), np.sin(angles)
-    matrix = jnp.asarray(np.stack([np.stack([cosine, -sine]), np.stack([sine, cosine])]), jnp.float32)
+    return jnp.asarray(np.stack([np.stack([cosine, -sine]), np.stack([sine, cosine])]), jnp.float32)
+
+
+def transform_tables(parts, length):
+    seq_total = parts * length
+    index_a = np.arange(parts, dtype=np.int64)[:, None]
+    index_j = np.arange(length, dtype=np.int64)[None, :]
+    return {
+        "small": block_matrix(parts),
+        "large": block_matrix(length),
+        "twist": turning(grid_places(parts, length), 2 * seq_total, -1.0),
+        "spin": turning(index_a * index_j, seq_total, -1.0),
+    }
+
+
+def mix_axis(values, matrix, direction, pattern):
     pair, result = pattern.split("->")
     table, operand = pair.split(",")
     order = "zy" if direction < 0 else "yz"
@@ -55,23 +70,23 @@
     )
 
 
-def forward_padded(signal):
+def forward_padded(signal, tables):
     parts = signal.shape[1]
     length = signal.shape[2]
     seq_total = parts * length
-    cosine, sine = turning(grid_places(parts, length), 2 * seq_total, -1.0)
+    cosine, sine = tables["twist"]
     values = jnp.stack(
         [jnp.stack([signal, signal * cosine]), jnp.stack([jnp.zeros_like(signal), signal * sine])]
     )
-    values = mix_axis(values, parts, -1.0, "ap,hrpj->hraj")
+    values = mix_axis(values, tables["small"], -1.0, "ap,hrpj->hraj")
     index_a = np.arange(parts, dtype=np.int64)[:, None]
     index_j = np.arange(length, dtype=np.int64)[None, :]
-    cosine, sine = turning(index_a * index_j, seq_total, -1.0)
+    cosine, sine = tables["spin"]
     values = rotate(values, cosine, sine)
-    return mix_axis(values, length, -1.0, "bj,hraj->hrab")
-
-
-def inverse_padded(spectrum):
+    return mix_axis(values, tables["large"], -1.0, "bj,hraj->hrab")
+
+
+def inverse_padded(spectrum, tables):
     half = spectrum.shape[2] // 2
     first = spectrum[:, :, :half]
     second = spectrum[:, :, half:]
@@ -79,15 +94,15 @@
     parts = spectrum.shape[3]
     length = spectrum.shape[4]
     seq_total = parts * length
-    values = mix_axis(joined, length, 1.0, "jb,hrab->hraj")
+    values = mix_axis(joined, tables["large"], 1.0, "jb,hrab->hraj")
     index_a = np.arange(parts, dtype=np.int64)[:, None]
     index_j = np.arange(length, dtype=np.int64)[None, :]
-    cosine, sine = turning(index_a * index_j, seq_total, -1.0)
+    cosine, sine = tables["spin"]
     values = jnp.stack(
         [values[0] * cosine + values[1] * sine, values[1] * cosine - values[0] * sine]
     )
-    values = mix_axis(values, parts, 1.0, "pa,hraj->hrpj") / seq_total
-    cosine, sine = turning(grid_places(parts, length), 2 * seq_total, -1.0)
+    values = mix_axis(values, tables["small"], 1.0, "pa,hraj->hrpj") / seq_total
+    cosine, sine = tables["twist"]
     real_part = 0.5 * (values[0, 0] + values[0, 1] * cosine + values[1, 1] * sine)
     other_part = 0.5 * (values[1, 0] - values[0, 1] * sine + values[1, 1] * cosine)
     return jnp.concatenate([real_part, other_part], axis=0)
@@ -151,7 +166,7 @@
     outgoing = jnp.concatenate(
         [projected, cotangent[:, None], filter_upper[:, None], filter_lower[:, None]], axis=1
     )
-    outgoing = lax.optimization_barrier(outgoing)
+    outgoing, tables = lax.optimization_barrier((outgoing, transform_tables(parts, length)))
     arrived = lax.all_to_all(
         outgoing.reshape(length, 6, parts, slices), "inner", split_axis=2, concat_axis=0, tiled=True
     )
@@ -174,7 +189,7 @@
     signal_rows = product.reshape(slices, parts, length)
     filter_rows = long_rows.reshape(slices, parts, length)
     grad_rows = grad_conv.reshape(slices, parts, length)
-    spectra = forward_padded(jnp.concatenate([signal_rows, filter_rows, grad_rows], axis=0))
+    spectra = forward_padded(jnp.concatenate([signal_rows, filter_rows, grad_rows], axis=0), tables)
     signal_spec = spectra[:, :, :slices]
     filter_spec = spectra[:, :, slices : 2 * slices]
     grad_spec = spectra[:, :, 2 * slices :]
@@ -192,7 +207,7 @@
          paired[:, :, slices : 2 * slices], paired[:, :, 2 * slices + spread :]],
         axis=2,
     )
-    returned = inverse_padded(ordered)
+    returned = inverse_padded(ordered, tables)
     returned = jnp.concatenate(
         [returned[:slices], returned[slices + spread : 2 * slices + spread],
          returned[slices : slices + spread], returned[2 * slices + spread :]],

time: 73.5 us -> 72.4 us (0.985)
  local copies, waits for them, and re-layouts: 10.1 us -> 9.02 us
    unnamed x27 -> x23, local copies, waits for them, and re-layouts: 6.89 us -> 5.8 us
where the time goes in v11:
time: 72.4 us; the launch traced here: 71.9 us
  blocking collectives  20.6 us (28%)
  starting transfers between devices  18.2 us (25%)
  waiting for transfers between devices  13.8 us (19%)
  local copies, waits for them, and re-layouts  9.02 us (12%)
  other arithmetic  5.07 us (7%)
  matrix products  4.1 us (6%)
  between operations  1.1 us (2%)
    all_to_all x1, blocking collectives, body(): lax.all_to_all(leaving.reshape(parts, length, 6, 1, slices), 'inner', spl...  20.6 us
    all_to_all x1, starting transfers between devices, body(): lax.all_to_all(outgoing.reshape(length, 6, parts, slices), 'inner', split...  18.2 us
    all_to_all x1, waiting for transfers between devices, body(): lax.all_to_all(outgoing.reshape(length, 6, parts, slices), 'inner', split...  13.8 us
    unnamed x23, local copies, waits for them, and re-layouts  5.8 us
    unnamed x8, other arithmetic  2.68 us
    dot_general x4, matrix products, mix_axis(): return jnp.einsum(joined, matrix, values, precision=transform_mode)  2.67 us
  transfers between devices with their start and end apart: 1, of which 1 were waited for; matrix products, arithmetic and copies ran while one was open for 1% of the time, Pallas kernels for 0%

profile of v11, /device:TPU:1, one launch (start us, length us, event | category | flops | bytes accessed | tf_op | source)
XLA Modules:
  0.0 71.9 jit_solution(13613518244063344550)
XLA Ops:
  0.6 0.0 copy-start
  0.7 0.7 %fusion.51 = (f32[256]{0:T(256)S(1)}, f32[256]{0:T(256)S(1)}) fusion(f32[256]{0:T(256)} %param.19), kind=kLoop, calls=%fused_computation.145 | loop fusion | flops 768 | bytes 3072 | tf_op jit(solution)/shard_map/neg | solution.py:135
  1.4 1.0 %copy.57 = bf16[128,256]{0,1:T(8,128)(2,1)S(1)} copy(bf16[128,256]{1,0:T(8,128)(2,1)} %param.20) | data formatting | bytes 131072 | tf_op args[6]
  2.3 1.1 %fusion.18 = f32[128,64]{0,1:T(8,128)S(1)} fusion(f32[33,64]{1,0:T(8,128)} %param.16, f32[33,8192]{1,0:T(8,128)} %constant.43.clone, s32[]{:T(128)S(6)} %select_n.7, f32[64]{0:T(128)} %param.17), kind=kOutput, calls=%fused_computation.18 | convolution fusion | flops 3252224 | bytes 74244 | tf_op jit(solution)/shard_map/dot_general | solution.py:154
  3.5 0.0 copy-done
  3.5 0.3 fusion.44
  3.8 0.0 copy-start.7
  3.8 0.1 copy.59
  3.9 0.1 copy.60
  4.0 1.1 %copy.58 = bf16[128,3,256]{0,2,1:T(8,128)(2,1)S(1)} copy(bf16[128,3,256]{2,0,1:T(8,128)(2,1)} %param.14) | data formatting | bytes 393216 | tf_op args[0]
  5.1 0.1 pad_maximum_fusion.1
  5.2 0.9 %copy.61 = bf16[128,6,64,4]{0,3,1,2:T(4,128)(2,1)} copy(bf16[128,6,64,4]{0,3,2,1:T(4,128)(2,1)S(1)} %bitcast.213) | data formatting | bytes 786432 | tf_op jit(solution)/shard_map/reshape | solution.py:171
  6.1 18.2 %all-to-all-start = ((bf16[128,6,64,4]{0,3,1,2:T(4,128)(2,1)}), bf16[128,6,64,4]{0,3,1,2:T(4,128)(2,1)S(1)}, u32[]{:S(2)}, u32[]{:S(2)}) async-start(bf16[128,6,64,4]{0,3,1,2:T(4,128)(2,1)} %copy.61), calls=%async_computation | async-start | bytes 786432 | tf_op jit(solution)/shard_map/all_to_all | solution.py:170
  24.3 0.0 copy-done.7
  24.3 0.1 constant_dynamic-slice_fusion
  24.4 0.1 copy.56
  24.5 0.2 slice_reduce_fusion.20
  24.7 0.5 slice_reduce_fusion.6
  25.2 13.8 %all-to-all-done = bf16[128,6,64,4]{0,3,1,2:T(4,128)(2,1)S(1)} async-done(((bf16[128,6,64,4]{0,3,1,2:T(4,128)(2,1)}), bf16[128,6,64,4]{0,3,1,2:T(4,128)(2,1)S(1)}, u32[]{:S(2)}, u32[]{:S(2)}) %all-to-all-start) | async-done | bytes 393248 | tf_op jit(solution)/shard_map/all_to_all | solution.py:170
  39.0 0.1 copy.62
  39.1 0.1 reshape.207
  39.3 0.1 slice_bitcast_fusion.9
  39.3 0.0 copy-start.5
  39.4 0.0 copy-start.6
  39.4 0.6 multiply_bitcast_fusion
  40.1 0.3 fusion.33
  40.5 0.0 copy-done.5
  40.5 0.0 copy-done.6
  40.5 0.1 broadcast_multiply_fusion.1
  40.6 0.0 copy-start.2
  40.6 0.2 maximum_bitcast_fusion
  40.8 0.7 %copy-done.2 = f32[2,2,64,64]{3,2,0,1:T(8,128)S(1)} copy-done((f32[2,2,64,64]{3,2,0,1:T(8,128)S(1)}, f32[2,2,64,64]{3,2,0,1:T(8,128)}, u32[]{:S(2)}) %copy-start.2) | copy-done | bytes 65560
  41.5 0.0 copy-start.3
  41.5 0.0 copy-start.4
  41.5 0.8 %fusion.10 = f32[2,2,12,64,128]{4,3,0,2,1:T(8,128)S(1)} fusion(f32[1,2,12,64,128]{4,3,0,2,1:T(8,128)S(1)} %get-tuple-element.84, f32[1,2,12,64,128]{4,3,0,2,1:T(8,128)S(1)} %get-tuple-element.83, f32[2,2,64,64]{3,2,0,1:T(8,128)S(1)} %copy-done.2), kind=kOutput, calls=%fused_computation.10 | convolution fusion | flops 302383104 | bytes 3211264 | tf_op jit(solution)/shard_map/zyap,yhrpj->zhraj/dot_general | solution.py:63
  42.3 0.0 copy-done.3
  42.3 0.0 copy-done.4
  42.3 0.0 copy-start.1
  42.4 0.3 multiply_subtract_fusion
  42.7 0.6 copy-done.1
  43.3 0.8 %fusion.13 = f32[2,2,12,64,128]{4,3,0,2,1:T(8,128)S(1)} fusion(f32[1,2,12,64,128]{4,3,0,2,1:T(8,128)S(1)} %get-tuple-element.53, f32[1,2,12,64,128]{4,3,0,2,1:T(8,128)S(1)} %get-tuple-element.52, f32[2,2,128,128]{3,2,0,1:T(8,128)S(1)} %copy-done.1), kind=kOutput, calls=%fused_computation.11 | convolution fusion | flops 604372992 | bytes 3407872 | tf_op jit(solution)/shard_map/zybj,yhraj->zhrab/dot_general | solution.py:63
  44.1 0.1 multiply_subtract_fusion.2
  44.2 0.2 multiply_subtract_fusion.4
  44.4 0.1 fusion.19
  44.5 0.1 pad_maximum_fusion
  44.6 0.1 slice_subtract_fusion
  44.7 0.5 convolution_bitcast_fusion.1
  45.2 0.1 multiply_add_fusion.1
  45.3 0.5 fusion.17
  45.9 0.1 fusion.29
  46.0 0.1 convert_multiply_fusion
  46.2 0.1 fusion.40
  46.3 0.5 bitcast_dynamic-update-slice_fusion.5
  46.8 0.1 bitcast_multiply_fusion
  47.0 0.5 bitcast_dynamic-update-slice_fusion.4
  47.5 0.5 bitcast_dynamic-update-slice_fusion.3
  48.1 0.4 reshape.210
  48.5 0.3 copy.69
  48.8 20.6 %all_to_all.30 = bf16[64,128,6,1,4]{1,4,2,3,0:T(4,128)(2,1)S(1)} all-to-all(bf16[64,128,6,1,4]{1,4,2,3,0:T(4,128)(2,1)S(1)} %copy.69), channel_id=1, replica_groups=mesh['outer'=16,'inner'=64] {'inner'}, dimensions={0} | all-to-all | bytes 786432 | tf_op jit(solution)/shard_map/all_to_all | solution.py:232
  69.4 0.1 copy.70
  69.6 0.7 %copy.71 = bf16[128,256]{1,0:T(8,128)(2,1)} copy(bf16[128,256]{0,1:T(8,128)(2,1)S(1)} %slice_bitcast_fusion.6) | data formatting | bytes 131072
  70.4 0.8 %copy.72 = bf16[128,3,256]{2,0,1:T(8,128)(2,1)} copy(bf16[128,3,256]{0,2,1:T(8,128)(2,1)S(1)} %slice.486) | data formatting | bytes 393216
  71.2 0.8 %copy.73 = f32[128,256]{1,0:T(8,128)} copy(f32[128,256]{0,1:T(8,128)S(1)} %add_bitcast_fusion) | data formatting | bytes 262144
  (18 shorter events, 0.4 us)
Async XLA Ops:
  0.6 2.8 %copy-start = (f32[64,256]{1,0:T(8,128)S(1)}, f32[64,256]{1,0:T(8,128)}, u32[]{:S(2)}) copy-start(f32[64,256]{1,0:T(8,128)} %param.18) | copy-start | bytes 196612
  3.8 20.5 %copy-start.7 = (f32[7,3,256]{2,0,1:T(8,128)S(1)}, f32[7,3,256]{2,0,1:T(8,128)}, u32[]{:S(2)}) copy-start(f32[7,3,256]{2,0,1:T(8,128)} %param.15) | copy-start | bytes 64516
  6.1 32.9 %all-to-all-start = ((bf16[128,6,64,4]{0,3,1,2:T(4,128)(2,1)}), bf16[128,6,64,4]{0,3,1,2:T(4,128)(2,1)S(1)}, u32[]{:S(2)}, u32[]{:S(2)}) async-start(bf16[128,6,64,4]{0,3,1,2:T(4,128)(2,1)} %copy.61), calls=%async_computation | async-start | bytes 786432 | tf_op jit(solution)/shard_map/all_to_all | solution.py:170
  39.3 1.1 %copy-start.5 = (f32[64,128]{1,0:T(8,128)S(1)}, f32[64,128]{1,0:T(8,128)}, u32[]{:S(2)}) copy-start(f32[64,128]{1,0:T(8,128)} %constant.47.clone) | copy-start | bytes 98308
  39.4 1.1 %copy-start.6 = (f32[64,128]{1,0:T(8,128)S(1)}, f32[64,128]{1,0:T(8,128)}, u32[]{:S(2)}) copy-start(f32[64,128]{1,0:T(8,128)} %constant.46.clone) | copy-start | bytes 98308
  40.6 0.9 %copy-start.2 = (f32[2,2,64,64]{3,2,0,1:T(8,128)S(1)}, f32[2,2,64,64]{3,2,0,1:T(8,128)}, u32[]{:S(2)}) copy-start(f32[2,2,64,64]{3,2,0,1:T(8,128)} %constant.44.clone) | copy-start | bytes 196612
  41.5 0.8 %copy-start.3 = (f32[64,128]{1,0:T(8,128)S(1)}, f32[64,128]{1,0:T(8,128)}, u32[]{:S(2)}) copy-start(f32[64,128]{1,0:T(8,128)} %constant.49.clone) | copy-start | bytes 98308
  41.5 0.8 %copy-start.4 = (f32[64,128]{1,0:T(8,128)S(1)}, f32[64,128]{1,0:T(8,128)}, u32[]{:S(2)}) copy-start(f32[64,128]{1,0:T(8,128)} %constant.48.clone) | copy-start | bytes 98308
  42.3 1.0 %copy-start.1 = (f32[2,2,128,128]{3,2,0,1:T(8,128)S(1)}, f32[2,2,128,128]{3,2,0,1:T(8,128)}, u32[]{:S(2)}) copy-start(f32[2,2,128,128]{3,2,0,1:T(8,128)} %constant.45.clone) | copy-start | bytes 786436

commit v12 on v11

--- a/solution.py
+++ b/solution.py
@@ -39,8 +39,11 @@
 def block_matrix(count):
     index = np.arange(count, dtype=np.int64)
     angles = -full_turn / count * ((index[:, None] * index[None, :]) % count).astype(np.float64)
-    cosine, sine = np.cos(angles), np.sin(angles)
-    return jnp.asarray(np.stack([np.stack([cosine, -sine]), np.stack([sine, cosine])]), jnp.float32)
+    return jnp.asarray(np.stack([np.cos(angles), np.sin(angles)]), jnp.float32)
+
+
+def joined_matrix(parts):
+    return jnp.stack([jnp.stack([parts[0], -parts[1]]), jnp.stack([parts[1], parts[0]])])
 
 
 def transform_tables(parts, length):
@@ -167,6 +170,8 @@
         [projected, cotangent[:, None], filter_upper[:, None], filter_lower[:, None]], axis=1
     )
     outgoing, tables = lax.optimization_barrier((outgoing, transform_tables(parts, length)))
+    tables["small"] = joined_matrix(tables["small"])
+    tables["large"] = joined_matrix(tables["large"])
     arrived = lax.all_to_all(
         outgoing.reshape(length, 6, parts, slices), "inner", split_axis=2, concat_axis=0, tiled=True
     )

time: 72.4 us -> 71 us (0.981)
  local copies, waits for them, and re-layouts: 9.02 us -> 7.7 us
    unnamed x23, local copies, waits for them, and re-layouts: 5.8 us -> 4.48 us
where the time goes in v12:
time: 71 us; the launch traced here: 70.7 us
  blocking collectives  20.6 us (29%)
  starting transfers between devices  18.2 us (26%)
  waiting for transfers between devices  13.7 us (19%)
  local copies, waits for them, and re-layouts  7.7 us (11%)
  other arithmetic  5.13 us (7%)
  matrix products  4.1 us (6%)
  between operations  1.17 us (2%)
    all_to_all x1, blocking collectives, body(): lax.all_to_all(leaving.reshape(parts, length, 6, 1, slices), 'inner', spl...  20.6 us
    all_to_all x1, starting transfers between devices, body(): lax.all_to_all(outgoing.reshape(length, 6, parts, slices), 'inner', split...  18.2 us
    all_to_all x1, waiting for transfers between devices, body(): lax.all_to_all(outgoing.reshape(length, 6, parts, slices), 'inner', split...  13.7 us
    unnamed x23, local copies, waits for them, and re-layouts  4.48 us
    unnamed x8, other arithmetic  2.69 us
    dot_general x4, matrix products, mix_axis(): return jnp.einsum(joined, matrix, values, precision=transform_mode)  2.68 us
  transfers between devices with their start and end apart: 1, of which 1 were waited for; matrix products, arithmetic and copies ran while one was open for 1% of the time, Pallas kernels for 0%

profile of v12, /device:TPU:1, one launch (start us, length us, event | category | flops | bytes accessed | tf_op | source)
XLA Modules:
  0.0 70.7 jit_solution(9812890555539234378)
XLA Ops:
  0.6 0.0 copy-start
  0.7 0.7 %fusion.43 = (f32[256]{0:T(256)S(1)}, f32[256]{0:T(256)S(1)}) fusion(f32[256]{0:T(256)} %param.19), kind=kLoop, calls=%fused_computation.149 | loop fusion | flops 768 | bytes 3072 | tf_op jit(solution)/shard_map/neg | solution.py:138
  1.4 1.0 %copy.57 = bf16[128,256]{0,1:T(8,128)(2,1)S(1)} copy(bf16[128,256]{1,0:T(8,128)(2,1)} %param.20) | data formatting | bytes 131072 | tf_op args[6]
  2.3 1.1 %fusion.10 = f32[128,64]{0,1:T(8,128)S(1)} fusion(f32[33,64]{1,0:T(8,128)} %param.16, f32[33,8192]{1,0:T(8,128)} %constant.43.clone, s32[]{:T(128)S(6)} %select_n.7, f32[64]{0:T(128)} %param.17), kind=kOutput, calls=%fused_computation.16 | convolution fusion | flops 3252224 | bytes 74244 | tf_op jit(solution)/shard_map/dot_general | solution.py:157
  3.5 0.0 copy-done
  3.5 0.3 fusion.36
  3.8 0.0 copy-start.7
  3.8 0.0 copy-start.6
  3.8 0.1 copy.59
  3.9 0.1 copy.60
  4.1 0.0 copy-start.5
  4.1 1.1 %copy.58 = bf16[128,3,256]{0,2,1:T(8,128)(2,1)S(1)} copy(bf16[128,3,256]{2,0,1:T(8,128)(2,1)} %param.14) | data formatting | bytes 393216 | tf_op args[0]
  5.2 0.1 pad_maximum_fusion.1
  5.3 0.9 %copy.61 = bf16[128,6,64,4]{0,3,1,2:T(4,128)(2,1)} copy(bf16[128,6,64,4]{0,3,2,1:T(4,128)(2,1)S(1)} %bitcast.219) | data formatting | bytes 786432 | tf_op jit(solution)/shard_map/reshape | solution.py:176
  6.1 18.2 %all-to-all-start = ((bf16[128,6,64,4]{0,3,1,2:T(4,128)(2,1)}), bf16[128,6,64,4]{0,3,1,2:T(4,128)(2,1)S(1)}, u32[]{:S(2)}, u32[]{:S(2)}) async-start(bf16[128,6,64,4]{0,3,1,2:T(4,128)(2,1)} %copy.61), calls=%async_computation | async-start | bytes 786432 | tf_op jit(solution)/shard_map/all_to_all | solution.py:175
  24.4 0.0 copy-done.7
  24.4 0.1 constant_dynamic-slice_fusion
  24.5 0.1 copy.56
  24.6 0.5 slice_reduce_fusion.6
  25.1 0.2 slice_reduce_fusion.20
  25.3 0.0 copy-done.6
  25.3 0.0 copy-done.5
  25.4 13.7 %all-to-all-done = bf16[128,6,64,4]{0,3,1,2:T(4,128)(2,1)S(1)} async-done(((bf16[128,6,64,4]{0,3,1,2:T(4,128)(2,1)}), bf16[128,6,64,4]{0,3,1,2:T(4,128)(2,1)S(1)}, u32[]{:S(2)}, u32[]{:S(2)}) %all-to-all-start) | async-done | bytes 393248 | tf_op jit(solution)/shard_map/all_to_all | solution.py:175
  39.1 0.1 copy.62
  39.2 0.1 reshape.207
  39.3 0.1 slice_bitcast_fusion.9
  39.4 0.0 copy-start.3
  39.4 0.0 copy-start.4
  39.4 0.6 multiply_bitcast_fusion
  40.1 0.4 fusion.27
  40.5 0.0 copy-done.3
  40.5 0.0 copy-done.4
  40.6 0.1 broadcast_multiply_fusion.1
  40.6 0.2 maximum_bitcast_fusion.8
  40.8 0.0 copy-start.1
  40.8 0.0 copy-start.2
  40.8 0.8 %fusion.7 = f32[2,2,12,64,128]{4,3,0,2,1:T(8,128)S(1)} fusion(f32[1,2,12,64,128]{4,3,0,2,1:T(8,128)S(1)} %get-tuple-element.94, f32[1,2,12,64,128]{4,3,0,2,1:T(8,128)S(1)} %get-tuple-element.93, f32[1,2,64,64]{3,2,1,0:T(8,128)S(1)} %get-tuple-element.90, f32[1,2,64,64]{3,2,1,0:T(8,128)S(1)} %get-tuple-element.89), kind=kOutput, calls=%fused_computation.9 | convolution fusion | flops 302399488 | bytes 3211264 | tf_op jit(solution)/shard_map/zyap,yhrpj->zhraj/dot_general | solution.py:66
  41.7 0.0 copy-done.1
  41.7 0.0 copy-done.2
  41.7 0.3 multiply_subtract_fusion
  42.0 0.8 %fusion.6 = f32[2,2,12,64,128]{4,3,0,2,1:T(8,128)S(1)} fusion(f32[1,2,12,64,128]{4,3,0,2,1:T(8,128)S(1)} %get-tuple-element.53, f32[1,2,12,64,128]{4,3,0,2,1:T(8,128)S(1)} %get-tuple-element.52, f32[1,2,128,128]{3,2,1,0:T(8,128)S(1)} %get-tuple-element.85, f32[1,2,128,128]{3,2,1,0:T(8,128)S(1)} %get-tuple-element.84), kind=kOutput, calls=%fused_computation.8 | convolution fusion | flops 604438528 | bytes 3407872 | tf_op jit(solution)/shard_map/zybj,yhraj->zhrab/dot_general | solution.py:66
  42.8 0.1 multiply_subtract_fusion.2
  42.9 0.2 multiply_subtract_fusion.4
  43.2 0.1 fusion.11
  43.2 0.1 pad_maximum_fusion
  43.3 0.1 slice_subtract_fusion
  43.4 0.5 convolution_bitcast_fusion.1
  43.9 0.1 multiply_add_fusion.1
  44.0 0.5 fusion.9
  44.6 0.1 fusion.23
  44.7 0.1 convert_multiply_fusion
  44.9 0.1 fusion.32
  45.0 0.5 bitcast_dynamic-update-slice_fusion.5
  45.5 0.1 bitcast_multiply_fusion
  45.7 0.5 bitcast_dynamic-update-slice_fusion.4
  46.2 0.5 bitcast_dynamic-update-slice_fusion.3
  46.8 0.4 reshape.210
  47.2 0.3 copy.69
  47.5 20.6 %all_to_all.30 = bf16[64,128,6,1,4]{1,4,2,3,0:T(4,128)(2,1)S(1)} all-to-all(bf16[64,128,6,1,4]{1,4,2,3,0:T(4,128)(2,1)S(1)} %copy.69), channel_id=1, replica_groups=mesh['outer'=16,'inner'=64] {'inner'}, dimensions={0} | all-to-all | bytes 786432 | tf_op jit(solution)/shard_map/all_to_all | solution.py:237
  68.1 0.1 copy.70
  68.3 0.7 %copy.71 = bf16[128,256]{1,0:T(8,128)(2,1)} copy(bf16[128,256]{0,1:T(8,128)(2,1)S(1)} %slice_bitcast_fusion.6) | data formatting | bytes 131072
  69.1 0.8 %copy.72 = bf16[128,3,256]{2,0,1:T(8,128)(2,1)} copy(bf16[128,3,256]{0,2,1:T(8,128)(2,1)S(1)} %slice.506) | data formatting | bytes 393216
  69.9 0.8 %copy.73 = f32[128,256]{1,0:T(8,128)} copy(f32[128,256]{0,1:T(8,128)S(1)} %add_bitcast_fusion) | data formatting | bytes 262144
  (22 shorter events, 0.4 us)
Async XLA Ops:
  0.6 2.8 %copy-start = (f32[64,256]{1,0:T(8,128)S(1)}, f32[64,256]{1,0:T(8,128)}, u32[]{:S(2)}) copy-start(f32[64,256]{1,0:T(8,128)} %param.18) | copy-start | bytes 196612
  3.8 20.6 %copy-start.7 = (f32[7,3,256]{2,0,1:T(8,128)S(1)}, f32[7,3,256]{2,0,1:T(8,128)}, u32[]{:S(2)}) copy-start(f32[7,3,256]{2,0,1:T(8,128)} %param.15) | copy-start | bytes 64516
  3.8 21.4 %copy-start.6 = (f32[2,64,64]{2,1,0:T(8,128)S(1)}, f32[2,64,64]{2,1,0:T(8,128)}, u32[]{:S(2)}) copy-start(f32[2,64,64]{2,1,0:T(8,128)} %constant.44.clone) | copy-start | bytes 98308
  4.1 21.2 %copy-start.5 = (f32[2,128,128]{2,1,0:T(8,128)S(1)}, f32[2,128,128]{2,1,0:T(8,128)}, u32[]{:S(2)}) copy-start(f32[2,128,128]{2,1,0:T(8,128)} %constant.45.clone) | copy-start | bytes 393220
  6.1 32.9 %all-to-all-start = ((bf16[128,6,64,4]{0,3,1,2:T(4,128)(2,1)}), bf16[128,6,64,4]{0,3,1,2:T(4,128)(2,1)S(1)}, u32[]{:S(2)}, u32[]{:S(2)}) async-start(bf16[128,6,64,4]{0,3,1,2:T(4,128)(2,1)} %copy.61), calls=%async_computation | async-start | bytes 786432 | tf_op jit(solution)/shard_map/all_to_all | solution.py:175
  39.4 1.1 %copy-start.3 = (f32[64,128]{1,0:T(8,128)S(1)}, f32[64,128]{1,0:T(8,128)}, u32[]{:S(2)}) copy-start(f32[64,128]{1,0:T(8,128)} %constant.47.clone) | copy-start | bytes 98308
  39.4 1.1 %copy-start.4 = (f32[64,128]{1,0:T(8,128)S(1)}, f32[64,128]{1,0:T(8,128)}, u32[]{:S(2)}) copy-start(f32[64,128]{1,0:T(8,128)} %constant.46.clone) | copy-start | bytes 98308
  40.8 0.9 %copy-start.1 = (f32[64,128]{1,0:T(8,128)S(1)}, f32[64,128]{1,0:T(8,128)}, u32[]{:S(2)}) copy-start(f32[64,128]{1,0:T(8,128)} %constant.49.clone) | copy-start | bytes 98308
  40.8 0.9 %copy-start.2 = (f32[64,128]{1,0:T(8,128)S(1)}, f32[64,128]{1,0:T(8,128)}, u32[]{:S(2)}) copy-start(f32[64,128]{1,0:T(8,128)} %constant.48.clone) | copy-start | bytes 98308
